TPU v7x, 32 devices: a whole 2x2x4 slice. The times are simulated.
32 devices in a mesh: row: 8 (over z, y), col: 4 (over x, core).
Axes of the slice: x: 2, y: 2, z: 4, core: 2. Of those that a mesh axis runs over, the one named last changes fastest.
Arguments:
- x_t: bfloat16 [128, 8192], P('col', 'row'), may hold values from -6 to 6
- tiles: bfloat16 [64, 128, 128], P('row'), may hold values from -0.375 to 0.375
- tile_owner: int32 [64, 1], P('row'), may hold values from 0 to 7; in each aligned block of 8 rows (0 to 7, 8 to 15, ...) at most 2 rows name the same one
- tile_local: int32 [64, 2], P('row'), may hold values from 0 to 7
- weight: bfloat16 [128, 256], replicated, may hold values from -0.5 to 0.5
- cotangent: bfloat16 [8192, 256], P('row'), may hold values from -0.0625 to 0.0625
Outputs:
- act: bfloat16 [8192, 256], P('row')
- grad_w: float32 [128, 256], P('col')
Inputs may be any that keep to these rules, and one draw needn't show every extreme that they name: `tile_owner`: within the 8 stored tiles of one index of row (aligned blocks of 8 rows) no owner appears more than 2 times, and some owner appears exactly 2 times.
All inputs are finite; a program needn't handle non-finite values.
Results may differ from a plain program's by a relative error of at most 0.0059.
Values may be sent and summed in bfloat16 or wider, within the bound.
No kernel may reach another device: no remote copies, remote signals or barrier semaphores. Data moves between devices by JAX's collectives and lax.ppermute only.
A program may use at most 64 MiB of HBM per device.

v0:
```python
import jax
import jax.numpy as jnp
from jax import lax
from jax.sharding import PartitionSpec as P


def body(x_t, tiles, tile_owner, tile_local, weight, cotangent):
    n_row = lax.axis_size("row")
    n_tiles, tile_dim = (tiles.shape[0], tiles.shape[1])
    feat_q, rows = x_t.shape
    n_blocks = rows // tile_dim
    capacity = 2 * (n_tiles // n_row)
    xb = x_t.reshape(feat_q, n_blocks, tile_dim).transpose(1, 0, 2)
    flat_blocks = xb.reshape(n_blocks, feat_q * tile_dim)
    owner = tile_owner[:, 0]
    row_local = tile_local[:, 0]
    col_local = tile_local[:, 1]
    owner_hot = (owner[:, None] == jnp.arange(n_row, dtype=jnp.int32)[None, :]).astype(jnp.int32)
    rank = jnp.sum(owner_hot * (jnp.cumsum(owner_hot, axis=0) - 1), axis=1)
    slot = owner * capacity + rank
    requests = (
        jnp.zeros((n_row * capacity,), jnp.int32).at[slot].set(col_local).reshape(n_row, capacity)
    )
    own_blocks = jnp.take(xb, row_local, axis=0)
    mirror_terms = jnp.einsum(
        "tfi,tij->tfj", own_blocks, tiles, preferred_element_type=jnp.float32
    ).astype(jnp.bfloat16)
    outgoing = jnp.zeros((n_row * capacity, feat_q * tile_dim), jnp.bfloat16)
    outgoing = (
        outgoing.at[slot]
        .set(mirror_terms.reshape(n_tiles, feat_q * tile_dim))
        .reshape(n_row, capacity, feat_q * tile_dim)
    )
    block_ids = lax.all_to_all(requests, "row", split_axis=0, concat_axis=0, tiled=True)
    picked = jnp.take(flat_blocks, block_ids, axis=0)
    fetched = lax.all_to_all(picked, "row", split_axis=0, concat_axis=0, tiled=True)
    incoming = lax.all_to_all(outgoing, "row", split_axis=0, concat_axis=0, tiled=True)
    fetched_tiles = jnp.take(fetched.reshape(n_row * capacity, feat_q, tile_dim), slot, axis=0)
    forward_terms = jnp.einsum(
        "tfj,tij->tfi", fetched_tiles, tiles, preferred_element_type=jnp.float32
    )
    block_range = jnp.arange(n_blocks, dtype=jnp.int32)
    row_hot = (row_local[:, None] == block_range[None, :]).astype(jnp.float32)
    local_sum = jnp.einsum("tfi,tb->fbi", forward_terms, row_hot, precision=lax.Precision.HIGHEST)
    in_hot = (block_ids.reshape(-1)[:, None] == block_range[None, :]).astype(jnp.bfloat16)
    mirror_sum = jnp.einsum(
        "sk,sb->bk",
        incoming.reshape(n_row * capacity, feat_q * tile_dim),
        in_hot,
        preferred_element_type=jnp.float32,
    )
    mirror_sum = mirror_sum.reshape(n_blocks, feat_q, tile_dim).transpose(1, 0, 2)
    z_part = (local_sum + mirror_sum).reshape(feat_q, rows).astype(jnp.bfloat16)
    w_rows = lax.dynamic_slice_in_dim(weight, lax.axis_index("col") * feat_q, feat_q, 0)
    partial_y = lax.dot_general(
        z_part, w_rows, (((0,), (0,)), ((), ())), preferred_element_type=jnp.float32
    )
    y_full = lax.psum(partial_y, "col")
    act = jax.nn.silu(y_full).astype(jnp.bfloat16)
    sig = jax.nn.sigmoid(y_full)
    grad_y = (cotangent.astype(jnp.float32) * sig * (1.0 + y_full * (1.0 - sig))).astype(
        jnp.bfloat16
    )
    grad_part = jnp.dot(z_part, grad_y, preferred_element_type=jnp.float32)
    grad_w = lax.psum(grad_part, "row")
    return (act, grad_w)


def solution(mesh):
    in_specs = (
        P("col", "row"),
        P("row", None, None),
        P("row", None),
        P("row", None),
        P(),
        P("row", None),
    )
    out_specs = (P("row", None), P("col", None))
    return jax.shard_map(body, mesh=mesh, in_specs=in_specs, out_specs=out_specs, check_vma=False)
```

profile of v0, /device:TPU:0, one launch (start us, length us, event | category | flops | bytes accessed | tf_op | source)
XLA Modules:
  0.0 130.2 jit_solution(15986856091040692897)
XLA Ops:
  7.2 0.0 copy-start
  7.2 0.8 fusion.37
  7.9 0.0 copy-start.2
  7.9 0.7 copy-done.2
  8.6 0.1 fusion.24
  8.7 0.2 select_reduce_fusion
  8.9 0.6 scatter_custom_fusion
  9.5 0.7 all_to_all.16
  10.2 0.0 copy-start.3
  10.2 7.4 %all-to-all-start = ((s32[8,1,2]{2,1,0:T(1,128)}), s32[8,1,2]{2,1,0:T(1,128)S(1)}, u32[]{:S(2)}, u32[]{:S(2)}) async-start(s32[8,1,2]{2,1,0:T(1,128)} %bitcast.7), calls=%async_computation | async-start | bytes 8192 | tf_op jit(solution)/shard_map/all_to_all | solution.py:34
  17.6 0.0 copy-done.3
  17.6 0.9 bitcast_bitcast_fusion.1
  18.5 0.6 gather_fusion.2
  19.0 0.0 copy-done
  19.1 0.2 fusion.1
  19.3 0.8 scatter_custom_fusion.1
  20.1 0.7 reshape.80
  20.8 3.1 %all-to-all-done = s32[8,1,2]{2,1,0:T(1,128)S(1)} async-done(((s32[8,1,2]{2,1,0:T(1,128)}), s32[8,1,2]{2,1,0:T(1,128)S(1)}, u32[]{:S(2)}, u32[]{:S(2)}) %all-to-all-start) | async-done | bytes 96 | tf_op jit(solution)/shard_map/all_to_all | solution.py:34
  24.0 3.4 %all-to-all-start.2 = ((bf16[8,2,4096]{2,1,0:T(2,128)(2,1)}), bf16[8,2,4096]{2,1,0:T(2,128)(2,1)S(1)}, u32[]{:S(2)}, u32[]{:S(2)}) async-start(bf16[8,2,4096]{2,1,0:T(2,128)(2,1)} %reshape.80), calls=%async_computation.2 | async-start | bytes 262144 | tf_op jit(solution)/shard_map/all_to_all | solution.py:37
  27.4 0.1 copy.33
  27.4 0.1 copy.34
  27.5 0.1 copy.37
  27.6 0.1 reshape.84
  27.7 0.6 gather_fusion
  28.4 0.1 reshape.83
  28.5 0.8 broadcast_select_fusion
  29.3 5.3 %all-to-all-done.2 = bf16[8,2,4096]{2,1,0:T(2,128)(2,1)S(1)} async-done(((bf16[8,2,4096]{2,1,0:T(2,128)(2,1)}), bf16[8,2,4096]{2,1,0:T(2,128)(2,1)S(1)}, u32[]{:S(2)}, u32[]{:S(2)}) %all-to-all-start.2) | async-done | bytes 131104 | tf_op jit(solution)/shard_map/all_to_all | solution.py:37
  34.6 3.4 %all-to-all-start.1 = ((bf16[8,2,4096]{2,1,0:T(2,128)(2,1)}), bf16[8,2,4096]{2,1,0:T(2,128)(2,1)S(1)}, u32[]{:S(2)}, u32[]{:S(2)}) async-start(bf16[8,2,4096]{2,1,0:T(2,128)(2,1)} %broadcast_select_fusion), calls=%async_computation.1 | async-start | bytes 262144 | tf_op jit(solution)/shard_map/all_to_all | solution.py:36
  38.0 0.0 all-reduce.2.cloned.1.call-start
  38.1 0.5 broadcast.107
  38.6 0.7 reduce.3
  39.3 0.1 eq.53
  39.3 0.1 reshape.81
  39.4 5.9 %all-to-all-done.1 = bf16[8,2,4096]{2,1,0:T(2,128)(2,1)S(1)} async-done(((bf16[8,2,4096]{2,1,0:T(2,128)(2,1)}), bf16[8,2,4096]{2,1,0:T(2,128)(2,1)S(1)}, u32[]{:S(2)}, u32[]{:S(2)}) %all-to-all-start.1) | async-done | bytes 131104 | tf_op jit(solution)/shard_map/all_to_all | solution.py:36
  45.3 0.1 reshape.78
  45.4 0.6 gather_fusion.1
  46.0 0.3 fusion.15
  46.3 0.3 fusion.5
  46.5 0.1 fusion
  46.7 2.1 %fusion.8 = f32[1024,256]{1,0:T(8,128)} fusion(bf16[4,8,8,128]{3,2,1,0:T(8,128)(2,1)S(1)} %bitcast.68, bf16[128,256]{1,0:T(8,128)(2,1)} %param.10, s32[]{:T(128)S(6)} %select_n.53), kind=kOutput, calls=%fused_computation.19 | convolution fusion | flops 16777216 | bytes 1130500 | tf_op jit(solution)/shard_map/dot_general | solution.py:55
  48.8 0.0 copy-start.4
  48.8 0.0 all-reduce.2.cloned.1.call-update
  48.8 34.0 %all-reduce.2.cloned.1.call-done = f32[1024,256]{1,0:T(8,128)} async-done(((f32[1024,256]{1,0:T(8,128)}), f32[1024,256]{1,0:T(8,128)}) %all-reduce.2.cloned.1.call-update) | async-done | bytes 1048592 | tf_op jit(solution)/shard_map/psum | solution.py:58
  82.8 0.0 copy-done.4
  82.8 1.8 %fusion.2 = f32[32,256]{1,0:T(8,128)S(1)} fusion(f32[1024,256]{1,0:T(8,128)} %all-reduce.2.cloned.1.call-done, bf16[1024,256]{1,0:T(8,128)(2,1)S(1)} %copy-done.4, bf16[4,8,8,128]{3,2,1,0:T(8,128)(2,1)S(1)} %bitcast.69), kind=kOutput, calls=%fused_computation.12 | convolution fusion | flops 19398656 | bytes 1671168 | tf_op jit(solution)/shard_map/dot_general | solution.py:64
  84.6 37.7 %psum.15 = f32[32,256]{1,0:T(8,128)} all-reduce(f32[32,256]{1,0:T(8,128)S(1)} %fusion.2), channel_id=1, replica_groups=mesh['row'=8,'col'=4] {'row'}, use_global_device_ids=true, to_apply=%region_5.6 | all-reduce | flops 8192 | bytes 65536 | tf_op jit(solution)/shard_map/psum | solution.py:65
  122.3 0.0 copy-done.1
  122.3 1.1 multiply_convert_fusion.1
  (10 shorter events, 0.1 us)
Async XLA Ops:
  7.2 11.9 %copy-start = (bf16[8,128,128]{2,1,0:T(8,128)(2,1)S(1)}, bf16[8,128,128]{2,1,0:T(8,128)(2,1)}, u32[]{:S(2)}) copy-start(bf16[8,128,128]{2,1,0:T(8,128)(2,1)} %param.7) | copy-start | bytes 786436
  7.9 0.7 copy-start.2
  10.2 7.4 %copy-start.3 = (s32[8,2]{0,1:T(2,128)S(1)}, s32[8,2]{0,1:T(2,128)}, u32[]{:S(2)}) copy-start(s32[8,2]{0,1:T(2,128)} %param.9) | copy-start | bytes 196
  10.2 13.8 %all-to-all-start = ((s32[8,1,2]{2,1,0:T(1,128)}), s32[8,1,2]{2,1,0:T(1,128)S(1)}, u32[]{:S(2)}, u32[]{:S(2)}) async-start(s32[8,1,2]{2,1,0:T(1,128)} %bitcast.7), calls=%async_computation | async-start | bytes 8192 | tf_op jit(solution)/shard_map/all_to_all | solution.py:34
  24.0 10.7 %all-to-all-start.2 = ((bf16[8,2,4096]{2,1,0:T(2,128)(2,1)}), bf16[8,2,4096]{2,1,0:T(2,128)(2,1)S(1)}, u32[]{:S(2)}, u32[]{:S(2)}) async-start(bf16[8,2,4096]{2,1,0:T(2,128)(2,1)} %reshape.80), calls=%async_computation.2 | async-start | bytes 262144 | tf_op jit(solution)/shard_map/all_to_all | solution.py:37
  34.6 10.7 %all-to-all-start.1 = ((bf16[8,2,4096]{2,1,0:T(2,128)(2,1)}), bf16[8,2,4096]{2,1,0:T(2,128)(2,1)S(1)}, u32[]{:S(2)}, u32[]{:S(2)}) async-start(bf16[8,2,4096]{2,1,0:T(2,128)(2,1)} %broadcast_select_fusion), calls=%async_computation.1 | async-start | bytes 262144 | tf_op jit(solution)/shard_map/all_to_all | solution.py:36
  38.0 44.8 %all-reduce.2.cloned.1.call-start = ((), (), s32[]{:S(2)}) async-start(), calls=%async_computation.3 | async-start | bytes 2097152 | tf_op jit(solution)/shard_map/psum | solution.py:58
  48.8 34.0 %copy-start.4 = (bf16[1024,256]{1,0:T(8,128)(2,1)S(1)}, bf16[1024,256]{1,0:T(8,128)(2,1)}, u32[]{:S(2)}) copy-start(bf16[1024,256]{1,0:T(8,128)(2,1)} %param.11) | copy-start | bytes 1572868
  82.8 39.5 %copy-start.1 = (f32[1024,256]{1,0:T(8,128)S(1)}, f32[1024,256]{1,0:T(8,128)}, u32[]{:S(2)}) copy-start(f32[1024,256]{1,0:T(8,128)} %all-reduce.2.cloned.1.call-done) | copy-start | bytes 3145732
Sparse Core Ops, SparseCore 0:
  48.9 33.8 all-reduce.1
where the time goes:
time: 131 us; the launch traced here: 130 us
  waiting for transfers between devices  48.4 us (37%)
  blocking collectives  37.7 us (29%)
  starting transfers between devices  14.2 us (11%)
  between operations  14.2 us (11%)
  local copies, waits for them, and re-layouts  7.28 us (6%)
  matrix products  4.85 us (4%)
  other arithmetic  3.66 us (3%)
    psum x1, blocking collectives, body(): grad_w = lax.psum(grad_part, 'row')  37.7 us
    psum x1, waiting for transfers between devices, body(): y_full = lax.psum(partial_y, 'col')  34 us
    all_to_all x1, starting transfers between devices, body(): lax.all_to_all(requests, 'row', split_axis=0, concat_axis=0, tiled=True)  7.41 us
    all_to_all x1, waiting for transfers between devices, body(): lax.all_to_all(picked, 'row', split_axis=0, concat_axis=0, tiled=True)  5.9 us
    all_to_all x1, waiting for transfers between devices, body(): lax.all_to_all(outgoing, 'row', split_axis=0, concat_axis=0, tiled=True)  5.33 us
    all_to_all x1, starting transfers between devices, body(): lax.all_to_all(picked, 'row', split_axis=0, concat_axis=0, tiled=True)  3.37 us
    all_to_all x1, starting transfers between devices, body(): lax.all_to_all(outgoing, 'row', split_axis=0, concat_axis=0, tiled=True)  3.37 us
    all_to_all x1, waiting for transfers between devices, body(): lax.all_to_all(requests, 'row', split_axis=0, concat_axis=0, tiled=True)  3.14 us
  transfers between devices with their start and end apart: 4, of which 4 were waited for; matrix products, arithmetic and copies ran while one was open for 5% of the time, Pallas kernels for 0%

commit v1 on v0

--- a/solution.py
+++ b/solution.py
@@ -4,8 +4,34 @@
 from jax.sharding import PartitionSpec as P
 
 
+def gather_groups(z_part, n_col):
+    if n_col == 1:
+        return z_part
+    me = lax.axis_index("col")
+    parts = [z_part]
+    for k in range(1, n_col):
+        perm = [(i, (i + k) % n_col) for i in range(n_col)]
+        parts.append(lax.ppermute(z_part, "col", perm))
+    stacked = jnp.stack(parts)
+    order = (me - jnp.arange(n_col, dtype=jnp.int32)) % n_col
+    full = jnp.take(stacked, order, axis=0)
+    return full.reshape(n_col * z_part.shape[0], z_part.shape[1])
+
+
+def sum_over_row(x, n_row):
+    if n_row & (n_row - 1):
+        return lax.psum(x, "row")
+    k = 1
+    while k < n_row:
+        perm = [(i, i ^ k) for i in range(n_row)]
+        x = x + lax.ppermute(x, "row", perm)
+        k *= 2
+    return x
+
+
 def body(x_t, tiles, tile_owner, tile_local, weight, cotangent):
     n_row = lax.axis_size("row")
+    n_col = lax.axis_size("col")
     n_tiles, tile_dim = (tiles.shape[0], tiles.shape[1])
     feat_q, rows = x_t.shape
     n_blocks = rows // tile_dim
@@ -33,8 +59,11 @@
     )
     block_ids = lax.all_to_all(requests, "row", split_axis=0, concat_axis=0, tiled=True)
     picked = jnp.take(flat_blocks, block_ids, axis=0)
-    fetched = lax.all_to_all(picked, "row", split_axis=0, concat_axis=0, tiled=True)
-    incoming = lax.all_to_all(outgoing, "row", split_axis=0, concat_axis=0, tiled=True)
+    both = lax.all_to_all(
+        jnp.concatenate([picked, outgoing], axis=1), "row", split_axis=0, concat_axis=0, tiled=True
+    )
+    fetched = both[:, :capacity]
+    incoming = both[:, capacity:]
     fetched_tiles = jnp.take(fetched.reshape(n_row * capacity, feat_q, tile_dim), slot, axis=0)
     forward_terms = jnp.einsum(
         "tfj,tij->tfi", fetched_tiles, tiles, preferred_element_type=jnp.float32
@@ -51,18 +80,17 @@
     )
     mirror_sum = mirror_sum.reshape(n_blocks, feat_q, tile_dim).transpose(1, 0, 2)
     z_part = (local_sum + mirror_sum).reshape(feat_q, rows).astype(jnp.bfloat16)
-    w_rows = lax.dynamic_slice_in_dim(weight, lax.axis_index("col") * feat_q, feat_q, 0)
-    partial_y = lax.dot_general(
-        z_part, w_rows, (((0,), (0,)), ((), ())), preferred_element_type=jnp.float32
+    z_full = gather_groups(z_part, n_col)
+    y_full = lax.dot_general(
+        z_full, weight, (((0,), (0,)), ((), ())), preferred_element_type=jnp.float32
     )
-    y_full = lax.psum(partial_y, "col")
     act = jax.nn.silu(y_full).astype(jnp.bfloat16)
     sig = jax.nn.sigmoid(y_full)
     grad_y = (cotangent.astype(jnp.float32) * sig * (1.0 + y_full * (1.0 - sig))).astype(
         jnp.bfloat16
     )
     grad_part = jnp.dot(z_part, grad_y, preferred_element_type=jnp.float32)
-    grad_w = lax.psum(grad_part, "row")
+    grad_w = sum_over_row(grad_part, n_row)
     return (act, grad_w)
 
 

time: 131 us -> 56.1 us (0.43)
  blocking collectives: 37.7 us -> 0 us
  waiting for transfers between devices: 48.4 us -> 25.2 us
  between operations: 14.2 us -> 0.86 us
  matrix products: 4.85 us -> 2.71 us
    psum x1 -> x0, blocking collectives: 37.7 us -> none  [body(): grad_w = lax.psum(grad_part, 'row')]
    psum x1 -> x0, waiting for transfers between devices: 34 us -> none  [body(): y_full = lax.psum(partial_y, 'col')]
    ppermute x0 -> x6, waiting for transfers between devices: none -> 14.8 us  [the longest x3 10.7 us: sum_over_row(): x = x + lax.ppermute(x, 'row', perm)]
    all_to_all x2 -> x1, waiting for transfers between devices: 11.2 us -> 6.69 us  [body(): lax.all_to_all(jnp.concatenate([picked, outgoing], axis=1), 'row', split_...]
    ppermute x0 -> x6, starting transfers between devices: none -> 3.96 us  [the longest x3 2.18 us: sum_over_row(): x = x + lax.ppermute(x, 'row', perm)]
    all_to_all x2 -> x1, starting transfers between devices: 6.74 us -> 3.41 us  [body(): lax.all_to_all(jnp.concatenate([picked, outgoing], axis=1), 'row', split_...]
    unnamed x11 -> x13, local copies, waits for them, and re-layouts: 0.7 us -> 2.31 us
    dot_general x1, matrix products: 1.84 us -> 0.52 us  [body(): grad_part = jnp.dot(z_part, grad_y, preferred_element_type=jnp.float32)]
  transfers between devices with their start and end apart: 4 -> 8, of which waited for: 4 -> 8; matrix products, arithmetic and copies ran while one was open for 5% -> 7% of each run, Pallas kernels for 0% -> 0%
where the time goes in v1:
time: 56.1 us; the launch traced here: 55.7 us
  waiting for transfers between devices  25.2 us (45%)
  starting transfers between devices  14.8 us (26%)
  local copies, waits for them, and re-layouts  8.38 us (15%)
  other arithmetic  3.71 us (7%)
  matrix products  2.71 us (5%)
  between operations  0.86 us (2%)
    ppermute x3, waiting for transfers between devices, sum_over_row(): x = x + lax.ppermute(x, 'row', perm)  10.7 us
    all_to_all x1, starting transfers between devices, body(): lax.all_to_all(requests, 'row', split_axis=0, concat_axis=0, tiled=True)  7.41 us
    all_to_all x1, waiting for transfers between devices, body(): lax.all_to_all(jnp.concatenate([picked, outgoing], axis=1), 'row', split_...  6.69 us
    ppermute x3, waiting for transfers between devices, gather_groups(): parts.append(lax.ppermute(z_part, 'col', perm))  4.06 us
    all_to_all x1, waiting for transfers between devices, body(): lax.all_to_all(requests, 'row', split_axis=0, concat_axis=0, tiled=True)  3.77 us
    all_to_all x1, starting transfers between devices, body(): lax.all_to_all(jnp.concatenate([picked, outgoing], axis=1), 'row', split_...  3.41 us
    unnamed x13, local copies, waits for them, and re-layouts  2.31 us
    ppermute x3, starting transfers between devices, sum_over_row(): x = x + lax.ppermute(x, 'row', perm)  2.18 us
  transfers between devices with their start and end apart: 8, of which 8 were waited for; matrix products, arithmetic and copies ran while one was open for 7% of the time, Pallas kernels for 0%

profile of v1, /device:TPU:0, one launch (start us, length us, event | category | flops | bytes accessed | tf_op | source)
XLA Modules:
  0.0 55.7 jit_solution(13285435770127501888)
XLA Ops:
  0.6 0.8 %slice_bitcast_fusion.1 = (s32[8]{0:T(128)S(1)}, s32[8]{0:T(128)S(1)}, s32[8]{0:T(128)S(1)}) fusion(s32[8,2]{0,1:T(2,128)} %param.9), kind=kLoop, calls=%fused_computation.71 | loop fusion | flops 24 | bytes 160 | tf_op jit(solution)/shard_map/eq | solution.py:72
  1.4 0.7 %copy-done.1 = s32[8,1]{0,1:T(1,128)S(1)} copy-done((s32[8,1]{0,1:T(1,128)S(1)}, s32[8,1]{0,1:T(1,128)}, u32[]{:S(2)}) %copy-start.1) | copy-done | bytes 56
  2.2 0.2 select_reduce_fusion
  2.4 0.6 %scatter_custom_fusion = s32[16]{0:T(128)S(1)} fusion(s32[8]{0:T(128)S(1)} %bitcast.87, s32[8]{0:T(128)S(1)} %get-tuple-element.10, s32[]{:T(128)} %constant.81.clone.1), kind=kCustom, calls=%fused_computation.72 | custom fusion | bytes 68 | tf_op jit(solution)/shard_map/scatter | solution.py:48
  3.0 0.7 %all_to_all.13 = s32[8,1,2]{2,0,1:T(8,128)} reshape(s32[16]{0:T(128)S(1)} %scatter_custom_fusion) | data formatting | bytes 128 | tf_op jit(solution)/shard_map/all_to_all | solution.py:60
  3.6 7.4 %all-to-all-start = ((s32[8,1,2]{2,1,0:T(1,128)}), s32[8,1,2]{2,1,0:T(1,128)S(1)}, u32[]{:S(2)}, u32[]{:S(2)}) async-start(s32[8,1,2]{2,1,0:T(1,128)} %bitcast.7), calls=%async_computation | async-start | bytes 8192 | tf_op jit(solution)/shard_map/all_to_all | solution.py:60
  11.1 0.9 %bitcast_bitcast_fusion = (bf16[1,8,32,128]{3,2,1,0:T(8,128)(2,1)S(1)}, bf16[8,32,128]{2,1,0:T(8,128)(2,1)S(1)}) fusion(bf16[32,1024]{1,0:T(8,128)(2,1)} %param.6), kind=kLoop, calls=%fused_computation.27 | loop fusion | bytes 196608
  12.0 0.6 %gather_fusion.1 = bf16[8,32,128]{2,1,0:T(8,128)(2,1)S(1)} fusion(bf16[8,32,128]{2,1,0:T(8,128)(2,1)S(1)} %get-tuple-element.7, s32[1024]{0:T(1024)S(1)} %pad_clamp_fusion.2), kind=kCustom, calls=%fused_computation.1 | custom fusion | bytes 131104 | tf_op jit(solution)/shard_map/jit(_take)/gather | solution.py:50
  12.6 0.2 fusion.1
  12.8 0.8 %scatter_custom_fusion.1 = bf16[16,4096]{1,0:T(8,128)(2,1)S(1)} fusion(s32[8]{0:T(128)S(1)} %bitcast.88, bf16[1,8,32,128]{3,2,1,0:T(8,128)(2,1)S(1)} %fusion.1, bf16[]{:T(256)} %constant.91.clone.1), kind=kCustom, calls=%fused_computation.23 | custom fusion | bytes 196610 | tf_op jit(solution)/shard_map/scatter | solution.py:57
  13.6 0.1 reshape.147
  13.7 3.8 %all-to-all-done = s32[8,1,2]{2,1,0:T(1,128)S(1)} async-done(((s32[8,1,2]{2,1,0:T(1,128)}), s32[8,1,2]{2,1,0:T(1,128)S(1)}, u32[]{:S(2)}, u32[]{:S(2)}) %all-to-all-start) | async-done | bytes 96 | tf_op jit(solution)/shard_map/all_to_all | solution.py:60
  17.4 0.1 copy.33
  17.5 0.1 copy.34
  17.6 0.1 copy.37
  17.7 0.1 reshape.152
  17.8 0.6 %gather_fusion = bf16[16,4096]{1,0:T(8,128)(2,1)S(1)} fusion(bf16[8,4096]{1,0:T(8,128)(2,1)S(1)} %bitcast.75, s32[1024]{0:T(1024)S(1)} %pad_clamp_fusion.3), kind=kCustom, calls=%fused_computation | custom fusion | bytes 262208 | tf_op jit(solution)/shard_map/jit(_take)/gather | solution.py:61
  18.4 0.1 reshape.151
  18.5 0.2 broadcast_select_fusion
  18.7 1.0 %pad_maximum_fusion = bf16[8,4,4096]{2,1,0:T(4,128)(2,1)} fusion(bf16[8,2,4096]{2,1,0:T(2,128)(2,1)S(1)} %reshape.147, bf16[8,2,4096]{2,1,0:T(2,128)(2,1)S(1)} %broadcast_select_fusion), kind=kLoop, calls=%fused_computation.14 | loop fusion | flops 524288 | bytes 524288 | tf_op jit(solution)/shard_map/concatenate | solution.py:63
  19.7 3.4 %all-to-all-start.1 = ((bf16[8,4,4096]{2,1,0:T(4,128)(2,1)}), bf16[8,4,4096]{2,1,0:T(4,128)(2,1)S(1)}, u32[]{:S(2)}, u32[]{:S(2)}) async-start(bf16[8,4,4096]{2,1,0:T(4,128)(2,1)} %pad_maximum_fusion), calls=%async_computation.1 | async-start | bytes 524288 | tf_op jit(solution)/shard_map/all_to_all | solution.py:62
  23.2 0.1 broadcast_in_dim.51
  23.3 0.5 broadcast.211
  23.9 0.7 %reduce.3 = s32[8,2]{1,0:T(8,128)S(1)} reduce(s32[8,1,2]{2,1,0:T(1,128)S(1)} %all-to-all-done, s32[]{:T(128)} %broadcast.211), dimensions={1}, to_apply=%all_to_all.14.reduce_sub_computation.3 | reduce | bytes 132 | tf_op jit(solution)/shard_map/all_to_all | solution.py:60
  24.6 6.7 %all-to-all-done.1 = bf16[8,4,4096]{2,1,0:T(4,128)(2,1)S(1)} async-done(((bf16[8,4,4096]{2,1,0:T(4,128)(2,1)}), bf16[8,4,4096]{2,1,0:T(4,128)(2,1)S(1)}, u32[]{:S(2)}, u32[]{:S(2)}) %all-to-all-start.1) | async-done | bytes 262176 | tf_op jit(solution)/shard_map/all_to_all | solution.py:62
  31.3 0.2 fusion.34
  31.6 0.1 reshape.148
  31.7 0.6 %gather_fusion.2 = bf16[8,32,128]{2,1,0:T(8,128)(2,1)S(1)} fusion(bf16[16,32,128]{2,1,0:T(8,128)(2,1)S(1)} %reshape.148, s32[1024]{0:T(1024)S(1)} %pad_clamp_fusion.1), kind=kCustom, calls=%fused_computation.2 | custom fusion | bytes 131104 | tf_op jit(solution)/shard_map/jit(_take)/gather | solution.py:67
  32.3 0.3 fusion.10
  32.6 0.3 fusion.5
  32.8 0.1 fusion
  33.1 1.6 %collective-permute-start.1 = (bf16[32,1024]{1,0:T(8,128)(2,1)S(1)}, bf16[32,1024]{1,0:T(8,128)(2,1)S(1)}, u32[]{:S(2)}, u32[]{:S(2)}) collective-permute-start(bf16[32,1024]{1,0:T(8,128)(2,1)S(1)} %bitcast.80), channel_id=1, source_target_pairs={{0,2},{1,3},{2,0},{3,1},{4,6},{5,7},{6,4},{7,5},{8,10},{9,11},{10,... | collective-permute-start | bytes 196616 | tf_op jit(solution)/shard_map/ppermute | solution.py:14
  34.6 0.2 collective-permute-start
  34.8 0.1 collective-permute-done.2
  35.0 3.7 %collective-permute-done.1 = bf16[32,1024]{1,0:T(8,128)(2,1)S(1)} collective-permute-done((bf16[32,1024]{1,0:T(8,128)(2,1)S(1)}, bf16[32,1024]{1,0:T(8,128)(2,1)S(1)}, u32[]{:S(2)}, u32[]{:S(2)}) %collective-permute-start.1) | collective-permute-done | bytes 65568 | tf_op jit(solution)/shard_map/ppermute | solution.py:14
  38.7 0.2 collective-permute-done
  38.9 0.6 %gather_fusion.3 = bf16[4,32,1024]{2,1,0:T(8,128)(2,1)S(1)} fusion(bf16[4,32,1024]{2,1,0:T(8,128)(2,1)S(1)} %pad_maximum_fusion.1, s32[1024]{0:T(1024)S(1)} %pad_clamp_fusion), kind=kCustom, calls=%fused_computation.3 | custom fusion | bytes 524304 | tf_op jit(solution)/shard_map/jit(_take)/gather | solution.py:17
  39.5 0.1 bitcast_select_fusion
  39.6 0.7 %copy-done.4 = bf16[128,256]{1,0:T(8,128)(2,1)S(1)} copy-done((bf16[128,256]{1,0:T(8,128)(2,1)S(1)}, bf16[128,256]{1,0:T(8,128)(2,1)}, u32[]{:S(2)}) %copy-start.4) | copy-done | bytes 65560
  40.4 1.3 %multiply_convert_fusion.1 = (bf16[1024,256]{1,0:T(8,128)(2,1)}, f32[1024,256]{1,0:T(8,128)S(1)}) fusion(bf16[128,1024]{1,0:T(8,128)(2,1)S(1)} %bitcast_select_fusion, bf16[128,256]{1,0:T(8,128)(2,1)S(1)} %copy-done.4), kind=kOutput, calls=%fused_computation.11 | convolution fusion | flops 68419584 | bytes 1900544 | tf_op jit(solution)/shard_map/dot_general | solution.py:84
  41.6 0.5 fusion.2
  42.1 1.2 %collective-permute-start.3 = (f32[32,256]{1,0:T(8,128)S(1)}, f32[32,256]{1,0:T(8,128)S(1)}, u32[]{:S(2)}, u32[]{:S(2)}) collective-permute-start(f32[32,256]{1,0:T(8,128)S(1)} %fusion.2), channel_id=1, source_target_pairs={{0,4},{4,0},{8,12},{12,8},{16,20},{20,16},{24,28},{28,24},{1,5},{5... | collective-permute-start | bytes 98312 | tf_op jit(solution)/shard_map/ppermute | solution.py:27
  43.4 2.8 %collective-permute-done.3 = f32[32,256]{1,0:T(8,128)S(1)} collective-permute-done((f32[32,256]{1,0:T(8,128)S(1)}, f32[32,256]{1,0:T(8,128)S(1)}, u32[]{:S(2)}, u32[]{:S(2)}) %collective-permute-start.3) | collective-permute-done | bytes 32800 | tf_op jit(solution)/shard_map/ppermute | solution.py:27
  46.1 0.1 collective-permute-start.4
  46.2 3.8 %collective-permute-done.4 = f32[32,256]{1,0:T(8,128)S(1)} collective-permute-done((f32[32,256]{1,0:T(8,128)S(1)}, f32[32,256]{1,0:T(8,128)S(1)}, u32[]{:S(2)}, u32[]{:S(2)}) %collective-permute-start.4) | collective-permute-done | bytes 32800 | tf_op jit(solution)/shard_map/ppermute | solution.py:27
  50.1 0.9 %collective-permute-start.5 = (f32[32,256]{1,0:T(8,128)S(1)}, f32[32,256]{1,0:T(8,128)S(1)}, u32[]{:S(2)}, u32[]{:S(2)}) collective-permute-start(f32[32,256]{1,0:T(8,128)S(1)} %add.101), channel_id=1, source_target_pairs={{0,16},{4,20},{8,24},{12,28},{16,0},{20,4},{24,8},{28,12},{1,17},{... | collective-permute-start | bytes 98312 | tf_op jit(solution)/shard_map/ppermute | solution.py:27
  50.9 4.1 %collective-permute-done.5 = f32[32,256]{1,0:T(8,128)S(1)} collective-permute-done((f32[32,256]{1,0:T(8,128)S(1)}, f32[32,256]{1,0:T(8,128)S(1)}, u32[]{:S(2)}, u32[]{:S(2)}) %collective-permute-start.5) | collective-permute-done | bytes 32800 | tf_op jit(solution)/shard_map/ppermute | solution.py:27
  55.0 0.6 %add.102 = f32[32,256]{1,0:T(8,128)} add(f32[32,256]{1,0:T(8,128)S(1)} %add.101, f32[32,256]{1,0:T(8,128)S(1)} %collective-permute-done.5) | non-fusion elementwise | flops 8192 | bytes 98304 | tf_op jit(solution)/shard_map/add | solution.py:27
  (30 shorter events, 0.6 us)
Async XLA Ops:
  0.6 11.9 %copy-start = (bf16[8,128,128]{2,1,0:T(8,128)(2,1)S(1)}, bf16[8,128,128]{2,1,0:T(8,128)(2,1)}, u32[]{:S(2)}) copy-start(bf16[8,128,128]{2,1,0:T(8,128)(2,1)} %param.7) | copy-start | bytes 786436
  1.4 0.7 %copy-start.1 = (s32[8,1]{0,1:T(1,128)S(1)}, s32[8,1]{0,1:T(1,128)}, u32[]{:S(2)}) copy-start(s32[8,1]{0,1:T(1,128)} %param.8) | copy-start | bytes 100
  3.6 7.4 %copy-start.2 = (s32[8,2]{0,1:T(2,128)S(1)}, s32[8,2]{0,1:T(2,128)}, u32[]{:S(2)}) copy-start(s32[8,2]{0,1:T(2,128)} %param.9) | copy-start | bytes 196
  3.6 13.8 %all-to-all-start = ((s32[8,1,2]{2,1,0:T(1,128)}), s32[8,1,2]{2,1,0:T(1,128)S(1)}, u32[]{:S(2)}, u32[]{:S(2)}) async-start(s32[8,1,2]{2,1,0:T(1,128)} %bitcast.7), calls=%async_computation | async-start | bytes 8192 | tf_op jit(solution)/shard_map/all_to_all | solution.py:60
  19.7 11.6 %all-to-all-start.1 = ((bf16[8,4,4096]{2,1,0:T(4,128)(2,1)}), bf16[8,4,4096]{2,1,0:T(4,128)(2,1)S(1)}, u32[]{:S(2)}, u32[]{:S(2)}) async-start(bf16[8,4,4096]{2,1,0:T(4,128)(2,1)} %pad_maximum_fusion), calls=%async_computation.1 | async-start | bytes 524288 | tf_op jit(solution)/shard_map/all_to_all | solution.py:62
  33.0 2.0 %collective-permute-start.2 = (bf16[32,1024]{1,0:T(8,128)(2,1)S(1)}, bf16[32,1024]{1,0:T(8,128)(2,1)S(1)}, u32[]{:S(2)}, u32[]{:S(2)}) collective-permute-start(bf16[32,1024]{1,0:T(8,128)(2,1)S(1)} %bitcast.79), channel_id=1, source_target_pairs={{0,3},{1,0},{2,1},{3,2},{4,7},{5,4},{6,5},{7,6},{8,11},{9,8},{10,9... | collective-permute-start | bytes 196616 | tf_op jit(solution)/shard_map/ppermute | solution.py:14
  33.1 5.6 %collective-permute-start.1 = (bf16[32,1024]{1,0:T(8,128)(2,1)S(1)}, bf16[32,1024]{1,0:T(8,128)(2,1)S(1)}, u32[]{:S(2)}, u32[]{:S(2)}) collective-permute-start(bf16[32,1024]{1,0:T(8,128)(2,1)S(1)} %bitcast.80), channel_id=1, source_target_pairs={{0,2},{1,3},{2,0},{3,1},{4,6},{5,7},{6,4},{7,5},{8,10},{9,11},{10,... | collective-permute-start | bytes 196616 | tf_op jit(solution)/shard_map/ppermute | solution.py:14
  34.6 4.3 %collective-permute-start = (bf16[32,1024]{1,0:T(8,128)(2,1)S(1)}, bf16[32,1024]{1,0:T(8,128)(2,1)S(1)}, u32[]{:S(2)}, u32[]{:S(2)}) collective-permute-start(bf16[32,1024]{1,0:T(8,128)(2,1)S(1)} %bitcast.81), channel_id=1, source_target_pairs={{0,1},{1,2},{2,3},{3,0},{4,5},{5,6},{6,7},{7,4},{8,9},{9,10},{10,1... | collective-permute-start | bytes 196616 | tf_op jit(solution)/shard_map/ppermute | solution.py:14
  39.5 0.8 %copy-start.4 = (bf16[128,256]{1,0:T(8,128)(2,1)S(1)}, bf16[128,256]{1,0:T(8,128)(2,1)}, u32[]{:S(2)}) copy-start(bf16[128,256]{1,0:T(8,128)(2,1)} %param.10) | copy-start | bytes 196612
  40.4 1.3 %copy-start.3 = (bf16[1024,256]{1,0:T(8,128)(2,1)S(1)}, bf16[1024,256]{1,0:T(8,128)(2,1)}, u32[]{:S(2)}) copy-start(bf16[1024,256]{1,0:T(8,128)(2,1)} %param.11) | copy-start | bytes 1572868
  42.1 4.0 %collective-permute-start.3 = (f32[32,256]{1,0:T(8,128)S(1)}, f32[32,256]{1,0:T(8,128)S(1)}, u32[]{:S(2)}, u32[]{:S(2)}) collective-permute-start(f32[32,256]{1,0:T(8,128)S(1)} %fusion.2), channel_id=1, source_target_pairs={{0,4},{4,0},{8,12},{12,8},{16,20},{20,16},{24,28},{28,24},{1,5},{5... | collective-permute-start | bytes 98312 | tf_op jit(solution)/shard_map/ppermute | solution.py:27
  46.1 3.9 %collective-permute-start.4 = (f32[32,256]{1,0:T(8,128)S(1)}, f32[32,256]{1,0:T(8,128)S(1)}, u32[]{:S(2)}, u32[]{:S(2)}) collective-permute-start(f32[32,256]{1,0:T(8,128)S(1)} %add.100), channel_id=1, source_target_pairs={{0,8},{4,12},{8,0},{12,4},{16,24},{20,28},{24,16},{28,20},{1,9},{5... | collective-permute-start | bytes 98312 | tf_op jit(solution)/shard_map/ppermute | solution.py:27
  50.1 5.0 %collective-permute-start.5 = (f32[32,256]{1,0:T(8,128)S(1)}, f32[32,256]{1,0:T(8,128)S(1)}, u32[]{:S(2)}, u32[]{:S(2)}) collective-permute-start(f32[32,256]{1,0:T(8,128)S(1)} %add.101), channel_id=1, source_target_pairs={{0,16},{4,20},{8,24},{12,28},{16,0},{20,4},{24,8},{28,12},{1,17},{... | collective-permute-start | bytes 98312 | tf_op jit(solution)/shard_map/ppermute | solution.py:27

commit v2 on v1

--- a/solution.py
+++ b/solution.py
@@ -44,9 +44,11 @@
     owner_hot = (owner[:, None] == jnp.arange(n_row, dtype=jnp.int32)[None, :]).astype(jnp.int32)
     rank = jnp.sum(owner_hot * (jnp.cumsum(owner_hot, axis=0) - 1), axis=1)
     slot = owner * capacity + rank
-    requests = (
+    slot_ids = (
         jnp.zeros((n_row * capacity,), jnp.int32).at[slot].set(col_local).reshape(n_row, capacity)
     )
+    id_rows = jnp.zeros((n_row, 1, feat_q * tile_dim), jnp.bfloat16)
+    id_rows = id_rows.at[:, 0, :capacity].set(slot_ids.astype(jnp.bfloat16))
     own_blocks = jnp.take(xb, row_local, axis=0)
     mirror_terms = jnp.einsum(
         "tfi,tij->tfj", own_blocks, tiles, preferred_element_type=jnp.float32
@@ -57,14 +59,13 @@
         .set(mirror_terms.reshape(n_tiles, feat_q * tile_dim))
         .reshape(n_row, capacity, feat_q * tile_dim)
     )
-    block_ids = lax.all_to_all(requests, "row", split_axis=0, concat_axis=0, tiled=True)
-    picked = jnp.take(flat_blocks, block_ids, axis=0)
-    both = lax.all_to_all(
-        jnp.concatenate([picked, outgoing], axis=1), "row", split_axis=0, concat_axis=0, tiled=True
-    )
-    fetched = both[:, :capacity]
-    incoming = both[:, capacity:]
-    fetched_tiles = jnp.take(fetched.reshape(n_row * capacity, feat_q, tile_dim), slot, axis=0)
+    every_block = jnp.broadcast_to(flat_blocks[None], (n_row, n_blocks, feat_q * tile_dim))
+    payload = jnp.concatenate([every_block, outgoing, id_rows], axis=1)
+    got = lax.all_to_all(payload, "row", split_axis=0, concat_axis=0, tiled=True)
+    all_x = got[:, :n_blocks].reshape(n_row * n_blocks, feat_q, tile_dim)
+    incoming = got[:, n_blocks : n_blocks + capacity]
+    block_ids = got[:, n_blocks + capacity, :capacity].astype(jnp.int32)
+    fetched_tiles = jnp.take(all_x, owner * n_blocks + col_local, axis=0)
     forward_terms = jnp.einsum(
         "tfj,tij->tfi", fetched_tiles, tiles, preferred_element_type=jnp.float32
     )

time: 56.1 us -> 64.2 us (1.14)
  waiting for transfers between devices: 25.2 us -> 38.8 us
  local copies, waits for them, and re-layouts: 8.38 us -> 4.72 us
  starting transfers between devices: 14.8 us -> 11.8 us
  other arithmetic: 3.71 us -> 5.09 us
    all_to_all x2 -> x1, waiting for transfers between devices: 10.5 us -> 25.6 us  [body(): lax.all_to_all(payload, 'row', split_axis=0, concat_axis=0, tiled=True)]
    all_to_all x2 -> x1, starting transfers between devices: 10.8 us -> 7.28 us  [body(): lax.all_to_all(payload, 'row', split_axis=0, concat_axis=0, tiled=True)]
    ppermute x3, waiting for transfers between devices: 4.06 us -> 1.86 us  [gather_groups(): parts.append(lax.ppermute(z_part, 'col', perm))]
    all_to_all x3 -> x0, local copies, waits for them, and re-layouts: 1.27 us -> none  [body(): lax.all_to_all(requests, 'row', split_axis=0, concat_axis=0, tiled=True)]
    unnamed x13 -> x11, local copies, waits for them, and re-layouts: 2.31 us -> 1.05 us
    ppermute x3, starting transfers between devices: 1.78 us -> 3 us  [gather_groups(): parts.append(lax.ppermute(z_part, 'col', perm))]
    reduce_and x2 -> x1, other arithmetic: 0.02 us -> 0.77 us  [body(): fetched_tiles = jnp.take(all_x, owner * n_blocks + col_local, axis=0)]
    gather x3 -> x1, local copies, waits for them, and re-layouts: 1.29 us -> 0.57 us  [body(): fetched_tiles = jnp.take(all_x, owner * n_blocks + col_local, axis=0)]
  transfers between devices with their start and end apart: 8 -> 7, of which waited for: 8 -> 7; matrix products, arithmetic and copies ran while one was open for 7% -> 0% of each run, Pallas kernels for 0% -> 0%
where the time goes in v2:
time: 64.2 us; the launch traced here: 63.9 us
  waiting for transfers between devices  38.8 us (60%)
  starting transfers between devices  11.8 us (18%)
  other arithmetic  5.09 us (8%)
  local copies, waits for them, and re-layouts  4.72 us (7%)
  matrix products  2.72 us (4%)
  between operations  0.86 us (1%)
    all_to_all x1, waiting for transfers between devices, body(): lax.all_to_all(payload, 'row', split_axis=0, concat_axis=0, tiled=True)  25.6 us
    ppermute x3, waiting for transfers between devices, sum_over_row(): x = x + lax.ppermute(x, 'row', perm)  11.3 us
    all_to_all x1, starting transfers between devices, body(): lax.all_to_all(payload, 'row', split_axis=0, concat_axis=0, tiled=True)  7.28 us
    ppermute x3, starting transfers between devices, gather_groups(): parts.append(lax.ppermute(z_part, 'col', perm))  3 us
    ppermute x3, waiting for transfers between devices, gather_groups(): parts.append(lax.ppermute(z_part, 'col', perm))  1.86 us
    ppermute x3, starting transfers between devices, sum_over_row(): x = x + lax.ppermute(x, 'row', perm)  1.49 us
  transfers between devices with their start and end apart: 7, of which 7 were waited for; matrix products, arithmetic and copies ran while one was open for 0% of the time, Pallas kernels for 0%

profile of v2, /device:TPU:0, one launch (start us, length us, event | category | flops | bytes accessed | tf_op | source)
XLA Modules:
  0.0 63.9 jit_solution(13298071320299670246)
XLA Ops:
  0.6 0.0 copy-start
  0.6 0.8 %fusion.21 = s32[8,8]{1,0:T(8,128)S(1)} fusion(s32[8]{0:T(128)} %bitcast.82), kind=kLoop, calls=%fused_computation.46 | loop fusion | flops 128 | bytes 288 | tf_op jit(solution)/shard_map/convert_element_type | solution.py:44
  1.4 0.8 %select_reduce_fusion = s32[8]{0:T(128)S(1)} fusion(s32[8,8]{1,0:T(8,128)S(1)} %reduce_window_sum.11, s32[8]{0:T(128)} %bitcast.83), kind=kLoop, calls=%fused_computation.44 | loop fusion | flops 248 | bytes 320 | tf_op jit(solution)/shard_map/reduce_sum | solution.py:45
  2.3 0.8 %and_bitcast_fusion.1 = (pred[8]{0:T(512)(128)(4,1)S(1)}, s32[8,1]{0,1:T(1,128)S(1)}, pred[8]{0:T(512)(128)(4,1)S(1)}) fusion(s32[8,2]{0,1:T(2,128)} %param.11, s32[8,1]{0,1:T(1,128)} %param.10), kind=kLoop, calls=%fused_computation.63 | loop fusion | flops 112 | bytes 144 | tf_op jit(solution)/shard_map/jit(_take)/reduce_and | solution.py:68
  3.0 0.8 %slice_bitcast_fusion.2 = (s32[8]{0:T(128)S(1)}, s32[8]{0:T(128)S(1)}, s32[8]{0:T(128)S(1)}, s32[8]{0:T(128)S(1)}) fusion(s32[8,2]{0,1:T(2,128)} %param.11, s32[8]{0:T(128)S(1)} %select_reduce_fusion, s32[8,1]{0,1:T(1,128)} %param.10), kind=kLoop, calls=%fused_computation.72 | loop fusion | flops 64 | bytes 256 | tf_op jit(solution)/shard_map/eq | solution.py:73
  3.8 0.9 %bitcast_bitcast_fusion = (bf16[1,8,32,128]{3,2,1,0:T(8,128)(2,1)S(1)}, bf16[8,32,128]{2,1,0:T(8,128)(2,1)S(1)}) fusion(bf16[32,1024]{1,0:T(8,128)(2,1)} %param.8), kind=kLoop, calls=%fused_computation.28 | loop fusion | bytes 196608
  4.7 0.6 gather_fusion
  5.2 0.0 copy-done
  5.3 0.2 fusion.2
  5.5 0.8 %scatter_custom_fusion = bf16[16,4096]{1,0:T(8,128)(2,1)S(1)} fusion(s32[8]{0:T(128)S(1)} %get-tuple-element.24, bf16[1,8,32,128]{3,2,1,0:T(8,128)(2,1)S(1)} %fusion.2, bf16[]{:T(256)} %constant.105.clone.1), kind=kCustom, calls=%fused_computation.24 | custom fusion | bytes 196610 | tf_op jit(solution)/shard_map/scatter | solution.py:59
  6.3 0.1 reshape.155
  6.4 0.6 scatter_custom_fusion.1
  7.0 0.1 convert_element_type.72
  7.2 1.1 %fusion.3 = bf16[8,11,4096]{2,1,0:T(8,128)(2,1)} fusion(bf16[8,1,2]{2,1,0:T(2,128)(2,1)S(1)} %convert_element_type.72, bf16[8,2,4096]{2,1,0:T(2,128)(2,1)S(1)} %reshape.155, bf16[8,8,4096]{2,1,0:T(8,128)(2,1)S(1)} %broadcast_in_dim.53), kind=kLoop, calls=%fused_computation.11 | loop fusion | flops 2883584 | bytes 1376288 | tf_op jit(solution)/shard_map/concatenate | solution.py:63
  8.3 7.3 %all-to-all-start = ((bf16[8,11,4096]{2,1,0:T(8,128)(2,1)}), bf16[8,11,4096]{2,1,0:T(8,128)(2,1)S(1)}, u32[]{:S(2)}, u32[]{:S(2)}) async-start(bf16[8,11,4096]{2,1,0:T(8,128)(2,1)} %fusion.3), calls=%async_computation | async-start | bytes 2097152 | tf_op jit(solution)/shard_map/all_to_all | solution.py:64
  15.6 0.1 broadcast_in_dim.48
  15.6 0.1 broadcast_in_dim.49
  15.7 25.6 %all-to-all-done = bf16[8,11,4096]{2,1,0:T(8,128)(2,1)S(1)} async-done(((bf16[8,11,4096]{2,1,0:T(8,128)(2,1)}), bf16[8,11,4096]{2,1,0:T(8,128)(2,1)S(1)}, u32[]{:S(2)}, u32[]{:S(2)}) %all-to-all-start) | async-done | bytes 720928 | tf_op jit(solution)/shard_map/all_to_all | solution.py:64
  41.3 0.1 copy.23
  41.4 0.1 slice.51
  41.5 0.1 reshape.157
  41.6 0.1 reshape.158
  41.7 0.6 gather_fusion.1
  42.3 0.3 fusion.12
  42.5 0.3 fusion.7
  42.8 0.0 copy-start.2
  42.8 0.1 fusion.1
  43.0 0.1 collective-permute-start
  43.1 1.6 %collective-permute-start.1 = (bf16[32,1024]{1,0:T(8,128)(2,1)S(1)}, bf16[32,1024]{1,0:T(8,128)(2,1)S(1)}, u32[]{:S(2)}, u32[]{:S(2)}) collective-permute-start(bf16[32,1024]{1,0:T(8,128)(2,1)S(1)} %bitcast.77), channel_id=1, source_target_pairs={{0,2},{1,3},{2,0},{3,1},{4,6},{5,7},{6,4},{7,5},{8,10},{9,11},{10,... | collective-permute-start | bytes 196616 | tf_op jit(solution)/shard_map/ppermute | solution.py:14
  44.6 1.4 %collective-permute-start.2 = (bf16[32,1024]{1,0:T(8,128)(2,1)S(1)}, bf16[32,1024]{1,0:T(8,128)(2,1)S(1)}, u32[]{:S(2)}, u32[]{:S(2)}) collective-permute-start(bf16[32,1024]{1,0:T(8,128)(2,1)S(1)} %bitcast.78), channel_id=1, source_target_pairs={{0,3},{1,0},{2,1},{3,2},{4,7},{5,4},{6,5},{7,6},{8,11},{9,8},{10,9... | collective-permute-start | bytes 196616 | tf_op jit(solution)/shard_map/ppermute | solution.py:14
  46.0 0.8 %collective-permute-done = bf16[32,1024]{1,0:T(8,128)(2,1)S(1)} collective-permute-done((bf16[32,1024]{1,0:T(8,128)(2,1)S(1)}, bf16[32,1024]{1,0:T(8,128)(2,1)S(1)}, u32[]{:S(2)}, u32[]{:S(2)}) %collective-permute-start) | collective-permute-done | bytes 65568 | tf_op jit(solution)/shard_map/ppermute | solution.py:14
  46.8 0.9 %collective-permute-done.1 = bf16[32,1024]{1,0:T(8,128)(2,1)S(1)} collective-permute-done((bf16[32,1024]{1,0:T(8,128)(2,1)S(1)}, bf16[32,1024]{1,0:T(8,128)(2,1)S(1)}, u32[]{:S(2)}, u32[]{:S(2)}) %collective-permute-start.1) | collective-permute-done | bytes 65568 | tf_op jit(solution)/shard_map/ppermute | solution.py:14
  47.7 0.2 collective-permute-done.2
  47.9 0.6 gather_fusion.2
  48.5 0.1 bitcast_select_fusion
  48.6 0.0 copy-done.2
  48.6 0.0 copy-start.1
  48.6 1.3 %multiply_convert_fusion.1 = (bf16[1024,256]{1,0:T(8,128)(2,1)}, f32[1024,256]{1,0:T(8,128)S(1)}) fusion(bf16[128,1024]{1,0:T(8,128)(2,1)S(1)} %bitcast_select_fusion, bf16[128,256]{1,0:T(8,128)(2,1)S(1)} %copy-done.2), kind=kOutput, calls=%fused_computation.13 | convolution fusion | flops 68419584 | bytes 1900544 | tf_op jit(solution)/shard_map/dot_general | solution.py:85
  49.9 0.0 copy-done.1
  49.9 0.5 fusion.4
  50.4 1.5 %collective-permute-start.3 = (f32[32,256]{1,0:T(8,128)S(1)}, f32[32,256]{1,0:T(8,128)S(1)}, u32[]{:S(2)}, u32[]{:S(2)}) collective-permute-start(f32[32,256]{1,0:T(8,128)S(1)} %fusion.4), channel_id=1, source_target_pairs={{0,4},{4,0},{8,12},{12,8},{16,20},{20,16},{24,28},{28,24},{1,5},{5... | collective-permute-start | bytes 98312 | tf_op jit(solution)/shard_map/ppermute | solution.py:27
  51.9 2.6 %collective-permute-done.3 = f32[32,256]{1,0:T(8,128)S(1)} collective-permute-done((f32[32,256]{1,0:T(8,128)S(1)}, f32[32,256]{1,0:T(8,128)S(1)}, u32[]{:S(2)}, u32[]{:S(2)}) %collective-permute-start.3) | collective-permute-done | bytes 32800 | tf_op jit(solution)/shard_map/ppermute | solution.py:27
  54.6 0.0 collective-permute-start.4
  54.6 3.9 %collective-permute-done.4 = f32[32,256]{1,0:T(8,128)S(1)} collective-permute-done((f32[32,256]{1,0:T(8,128)S(1)}, f32[32,256]{1,0:T(8,128)S(1)}, u32[]{:S(2)}, u32[]{:S(2)}) %collective-permute-start.4) | collective-permute-done | bytes 32800 | tf_op jit(solution)/shard_map/ppermute | solution.py:27
  58.5 0.0 collective-permute-start.5
  58.5 4.8 %collective-permute-done.5 = f32[32,256]{1,0:T(8,128)S(1)} collective-permute-done((f32[32,256]{1,0:T(8,128)S(1)}, f32[32,256]{1,0:T(8,128)S(1)}, u32[]{:S(2)}, u32[]{:S(2)}) %collective-permute-start.5) | collective-permute-done | bytes 32800 | tf_op jit(solution)/shard_map/ppermute | solution.py:27
  63.3 0.6 add.98
  (16 shorter events, 0.3 us)
Async XLA Ops:
  0.6 4.6 %copy-start = (bf16[8,128,128]{2,1,0:T(8,128)(2,1)S(1)}, bf16[8,128,128]{2,1,0:T(8,128)(2,1)}, u32[]{:S(2)}) copy-start(bf16[8,128,128]{2,1,0:T(8,128)(2,1)} %param.9) | copy-start | bytes 786436
  8.3 33.0 %all-to-all-start = ((bf16[8,11,4096]{2,1,0:T(8,128)(2,1)}), bf16[8,11,4096]{2,1,0:T(8,128)(2,1)S(1)}, u32[]{:S(2)}, u32[]{:S(2)}) async-start(bf16[8,11,4096]{2,1,0:T(8,128)(2,1)} %fusion.3), calls=%async_computation | async-start | bytes 2097152 | tf_op jit(solution)/shard_map/all_to_all | solution.py:64
  42.8 5.8 %copy-start.2 = (bf16[128,256]{1,0:T(8,128)(2,1)S(1)}, bf16[128,256]{1,0:T(8,128)(2,1)}, u32[]{:S(2)}) copy-start(bf16[128,256]{1,0:T(8,128)(2,1)} %param.12) | copy-start | bytes 196612
  43.0 3.8 %collective-permute-start = (bf16[32,1024]{1,0:T(8,128)(2,1)S(1)}, bf16[32,1024]{1,0:T(8,128)(2,1)S(1)}, u32[]{:S(2)}, u32[]{:S(2)}) collective-permute-start(bf16[32,1024]{1,0:T(8,128)(2,1)S(1)} %bitcast.76), channel_id=1, source_target_pairs={{0,1},{1,2},{2,3},{3,0},{4,5},{5,6},{6,7},{7,4},{8,9},{9,10},{10,1... | collective-permute-start | bytes 196616 | tf_op jit(solution)/shard_map/ppermute | solution.py:14
  43.1 4.6 %collective-permute-start.1 = (bf16[32,1024]{1,0:T(8,128)(2,1)S(1)}, bf16[32,1024]{1,0:T(8,128)(2,1)S(1)}, u32[]{:S(2)}, u32[]{:S(2)}) collective-permute-start(bf16[32,1024]{1,0:T(8,128)(2,1)S(1)} %bitcast.77), channel_id=1, source_target_pairs={{0,2},{1,3},{2,0},{3,1},{4,6},{5,7},{6,4},{7,5},{8,10},{9,11},{10,... | collective-permute-start | bytes 196616 | tf_op jit(solution)/shard_map/ppermute | solution.py:14
  44.6 3.3 %collective-permute-start.2 = (bf16[32,1024]{1,0:T(8,128)(2,1)S(1)}, bf16[32,1024]{1,0:T(8,128)(2,1)S(1)}, u32[]{:S(2)}, u32[]{:S(2)}) collective-permute-start(bf16[32,1024]{1,0:T(8,128)(2,1)S(1)} %bitcast.78), channel_id=1, source_target_pairs={{0,3},{1,0},{2,1},{3,2},{4,7},{5,4},{6,5},{7,6},{8,11},{9,8},{10,9... | collective-permute-start | bytes 196616 | tf_op jit(solution)/shard_map/ppermute | solution.py:14
  48.6 1.3 %copy-start.1 = (bf16[1024,256]{1,0:T(8,128)(2,1)S(1)}, bf16[1024,256]{1,0:T(8,128)(2,1)}, u32[]{:S(2)}) copy-start(bf16[1024,256]{1,0:T(8,128)(2,1)} %param.13) | copy-start | bytes 1572868
  50.4 4.1 %collective-permute-start.3 = (f32[32,256]{1,0:T(8,128)S(1)}, f32[32,256]{1,0:T(8,128)S(1)}, u32[]{:S(2)}, u32[]{:S(2)}) collective-permute-start(f32[32,256]{1,0:T(8,128)S(1)} %fusion.4), channel_id=1, source_target_pairs={{0,4},{4,0},{8,12},{12,8},{16,20},{20,16},{24,28},{28,24},{1,5},{5... | collective-permute-start | bytes 98312 | tf_op jit(solution)/shard_map/ppermute | solution.py:27
  54.6 3.9 %collective-permute-start.4 = (f32[32,256]{1,0:T(8,128)S(1)}, f32[32,256]{1,0:T(8,128)S(1)}, u32[]{:S(2)}, u32[]{:S(2)}) collective-permute-start(f32[32,256]{1,0:T(8,128)S(1)} %add.96), channel_id=1, source_target_pairs={{0,8},{4,12},{8,0},{12,4},{16,24},{20,28},{24,16},{28,20},{1,9},{5... | collective-permute-start | bytes 98312 | tf_op jit(solution)/shard_map/ppermute | solution.py:27
  58.5 4.8 %collective-permute-start.5 = (f32[32,256]{1,0:T(8,128)S(1)}, f32[32,256]{1,0:T(8,128)S(1)}, u32[]{:S(2)}, u32[]{:S(2)}) collective-permute-start(f32[32,256]{1,0:T(8,128)S(1)} %add.97), channel_id=1, source_target_pairs={{0,16},{4,20},{8,24},{12,28},{16,0},{20,4},{24,8},{28,12},{1,17},{... | collective-permute-start | bytes 98312 | tf_op jit(solution)/shard_map/ppermute | solution.py:27

commit v3 on v1

--- a/solution.py
+++ b/solution.py
@@ -19,14 +19,12 @@
 
 
 def sum_over_row(x, n_row):
-    if n_row & (n_row - 1):
-        return lax.psum(x, "row")
-    k = 1
-    while k < n_row:
-        perm = [(i, i ^ k) for i in range(n_row)]
-        x = x + lax.ppermute(x, "row", perm)
-        k *= 2
-    return x
+    every = jnp.broadcast_to(x[None], (n_row,) + x.shape)
+    parts = lax.all_to_all(every, "row", split_axis=0, concat_axis=0, tiled=True)
+    total = parts[0]
+    for i in range(1, n_row):
+        total = total + parts[i]
+    return total
 
 
 def body(x_t, tiles, tile_owner, tile_local, weight, cotangent):

time: 56.1 us -> 54.4 us (0.970)
  blocking collectives: 0 us -> 11.1 us
  waiting for transfers between devices: 25.2 us -> 14.5 us
  starting transfers between devices: 14.8 us -> 12.6 us
    all_to_all x0 -> x1, blocking collectives: none -> 11.1 us  [sum_over_row(): lax.all_to_all(every, 'row', split_axis=0, concat_axis=0, tiled=True)]
    ppermute x3 -> x0, waiting for transfers between devices: 10.7 us -> none  [sum_over_row(): x = x + lax.ppermute(x, 'row', perm)]
    ppermute x3 -> x0, starting transfers between devices: 2.18 us -> none  [sum_over_row(): x = x + lax.ppermute(x, 'row', perm)]
  transfers between devices with their start and end apart: 8 -> 5, of which waited for: 8 -> 5; matrix products, arithmetic and copies ran while one was open for 7% -> 7% of each run, Pallas kernels for 0% -> 0%
where the time goes in v3:
time: 54.4 us; the launch traced here: 53.9 us
  waiting for transfers between devices  14.5 us (27%)
  starting transfers between devices  12.6 us (23%)
  blocking collectives  11.1 us (20%)
  local copies, waits for them, and re-layouts  8.4 us (15%)
  other arithmetic  3.71 us (7%)
  matrix products  2.71 us (5%)
  between operations  0.86 us (2%)
    all_to_all x1, blocking collectives, sum_over_row(): lax.all_to_all(every, 'row', split_axis=0, concat_axis=0, tiled=True)  11.1 us
    all_to_all x1, starting transfers between devices, body(): lax.all_to_all(requests, 'row', split_axis=0, concat_axis=0, tiled=True)  7.41 us
    all_to_all x1, waiting for transfers between devices, body(): lax.all_to_all(jnp.concatenate([picked, outgoing], axis=1), 'row', split_...  6.69 us
    ppermute x3, waiting for transfers between devices, gather_groups(): parts.append(lax.ppermute(z_part, 'col', perm))  4.06 us
    all_to_all x1, waiting for transfers between devices, body(): lax.all_to_all(requests, 'row', split_axis=0, concat_axis=0, tiled=True)  3.77 us
    all_to_all x1, starting transfers between devices, body(): lax.all_to_all(jnp.concatenate([picked, outgoing], axis=1), 'row', split_...  3.41 us
    unnamed x13, local copies, waits for them, and re-layouts  2.31 us
    ppermute x3, starting transfers between devices, gather_groups(): parts.append(lax.ppermute(z_part, 'col', perm))  1.78 us
  transfers between devices with their start and end apart: 5, of which 5 were waited for; matrix products, arithmetic and copies ran while one was open for 7% of the time, Pallas kernels for 0%

profile of v3, /device:TPU:0, one launch (start us, length us, event | category | flops | bytes accessed | tf_op | source)
XLA Modules:
  0.0 53.9 jit_solution(15104546649343344516)
XLA Ops:
  0.6 0.8 %slice_bitcast_fusion.1 = (s32[8]{0:T(128)S(1)}, s32[8]{0:T(128)S(1)}, s32[8]{0:T(128)S(1)}) fusion(s32[8,2]{0,1:T(2,128)} %param.9), kind=kLoop, calls=%fused_computation.79 | loop fusion | flops 24 | bytes 160 | tf_op jit(solution)/shard_map/eq | solution.py:70
  1.4 0.7 %copy-done.1 = s32[8,1]{0,1:T(1,128)S(1)} copy-done((s32[8,1]{0,1:T(1,128)S(1)}, s32[8,1]{0,1:T(1,128)}, u32[]{:S(2)}) %copy-start.1) | copy-done | bytes 56
  2.1 0.1 fusion.19
  2.2 0.2 select_reduce_fusion
  2.4 0.6 %scatter_custom_fusion = s32[16]{0:T(128)S(1)} fusion(s32[8]{0:T(128)S(1)} %bitcast.89, s32[8]{0:T(128)S(1)} %get-tuple-element.10, s32[]{:T(128)} %constant.81.clone.1), kind=kCustom, calls=%fused_computation.80 | custom fusion | bytes 68 | tf_op jit(solution)/shard_map/scatter | solution.py:46
  3.0 0.7 %all_to_all.16 = s32[8,1,2]{2,0,1:T(8,128)} reshape(s32[16]{0:T(128)S(1)} %scatter_custom_fusion) | data formatting | bytes 128 | tf_op jit(solution)/shard_map/all_to_all | solution.py:58
  3.6 7.4 %all-to-all-start = ((s32[8,1,2]{2,1,0:T(1,128)}), s32[8,1,2]{2,1,0:T(1,128)S(1)}, u32[]{:S(2)}, u32[]{:S(2)}) async-start(s32[8,1,2]{2,1,0:T(1,128)} %bitcast.7), calls=%async_computation | async-start | bytes 8192 | tf_op jit(solution)/shard_map/all_to_all | solution.py:58
  11.1 0.9 %bitcast_bitcast_fusion = (bf16[1,8,32,128]{3,2,1,0:T(8,128)(2,1)S(1)}, bf16[8,32,128]{2,1,0:T(8,128)(2,1)S(1)}) fusion(bf16[32,1024]{1,0:T(8,128)(2,1)} %param.6), kind=kLoop, calls=%fused_computation.27 | loop fusion | bytes 196608
  12.0 0.6 %gather_fusion.1 = bf16[8,32,128]{2,1,0:T(8,128)(2,1)S(1)} fusion(bf16[8,32,128]{2,1,0:T(8,128)(2,1)S(1)} %get-tuple-element.7, s32[1024]{0:T(1024)S(1)} %pad_clamp_fusion.2), kind=kCustom, calls=%fused_computation.1 | custom fusion | bytes 131104 | tf_op jit(solution)/shard_map/jit(_take)/gather | solution.py:48
  12.6 0.2 fusion.1
  12.8 0.8 %scatter_custom_fusion.1 = bf16[16,4096]{1,0:T(8,128)(2,1)S(1)} fusion(s32[8]{0:T(128)S(1)} %bitcast.90, bf16[1,8,32,128]{3,2,1,0:T(8,128)(2,1)S(1)} %fusion.1, bf16[]{:T(256)} %constant.91.clone.1), kind=kCustom, calls=%fused_computation.23 | custom fusion | bytes 196610 | tf_op jit(solution)/shard_map/scatter | solution.py:55
  13.6 0.1 reshape.152
  13.7 3.8 %all-to-all-done = s32[8,1,2]{2,1,0:T(1,128)S(1)} async-done(((s32[8,1,2]{2,1,0:T(1,128)}), s32[8,1,2]{2,1,0:T(1,128)S(1)}, u32[]{:S(2)}, u32[]{:S(2)}) %all-to-all-start) | async-done | bytes 96 | tf_op jit(solution)/shard_map/all_to_all | solution.py:58
  17.4 0.1 copy.33
  17.5 0.1 copy.34
  17.6 0.1 copy.37
  17.7 0.1 reshape.160
  17.8 0.6 %gather_fusion = bf16[16,4096]{1,0:T(8,128)(2,1)S(1)} fusion(bf16[8,4096]{1,0:T(8,128)(2,1)S(1)} %bitcast.77, s32[1024]{0:T(1024)S(1)} %pad_clamp_fusion.3), kind=kCustom, calls=%fused_computation | custom fusion | bytes 262208 | tf_op jit(solution)/shard_map/jit(_take)/gather | solution.py:59
  18.4 0.1 reshape.159
  18.5 0.2 broadcast_select_fusion
  18.7 1.0 %pad_maximum_fusion = bf16[8,4,4096]{2,1,0:T(4,128)(2,1)} fusion(bf16[8,2,4096]{2,1,0:T(2,128)(2,1)S(1)} %reshape.152, bf16[8,2,4096]{2,1,0:T(2,128)(2,1)S(1)} %broadcast_select_fusion), kind=kLoop, calls=%fused_computation.14 | loop fusion | flops 524288 | bytes 524288 | tf_op jit(solution)/shard_map/concatenate | solution.py:61
  19.7 3.4 %all-to-all-start.1 = ((bf16[8,4,4096]{2,1,0:T(4,128)(2,1)}), bf16[8,4,4096]{2,1,0:T(4,128)(2,1)S(1)}, u32[]{:S(2)}, u32[]{:S(2)}) async-start(bf16[8,4,4096]{2,1,0:T(4,128)(2,1)} %pad_maximum_fusion), calls=%async_computation.1 | async-start | bytes 524288 | tf_op jit(solution)/shard_map/all_to_all | solution.py:60
  23.2 0.1 broadcast_in_dim.56
  23.2 0.1 broadcast_in_dim.57
  23.3 0.5 broadcast.212
  23.9 0.7 %reduce.3 = s32[8,2]{1,0:T(8,128)S(1)} reduce(s32[8,1,2]{2,1,0:T(1,128)S(1)} %all-to-all-done, s32[]{:T(128)} %broadcast.212), dimensions={1}, to_apply=%all_to_all.17.reduce_sub_computation.3 | reduce | bytes 132 | tf_op jit(solution)/shard_map/all_to_all | solution.py:58
  24.5 0.1 eq.55
  24.6 6.7 %all-to-all-done.1 = bf16[8,4,4096]{2,1,0:T(4,128)(2,1)S(1)} async-done(((bf16[8,4,4096]{2,1,0:T(4,128)(2,1)}), bf16[8,4,4096]{2,1,0:T(4,128)(2,1)S(1)}, u32[]{:S(2)}, u32[]{:S(2)}) %all-to-all-start.1) | async-done | bytes 262176 | tf_op jit(solution)/shard_map/all_to_all | solution.py:60
  31.3 0.2 fusion.35
  31.5 0.1 reshape.154
  31.6 0.1 reshape.153
  31.7 0.6 %gather_fusion.2 = bf16[8,32,128]{2,1,0:T(8,128)(2,1)S(1)} fusion(bf16[16,32,128]{2,1,0:T(8,128)(2,1)S(1)} %reshape.153, s32[1024]{0:T(1024)S(1)} %pad_clamp_fusion.1), kind=kCustom, calls=%fused_computation.2 | custom fusion | bytes 131104 | tf_op jit(solution)/shard_map/jit(_take)/gather | solution.py:65
  32.3 0.3 fusion.10
  32.6 0.3 fusion.5
  32.8 0.1 fusion
  33.0 0.1 collective-permute-start.2
  33.1 1.6 %collective-permute-start.1 = (bf16[32,1024]{1,0:T(8,128)(2,1)S(1)}, bf16[32,1024]{1,0:T(8,128)(2,1)S(1)}, u32[]{:S(2)}, u32[]{:S(2)}) collective-permute-start(bf16[32,1024]{1,0:T(8,128)(2,1)S(1)} %bitcast.82), channel_id=1, source_target_pairs={{0,2},{1,3},{2,0},{3,1},{4,6},{5,7},{6,4},{7,5},{8,10},{9,11},{10,... | collective-permute-start | bytes 196616 | tf_op jit(solution)/shard_map/ppermute | solution.py:14
  34.6 0.2 collective-permute-start
  34.8 0.1 collective-permute-done.2
  35.0 3.7 %collective-permute-done.1 = bf16[32,1024]{1,0:T(8,128)(2,1)S(1)} collective-permute-done((bf16[32,1024]{1,0:T(8,128)(2,1)S(1)}, bf16[32,1024]{1,0:T(8,128)(2,1)S(1)}, u32[]{:S(2)}, u32[]{:S(2)}) %collective-permute-start.1) | collective-permute-done | bytes 65568 | tf_op jit(solution)/shard_map/ppermute | solution.py:14
  38.7 0.2 collective-permute-done
  38.9 0.6 %gather_fusion.3 = bf16[4,32,1024]{2,1,0:T(8,128)(2,1)S(1)} fusion(bf16[4,32,1024]{2,1,0:T(8,128)(2,1)S(1)} %pad_maximum_fusion.1, s32[1024]{0:T(1024)S(1)} %pad_clamp_fusion), kind=kCustom, calls=%fused_computation.3 | custom fusion | bytes 524304 | tf_op jit(solution)/shard_map/jit(_take)/gather | solution.py:17
  39.5 0.1 bitcast_select_fusion
  39.6 0.7 %copy-done.4 = bf16[128,256]{1,0:T(8,128)(2,1)S(1)} copy-done((bf16[128,256]{1,0:T(8,128)(2,1)S(1)}, bf16[128,256]{1,0:T(8,128)(2,1)}, u32[]{:S(2)}) %copy-start.4) | copy-done | bytes 65560
  40.4 1.3 %multiply_convert_fusion.1 = (bf16[1024,256]{1,0:T(8,128)(2,1)}, f32[1024,256]{1,0:T(8,128)S(1)}) fusion(bf16[128,1024]{1,0:T(8,128)(2,1)S(1)} %bitcast_select_fusion, bf16[128,256]{1,0:T(8,128)(2,1)S(1)} %copy-done.4), kind=kOutput, calls=%fused_computation.11 | convolution fusion | flops 68419584 | bytes 1900544 | tf_op jit(solution)/shard_map/dot_general | solution.py:82
  41.6 0.5 fusion.2
  42.2 11.1 %all_to_all.25 = f32[8,32,256]{2,1,0:T(8,128)S(1)} all-to-all(f32[8,32,256]{2,1,0:T(8,128)S(1)} %broadcast_in_dim.66), channel_id=1, replica_groups=mesh['row'=8,'col'=4] {'row'}, dimensions={0} | all-to-all | bytes 524288 | tf_op jit(solution)/shard_map/all_to_all | solution.py:23
  53.3 0.6 %fusion.16 = f32[32,256]{1,0:T(8,128)} fusion(f32[8,32,256]{2,1,0:T(8,128)S(1)} %all_to_all.25), kind=kLoop, calls=%fused_computation.36 | loop fusion | flops 57344 | bytes 294912 | tf_op jit(solution)/shard_map/add | solution.py:26
  (24 shorter events, 0.3 us)
Async XLA Ops:
  0.6 11.9 %copy-start = (bf16[8,128,128]{2,1,0:T(8,128)(2,1)S(1)}, bf16[8,128,128]{2,1,0:T(8,128)(2,1)}, u32[]{:S(2)}) copy-start(bf16[8,128,128]{2,1,0:T(8,128)(2,1)} %param.7) | copy-start | bytes 786436
  1.4 0.7 %copy-start.1 = (s32[8,1]{0,1:T(1,128)S(1)}, s32[8,1]{0,1:T(1,128)}, u32[]{:S(2)}) copy-start(s32[8,1]{0,1:T(1,128)} %param.8) | copy-start | bytes 100
  3.6 7.4 %copy-start.2 = (s32[8,2]{0,1:T(2,128)S(1)}, s32[8,2]{0,1:T(2,128)}, u32[]{:S(2)}) copy-start(s32[8,2]{0,1:T(2,128)} %param.9) | copy-start | bytes 196
  3.6 13.8 %all-to-all-start = ((s32[8,1,2]{2,1,0:T(1,128)}), s32[8,1,2]{2,1,0:T(1,128)S(1)}, u32[]{:S(2)}, u32[]{:S(2)}) async-start(s32[8,1,2]{2,1,0:T(1,128)} %bitcast.7), calls=%async_computation | async-start | bytes 8192 | tf_op jit(solution)/shard_map/all_to_all | solution.py:58
  19.7 11.6 %all-to-all-start.1 = ((bf16[8,4,4096]{2,1,0:T(4,128)(2,1)}), bf16[8,4,4096]{2,1,0:T(4,128)(2,1)S(1)}, u32[]{:S(2)}, u32[]{:S(2)}) async-start(bf16[8,4,4096]{2,1,0:T(4,128)(2,1)} %pad_maximum_fusion), calls=%async_computation.1 | async-start | bytes 524288 | tf_op jit(solution)/shard_map/all_to_all | solution.py:60
  33.0 2.0 %collective-permute-start.2 = (bf16[32,1024]{1,0:T(8,128)(2,1)S(1)}, bf16[32,1024]{1,0:T(8,128)(2,1)S(1)}, u32[]{:S(2)}, u32[]{:S(2)}) collective-permute-start(bf16[32,1024]{1,0:T(8,128)(2,1)S(1)} %bitcast.81), channel_id=1, source_target_pairs={{0,3},{1,0},{2,1},{3,2},{4,7},{5,4},{6,5},{7,6},{8,11},{9,8},{10,9... | collective-permute-start | bytes 196616 | tf_op jit(solution)/shard_map/ppermute | solution.py:14
  33.1 5.6 %collective-permute-start.1 = (bf16[32,1024]{1,0:T(8,128)(2,1)S(1)}, bf16[32,1024]{1,0:T(8,128)(2,1)S(1)}, u32[]{:S(2)}, u32[]{:S(2)}) collective-permute-start(bf16[32,1024]{1,0:T(8,128)(2,1)S(1)} %bitcast.82), channel_id=1, source_target_pairs={{0,2},{1,3},{2,0},{3,1},{4,6},{5,7},{6,4},{7,5},{8,10},{9,11},{10,... | collective-permute-start | bytes 196616 | tf_op jit(solution)/shard_map/ppermute | solution.py:14
  34.6 4.3 %collective-permute-start = (bf16[32,1024]{1,0:T(8,128)(2,1)S(1)}, bf16[32,1024]{1,0:T(8,128)(2,1)S(1)}, u32[]{:S(2)}, u32[]{:S(2)}) collective-permute-start(bf16[32,1024]{1,0:T(8,128)(2,1)S(1)} %bitcast.83), channel_id=1, source_target_pairs={{0,1},{1,2},{2,3},{3,0},{4,5},{5,6},{6,7},{7,4},{8,9},{9,10},{10,1... | collective-permute-start | bytes 196616 | tf_op jit(solution)/shard_map/ppermute | solution.py:14
  39.5 0.8 %copy-start.4 = (bf16[128,256]{1,0:T(8,128)(2,1)S(1)}, bf16[128,256]{1,0:T(8,128)(2,1)}, u32[]{:S(2)}) copy-start(bf16[128,256]{1,0:T(8,128)(2,1)} %param.10) | copy-start | bytes 196612
  40.4 1.3 %copy-start.3 = (bf16[1024,256]{1,0:T(8,128)(2,1)S(1)}, bf16[1024,256]{1,0:T(8,128)(2,1)}, u32[]{:S(2)}) copy-start(bf16[1024,256]{1,0:T(8,128)(2,1)} %param.11) | copy-start | bytes 1572868

commit v4 on v3

--- a/solution.py
+++ b/solution.py
@@ -2,6 +2,10 @@
 import jax.numpy as jnp
 from jax import lax
 from jax.sharding import PartitionSpec as P
+
+
+def rows_of(a, idx):
+    return a.at[idx].get(mode="promise_in_bounds")
 
 
 def gather_groups(z_part, n_col):
@@ -14,7 +18,7 @@
         parts.append(lax.ppermute(z_part, "col", perm))
     stacked = jnp.stack(parts)
     order = (me - jnp.arange(n_col, dtype=jnp.int32)) % n_col
-    full = jnp.take(stacked, order, axis=0)
+    full = rows_of(stacked, order)
     return full.reshape(n_col * z_part.shape[0], z_part.shape[1])
 
 
@@ -39,30 +43,32 @@
     owner = tile_owner[:, 0]
     row_local = tile_local[:, 0]
     col_local = tile_local[:, 1]
-    owner_hot = (owner[:, None] == jnp.arange(n_row, dtype=jnp.int32)[None, :]).astype(jnp.int32)
-    rank = jnp.sum(owner_hot * (jnp.cumsum(owner_hot, axis=0) - 1), axis=1)
+    tile_ids = jnp.arange(n_tiles, dtype=jnp.int32)
+    same = owner[:, None] == owner[None, :]
+    rank = jnp.sum((same & (tile_ids[None, :] < tile_ids[:, None])).astype(jnp.int32), axis=1)
     slot = owner * capacity + rank
-    requests = (
-        jnp.zeros((n_row * capacity,), jnp.int32).at[slot].set(col_local).reshape(n_row, capacity)
-    )
-    own_blocks = jnp.take(xb, row_local, axis=0)
+    slot_range = jnp.arange(n_row * capacity, dtype=jnp.int32)
+    slot_hot = slot[None, :] == slot_range[:, None]
+    requests = jnp.sum(jnp.where(slot_hot, col_local[None, :], 0), axis=1)
+    requests = jnp.broadcast_to(requests.reshape(n_row, capacity, 1), (n_row, capacity, 128))
+    own_blocks = rows_of(xb, row_local)
     mirror_terms = jnp.einsum(
         "tfi,tij->tfj", own_blocks, tiles, preferred_element_type=jnp.float32
     ).astype(jnp.bfloat16)
     outgoing = jnp.zeros((n_row * capacity, feat_q * tile_dim), jnp.bfloat16)
-    outgoing = (
-        outgoing.at[slot]
-        .set(mirror_terms.reshape(n_tiles, feat_q * tile_dim))
-        .reshape(n_row, capacity, feat_q * tile_dim)
+    outgoing = outgoing.at[slot].set(
+        mirror_terms.reshape(n_tiles, feat_q * tile_dim), mode="promise_in_bounds", unique_indices=True
     )
-    block_ids = lax.all_to_all(requests, "row", split_axis=0, concat_axis=0, tiled=True)
-    picked = jnp.take(flat_blocks, block_ids, axis=0)
-    both = lax.all_to_all(
-        jnp.concatenate([picked, outgoing], axis=1), "row", split_axis=0, concat_axis=0, tiled=True
-    )
+    source = jnp.concatenate([flat_blocks, outgoing], axis=0)
+    got_ids = lax.all_to_all(requests, "row", split_axis=0, concat_axis=0, tiled=True)
+    block_ids = got_ids[:, :, 0]
+    mirror_rows = n_blocks + slot_range.reshape(n_row, capacity)
+    pick = jnp.concatenate([block_ids, mirror_rows], axis=1)
+    payload = rows_of(source, pick.reshape(-1)).reshape(n_row, 2 * capacity, feat_q * tile_dim)
+    both = lax.all_to_all(payload, "row", split_axis=0, concat_axis=0, tiled=True)
     fetched = both[:, :capacity]
     incoming = both[:, capacity:]
-    fetched_tiles = jnp.take(fetched.reshape(n_row * capacity, feat_q, tile_dim), slot, axis=0)
+    fetched_tiles = rows_of(fetched.reshape(n_row * capacity, feat_q, tile_dim), slot)
     forward_terms = jnp.einsum(
         "tfj,tij->tfi", fetched_tiles, tiles, preferred_element_type=jnp.float32
     )

time: 54.4 us -> 52.9 us (0.972)
  other arithmetic: 3.71 us -> 1.03 us
  waiting for transfers between devices: 14.5 us -> 16.2 us
    all_to_all x1, waiting for transfers between devices: 6.69 us -> 8.05 us  [body(): lax.all_to_all(payload, 'row', split_axis=0, concat_axis=0, tiled=True)]
    all_to_all x3 -> x0, local copies, waits for them, and re-layouts: 1.27 us -> none  [body(): lax.all_to_all(requests, 'row', split_axis=0, concat_axis=0, tiled=True)]
    concatenate x1 -> x2, other arithmetic: 0.98 us -> 0.03 us  [the longest x1 0.02 us: body(): source = jnp.concatenate([flat_blocks, outgoing], axis=0)]
    reshape x1 -> x2, local copies, waits for them, and re-layouts: 0.1 us -> 0.89 us  [the longest x1 0.81 us: body(): rows_of(source, pick.reshape(-1))]
    eq x1, other arithmetic: 0.76 us -> 0.01 us  [body(): row_hot = (row_local[:, None] == block_range[None, :]).astype(jnp.float32)]
    all_to_all x1 -> x0, other arithmetic: 0.66 us -> none  [body(): lax.all_to_all(requests, 'row', split_axis=0, concat_axis=0, tiled=True)]
    broadcast_in_dim x2, local copies, waits for them, and re-layouts: 0.16 us -> 0.76 us  [body(): jnp.broadcast_to(requests.reshape(n_row, capacity, 1), (n_row, capacity,...]
    scatter x2 -> x1, local copies, waits for them, and re-layouts: 1.35 us -> 0.76 us  [body(): outgoing.at[slot]]
  transfers between devices with their start and end apart: 5 -> 5, of which waited for: 5 -> 5; matrix products, arithmetic and copies ran while one was open for 7% -> 5% of each run, Pallas kernels for 0% -> 0%
where the time goes in v4:
time: 52.9 us; the launch traced here: 52.5 us
  waiting for transfers between devices  16.2 us (31%)
  starting transfers between devices  12.5 us (24%)
  blocking collectives  11.1 us (21%)
  local copies, waits for them, and re-layouts  8.26 us (16%)
  matrix products  2.62 us (5%)
  other arithmetic  1.03 us (2%)
  between operations  0.85 us (2%)
    all_to_all x1, blocking collectives, sum_over_row(): lax.all_to_all(every, 'row', split_axis=0, concat_axis=0, tiled=True)  11.1 us
    all_to_all x1, waiting for transfers between devices, body(): lax.all_to_all(payload, 'row', split_axis=0, concat_axis=0, tiled=True)  8.05 us
    all_to_all x1, starting transfers between devices, body(): lax.all_to_all(requests, 'row', split_axis=0, concat_axis=0, tiled=True)  7.28 us
    ppermute x3, waiting for transfers between devices, gather_groups(): parts.append(lax.ppermute(z_part, 'col', perm))  4.06 us
    all_to_all x1, waiting for transfers between devices, body(): lax.all_to_all(requests, 'row', split_axis=0, concat_axis=0, tiled=True)  4.04 us
    all_to_all x1, starting transfers between devices, body(): lax.all_to_all(payload, 'row', split_axis=0, concat_axis=0, tiled=True)  3.41 us
    unnamed x13, local copies, waits for them, and re-layouts  2.54 us
    gather x4, local copies, waits for them, and re-layouts, rows_of(): return a.at[idx].get(mode='promise_in_bounds')  2.4 us
  transfers between devices with their start and end apart: 5, of which 5 were waited for; matrix products, arithmetic and copies ran while one was open for 5% of the time, Pallas kernels for 0%

profile of v4, /device:TPU:0, one launch (start us, length us, event | category | flops | bytes accessed | tf_op | source)
XLA Modules:
  0.0 52.5 jit_solution(17037056306520796461)
XLA Ops:
  0.6 0.0 copy-start
  0.6 0.0 copy-start.4
  0.7 0.7 %copy-done.4 = s32[8,1]{0,1:T(1,128)S(1)} copy-done((s32[8,1]{0,1:T(1,128)S(1)}, s32[8,1]{0,1:T(1,128)}, u32[]{:S(2)}) %copy-start.4) | copy-done | bytes 56
  1.3 0.2 convert_reduce_fusion
  1.5 0.0 copy-start.1
  1.5 0.7 %copy-done.1 = s32[8,2]{0,1:T(2,128)S(1)} copy-done((s32[8,2]{0,1:T(2,128)S(1)}, s32[8,2]{0,1:T(2,128)}, u32[]{:S(2)}) %copy-start.1) | copy-done | bytes 88
  2.2 0.1 select_reduce_fusion
  2.3 0.1 broadcast_in_dim.26
  2.4 0.7 %broadcast_in_dim.46 = s32[8,2,128]{2,1,0:T(2,128)} broadcast(s32[8,2]{1,0:T(8,128)S(1)} %broadcast_in_dim.26), dimensions={0,1} | broadcast | bytes 8256 | tf_op jit(solution)/shard_map/broadcast_in_dim | solution.py:53
  3.1 7.3 %all-to-all-start = ((s32[8,2,128]{2,1,0:T(2,128)}), s32[8,2,128]{2,1,0:T(2,128)S(1)}, u32[]{:S(2)}, u32[]{:S(2)}) async-start(s32[8,2,128]{2,1,0:T(2,128)} %broadcast_in_dim.46), calls=%async_computation | async-start | bytes 16384 | tf_op jit(solution)/shard_map/all_to_all | solution.py:63
  10.4 0.9 %bitcast_bitcast_fusion = (bf16[1,8,32,128]{3,2,1,0:T(8,128)(2,1)S(1)}, bf16[8,32,128]{2,1,0:T(8,128)(2,1)S(1)}) fusion(bf16[32,1024]{1,0:T(8,128)(2,1)} %param.6), kind=kLoop, calls=%fused_computation.24 | loop fusion | bytes 196608
  11.3 0.6 %gather_fusion = bf16[8,32,128]{2,1,0:T(8,128)(2,1)S(1)} fusion(bf16[8,32,128]{2,1,0:T(8,128)(2,1)S(1)} %get-tuple-element.5, s32[1024]{0:T(1024)S(1)} %pad_clamp_fusion.3), kind=kCustom, calls=%fused_computation | custom fusion | bytes 131104 | tf_op jit(solution)/shard_map/gather | solution.py:8
  11.8 0.0 copy-done
  11.8 0.2 fusion.1
  12.0 0.8 %scatter_custom_fusion = bf16[16,4096]{1,0:T(8,128)(2,1)S(1)} fusion(s32[8]{0:T(128)S(1)} %fusion.20, bf16[1,8,32,128]{3,2,1,0:T(8,128)(2,1)S(1)} %fusion.1, bf16[]{:T(256)} %constant.11.clone.1), kind=kCustom, calls=%fused_computation.20 | custom fusion | bytes 196610 | tf_op jit(solution)/shard_map/scatter | solution.py:59
  12.8 4.0 %all-to-all-done = s32[8,2,128]{2,1,0:T(2,128)S(1)} async-done(((s32[8,2,128]{2,1,0:T(2,128)}), s32[8,2,128]{2,1,0:T(2,128)S(1)}, u32[]{:S(2)}, u32[]{:S(2)}) %all-to-all-start) | async-done | bytes 8224 | tf_op jit(solution)/shard_map/all_to_all | solution.py:63
  16.9 0.2 slice_reduce_fusion
  17.1 0.1 copy.24
  17.2 0.1 copy.25
  17.3 0.1 reshape.152
  17.4 0.7 %gather_fusion.1 = bf16[32,4096]{1,0:T(8,128)(2,1)S(1)} fusion(bf16[24,4096]{1,0:T(8,128)(2,1)S(1)} %pad_maximum_fusion.1, s32[1024]{0:T(1024)S(1)} %pad_clamp_fusion.2), kind=kCustom, calls=%fused_computation.1 | custom fusion | bytes 524416 | tf_op jit(solution)/shard_map/gather | solution.py:8
  18.1 0.8 %reshape.153 = bf16[8,4,4096]{2,1,0:T(4,128)(2,1)} reshape(bf16[32,4096]{1,0:T(8,128)(2,1)S(1)} %gather_fusion.1) | data formatting | bytes 524288 | tf_op jit(solution)/shard_map/reshape | solution.py:67
  18.9 3.4 %all-to-all-start.1 = ((bf16[8,4,4096]{2,1,0:T(4,128)(2,1)}), bf16[8,4,4096]{2,1,0:T(4,128)(2,1)S(1)}, u32[]{:S(2)}, u32[]{:S(2)}) async-start(bf16[8,4,4096]{2,1,0:T(4,128)(2,1)} %reshape.153), calls=%async_computation.1 | async-start | bytes 524288 | tf_op jit(solution)/shard_map/all_to_all | solution.py:68
  22.3 0.1 eq.74
  22.4 8.0 %all-to-all-done.1 = bf16[8,4,4096]{2,1,0:T(4,128)(2,1)S(1)} async-done(((bf16[8,4,4096]{2,1,0:T(4,128)(2,1)}), bf16[8,4,4096]{2,1,0:T(4,128)(2,1)S(1)}, u32[]{:S(2)}, u32[]{:S(2)}) %all-to-all-start.1) | async-done | bytes 262176 | tf_op jit(solution)/shard_map/all_to_all | solution.py:68
  30.5 0.2 fusion.25
  30.7 0.1 reshape.155
  30.8 0.1 reshape.154
  30.9 0.6 %gather_fusion.2 = bf16[8,32,128]{2,1,0:T(8,128)(2,1)S(1)} fusion(bf16[16,32,128]{2,1,0:T(8,128)(2,1)S(1)} %reshape.154, s32[1024]{0:T(1024)S(1)} %pad_clamp_fusion.1), kind=kCustom, calls=%fused_computation.2 | custom fusion | bytes 131104 | tf_op jit(solution)/shard_map/gather | solution.py:8
  31.4 0.2 fusion.26
  31.7 0.3 fusion.5
  32.0 0.1 fusion
  32.1 0.1 collective-permute-start.2
  32.2 1.6 %collective-permute-start.1 = (bf16[32,1024]{1,0:T(8,128)(2,1)S(1)}, bf16[32,1024]{1,0:T(8,128)(2,1)S(1)}, u32[]{:S(2)}, u32[]{:S(2)}) collective-permute-start(bf16[32,1024]{1,0:T(8,128)(2,1)S(1)} %bitcast.76), channel_id=1, source_target_pairs={{0,2},{1,3},{2,0},{3,1},{4,6},{5,7},{6,4},{7,5},{8,10},{9,11},{10,... | collective-permute-start | bytes 196616 | tf_op jit(solution)/shard_map/ppermute | solution.py:18
  33.8 0.2 collective-permute-start
  34.0 0.1 collective-permute-done.2
  34.1 3.7 %collective-permute-done.1 = bf16[32,1024]{1,0:T(8,128)(2,1)S(1)} collective-permute-done((bf16[32,1024]{1,0:T(8,128)(2,1)S(1)}, bf16[32,1024]{1,0:T(8,128)(2,1)S(1)}, u32[]{:S(2)}, u32[]{:S(2)}) %collective-permute-start.1) | collective-permute-done | bytes 65568 | tf_op jit(solution)/shard_map/ppermute | solution.py:18
  37.8 0.2 collective-permute-done
  38.1 0.0 copy-start.3
  38.1 0.6 %gather_fusion.3 = bf16[4,32,1024]{2,1,0:T(8,128)(2,1)S(1)} fusion(bf16[4,32,1024]{2,1,0:T(8,128)(2,1)S(1)} %pad_maximum_fusion, s32[1024]{0:T(1024)S(1)} %pad_clamp_fusion), kind=kCustom, calls=%fused_computation.3 | custom fusion | bytes 524304 | tf_op jit(solution)/shard_map/gather | solution.py:8
  38.6 0.3 copy-done.3
  38.9 0.0 copy-start.2
  38.9 1.3 %multiply_convert_fusion.1 = (bf16[1024,256]{1,0:T(8,128)(2,1)}, f32[1024,256]{1,0:T(8,128)S(1)}) fusion(bf16[128,1024]{1,0:T(8,128)(2,1)S(1)} %bitcast.73, bf16[128,256]{1,0:T(8,128)(2,1)S(1)} %copy-done.3), kind=kOutput, calls=%fused_computation.10 | convolution fusion | flops 68419584 | bytes 1900544 | tf_op jit(solution)/shard_map/dot_general | solution.py:88
  40.2 0.0 copy-done.2
  40.2 0.5 fusion.2
  40.7 11.1 %all_to_all.15 = f32[8,32,256]{2,1,0:T(8,128)S(1)} all-to-all(f32[8,32,256]{2,1,0:T(8,128)S(1)} %broadcast_in_dim.47), channel_id=1, replica_groups=mesh['row'=8,'col'=4] {'row'}, dimensions={0} | all-to-all | bytes 524288 | tf_op jit(solution)/shard_map/all_to_all | solution.py:27
  51.9 0.6 %fusion.11 = f32[32,256]{1,0:T(8,128)} fusion(f32[8,32,256]{2,1,0:T(8,128)S(1)} %all_to_all.15), kind=kLoop, calls=%fused_computation.28 | loop fusion | flops 57344 | bytes 294912 | tf_op jit(solution)/shard_map/add | solution.py:30
  (17 shorter events, 0.2 us)
Async XLA Ops:
  0.6 11.2 %copy-start = (bf16[8,128,128]{2,1,0:T(8,128)(2,1)S(1)}, bf16[8,128,128]{2,1,0:T(8,128)(2,1)}, u32[]{:S(2)}) copy-start(bf16[8,128,128]{2,1,0:T(8,128)(2,1)} %param.7) | copy-start | bytes 786436
  0.6 0.7 %copy-start.4 = (s32[8,1]{0,1:T(1,128)S(1)}, s32[8,1]{0,1:T(1,128)}, u32[]{:S(2)}) copy-start(s32[8,1]{0,1:T(1,128)} %param.8) | copy-start | bytes 100
  1.5 0.7 %copy-start.1 = (s32[8,2]{0,1:T(2,128)S(1)}, s32[8,2]{0,1:T(2,128)}, u32[]{:S(2)}) copy-start(s32[8,2]{0,1:T(2,128)} %param.9) | copy-start | bytes 196
  3.1 13.8 %all-to-all-start = ((s32[8,2,128]{2,1,0:T(2,128)}), s32[8,2,128]{2,1,0:T(2,128)S(1)}, u32[]{:S(2)}, u32[]{:S(2)}) async-start(s32[8,2,128]{2,1,0:T(2,128)} %broadcast_in_dim.46), calls=%async_computation | async-start | bytes 16384 | tf_op jit(solution)/shard_map/all_to_all | solution.py:63
  18.9 11.6 %all-to-all-start.1 = ((bf16[8,4,4096]{2,1,0:T(4,128)(2,1)}), bf16[8,4,4096]{2,1,0:T(4,128)(2,1)S(1)}, u32[]{:S(2)}, u32[]{:S(2)}) async-start(bf16[8,4,4096]{2,1,0:T(4,128)(2,1)} %reshape.153), calls=%async_computation.1 | async-start | bytes 524288 | tf_op jit(solution)/shard_map/all_to_all | solution.py:68
  32.1 2.0 %collective-permute-start.2 = (bf16[32,1024]{1,0:T(8,128)(2,1)S(1)}, bf16[32,1024]{1,0:T(8,128)(2,1)S(1)}, u32[]{:S(2)}, u32[]{:S(2)}) collective-permute-start(bf16[32,1024]{1,0:T(8,128)(2,1)S(1)} %bitcast.75), channel_id=1, source_target_pairs={{0,3},{1,0},{2,1},{3,2},{4,7},{5,4},{6,5},{7,6},{8,11},{9,8},{10,9... | collective-permute-start | bytes 196616 | tf_op jit(solution)/shard_map/ppermute | solution.py:18
  32.2 5.6 %collective-permute-start.1 = (bf16[32,1024]{1,0:T(8,128)(2,1)S(1)}, bf16[32,1024]{1,0:T(8,128)(2,1)S(1)}, u32[]{:S(2)}, u32[]{:S(2)}) collective-permute-start(bf16[32,1024]{1,0:T(8,128)(2,1)S(1)} %bitcast.76), channel_id=1, source_target_pairs={{0,2},{1,3},{2,0},{3,1},{4,6},{5,7},{6,4},{7,5},{8,10},{9,11},{10,... | collective-permute-start | bytes 196616 | tf_op jit(solution)/shard_map/ppermute | solution.py:18
  33.8 4.3 %collective-permute-start = (bf16[32,1024]{1,0:T(8,128)(2,1)S(1)}, bf16[32,1024]{1,0:T(8,128)(2,1)S(1)}, u32[]{:S(2)}, u32[]{:S(2)}) collective-permute-start(bf16[32,1024]{1,0:T(8,128)(2,1)S(1)} %bitcast.77), channel_id=1, source_target_pairs={{0,1},{1,2},{2,3},{3,0},{4,5},{5,6},{6,7},{7,4},{8,9},{9,10},{10,1... | collective-permute-start | bytes 196616 | tf_op jit(solution)/shard_map/ppermute | solution.py:18
  38.1 0.8 %copy-start.3 = (bf16[128,256]{1,0:T(8,128)(2,1)S(1)}, bf16[128,256]{1,0:T(8,128)(2,1)}, u32[]{:S(2)}) copy-start(bf16[128,256]{1,0:T(8,128)(2,1)} %param.10) | copy-start | bytes 196612
  38.9 1.3 %copy-start.2 = (bf16[1024,256]{1,0:T(8,128)(2,1)S(1)}, bf16[1024,256]{1,0:T(8,128)(2,1)}, u32[]{:S(2)}) copy-start(bf16[1024,256]{1,0:T(8,128)(2,1)} %param.11) | copy-start | bytes 1572868

commit v5 on v4

--- a/solution.py
+++ b/solution.py
@@ -12,14 +12,24 @@
     if n_col == 1:
         return z_part
     me = lax.axis_index("col")
+    if n_col & (n_col - 1):
+        parts = [z_part]
+        for k in range(1, n_col):
+            perm = [(i, (i + k) % n_col) for i in range(n_col)]
+            parts.append(lax.ppermute(z_part, "col", perm))
+        order = (me - jnp.arange(n_col, dtype=jnp.int32)) % n_col
+        full = rows_of(jnp.stack(parts), order)
+        return full.reshape(n_col * z_part.shape[0], z_part.shape[1])
     parts = [z_part]
     for k in range(1, n_col):
-        perm = [(i, (i + k) % n_col) for i in range(n_col)]
-        parts.append(lax.ppermute(z_part, "col", perm))
-    stacked = jnp.stack(parts)
-    order = (me - jnp.arange(n_col, dtype=jnp.int32)) % n_col
-    full = rows_of(stacked, order)
-    return full.reshape(n_col * z_part.shape[0], z_part.shape[1])
+        parts.append(lax.ppermute(z_part, "col", [(i, i ^ k) for i in range(n_col)]))
+    groups = []
+    for j in range(n_col):
+        pick = parts[n_col - 1]
+        for k in range(n_col - 2, -1, -1):
+            pick = jnp.where((me ^ k) == j, parts[k], pick)
+        groups.append(pick)
+    return jnp.concatenate(groups, axis=0)
 
 
 def sum_over_row(x, n_row):
@@ -49,26 +59,27 @@
     slot = owner * capacity + rank
     slot_range = jnp.arange(n_row * capacity, dtype=jnp.int32)
     slot_hot = slot[None, :] == slot_range[:, None]
-    requests = jnp.sum(jnp.where(slot_hot, col_local[None, :], 0), axis=1)
-    requests = jnp.broadcast_to(requests.reshape(n_row, capacity, 1), (n_row, capacity, 128))
+    lane_slots = jnp.broadcast_to(slot_range.reshape(n_row, capacity, 1), (n_row, capacity, 128))
+    requests = jnp.sum(
+        jnp.where(slot[None, None, None, :] == lane_slots[..., None], col_local[None, None, None, :], 0),
+        axis=-1,
+    )
     own_blocks = rows_of(xb, row_local)
     mirror_terms = jnp.einsum(
         "tfi,tij->tfj", own_blocks, tiles, preferred_element_type=jnp.float32
     ).astype(jnp.bfloat16)
-    outgoing = jnp.zeros((n_row * capacity, feat_q * tile_dim), jnp.bfloat16)
-    outgoing = outgoing.at[slot].set(
-        mirror_terms.reshape(n_tiles, feat_q * tile_dim), mode="promise_in_bounds", unique_indices=True
-    )
-    source = jnp.concatenate([flat_blocks, outgoing], axis=0)
+    outgoing = jnp.zeros((n_row * capacity, feat_q, tile_dim), jnp.bfloat16)
+    outgoing = outgoing.at[slot].set(mirror_terms, mode="promise_in_bounds", unique_indices=True)
+    source = jnp.concatenate([xb, outgoing], axis=0)
     got_ids = lax.all_to_all(requests, "row", split_axis=0, concat_axis=0, tiled=True)
     block_ids = got_ids[:, :, 0]
     mirror_rows = n_blocks + slot_range.reshape(n_row, capacity)
     pick = jnp.concatenate([block_ids, mirror_rows], axis=1)
-    payload = rows_of(source, pick.reshape(-1)).reshape(n_row, 2 * capacity, feat_q * tile_dim)
+    payload = rows_of(source, pick.reshape(-1)).reshape(n_row, 2 * capacity, feat_q, tile_dim)
     both = lax.all_to_all(payload, "row", split_axis=0, concat_axis=0, tiled=True)
-    fetched = both[:, :capacity]
+    fetched = both[:, :capacity].reshape(n_row * capacity, feat_q, tile_dim)
     incoming = both[:, capacity:]
-    fetched_tiles = rows_of(fetched.reshape(n_row * capacity, feat_q, tile_dim), slot)
+    fetched_tiles = rows_of(fetched, slot)
     forward_terms = jnp.einsum(
         "tfj,tij->tfi", fetched_tiles, tiles, preferred_element_type=jnp.float32
     )

time: 52.9 us -> 52.3 us (0.989)
  local copies, waits for them, and re-layouts: 8.26 us -> 6.08 us
  blocking collectives: 11.1 us -> 12 us
  other arithmetic: 1.03 us -> 1.65 us
    unnamed x13 -> x11, local copies, waits for them, and re-layouts: 2.54 us -> 1.39 us
    all_to_all x1, blocking collectives: 11.1 us -> 12 us  [sum_over_row(): lax.all_to_all(every, 'row', split_axis=0, concat_axis=0, tiled=True)]
    reshape x3 -> x1, local copies, waits for them, and re-layouts: 0.97 us -> 0.08 us  [body(): slot_range.reshape(n_row, capacity, 1)]
    transpose x0 -> x1, local copies, waits for them, and re-layouts: none -> 0.85 us  [body(): xb = x_t.reshape(feat_q, n_blocks, tile_dim).transpose(1, 0, 2)]
    broadcast_in_dim x2 -> x1, local copies, waits for them, and re-layouts: 0.76 us -> 0.03 us  [body(): outgoing = jnp.zeros((n_row * capacity, feat_q, tile_dim), jnp.bfloat16)]
    reduce_sum x1, other arithmetic: 0.09 us -> 0.71 us  [body(): jnp.sum(jnp.where(slot[None, None, None, :] == lane_slots[..., None], col...]
    gather x4 -> x3, local copies, waits for them, and re-layouts: 2.4 us -> 2.42 us  [rows_of(): return a.at[idx].get(mode='promise_in_bounds')]
  transfers between devices with their start and end apart: 5 -> 5, of which waited for: 5 -> 4; matrix products, arithmetic and copies ran while one was open for 5% -> 5% of each run, Pallas kernels for 0% -> 0%
where the time goes in v5:
time: 52.3 us; the launch traced here: 51.9 us
  waiting for transfers between devices  16.1 us (31%)
  starting transfers between devices  12.6 us (24%)
  blocking collectives  12 us (23%)
  local copies, waits for them, and re-layouts  6.08 us (12%)
  matrix products  2.63 us (5%)
  other arithmetic  1.65 us (3%)
  between operations  0.83 us (2%)
    all_to_all x1, blocking collectives, sum_over_row(): lax.all_to_all(every, 'row', split_axis=0, concat_axis=0, tiled=True)  12 us
    all_to_all x1, waiting for transfers between devices, body(): lax.all_to_all(payload, 'row', split_axis=0, concat_axis=0, tiled=True)  8.07 us
    all_to_all x1, starting transfers between devices, body(): lax.all_to_all(requests, 'row', split_axis=0, concat_axis=0, tiled=True)  7.28 us
    all_to_all x1, waiting for transfers between devices, body(): lax.all_to_all(requests, 'row', split_axis=0, concat_axis=0, tiled=True)  4.07 us
    ppermute x3, waiting for transfers between devices, gather_groups(): lax.ppermute(z_part, 'col', [(i, i ^ k) for i in range(n_col)])  3.93 us
    all_to_all x1, starting transfers between devices, body(): lax.all_to_all(payload, 'row', split_axis=0, concat_axis=0, tiled=True)  3.41 us
    gather x3, local copies, waits for them, and re-layouts, rows_of(): return a.at[idx].get(mode='promise_in_bounds')  2.42 us
    ppermute x3, starting transfers between devices, gather_groups(): lax.ppermute(z_part, 'col', [(i, i ^ k) for i in range(n_col)])  1.92 us
  transfers between devices with their start and end apart: 5, of which 4 were waited for; matrix products, arithmetic and copies ran while one was open for 5% of the time, Pallas kernels for 0%

profile of v5, /device:TPU:0, one launch (start us, length us, event | category | flops | bytes accessed | tf_op | source)
XLA Modules:
  0.0 51.9 jit_solution(15102144972703468562)
XLA Ops:
  0.6 0.0 copy-start
  0.7 0.0 copy-start.4
  0.7 0.7 %copy-done.4 = s32[8,1]{0,1:T(1,128)S(1)} copy-done((s32[8,1]{0,1:T(1,128)S(1)}, s32[8,1]{0,1:T(1,128)}, u32[]{:S(2)}) %copy-start.4) | copy-done | bytes 56
  1.4 0.2 convert_reduce_fusion
  1.5 0.0 copy-start.1
  1.6 0.7 %copy-done.1 = s32[8,2]{0,1:T(2,128)S(1)} copy-done((s32[8,2]{0,1:T(2,128)S(1)}, s32[8,2]{0,1:T(2,128)}, u32[]{:S(2)}) %copy-start.1) | copy-done | bytes 88
  2.2 0.1 copy.29
  2.3 0.7 %select_reduce_fusion = s32[8,2,128]{2,1,0:T(2,128)} fusion(s32[8]{0:T(128)S(1)} %get-tuple-element.12, s32[8,2]{1,0:T(8,128)S(1)} %copy.29, s32[8]{0:T(128)S(1)} %multiply_add_fusion.1), kind=kLoop, calls=%fused_computation.31 | loop fusion | flops 47104 | bytes 8320 | tf_op jit(solution)/shard_map/reduce_sum | solution.py:63
  3.0 7.3 %all-to-all-start = ((s32[8,2,128]{2,1,0:T(2,128)}), s32[8,2,128]{2,1,0:T(2,128)S(1)}, u32[]{:S(2)}, u32[]{:S(2)}) async-start(s32[8,2,128]{2,1,0:T(2,128)} %select_reduce_fusion), calls=%async_computation | async-start | bytes 16384 | tf_op jit(solution)/shard_map/all_to_all | solution.py:74
  10.3 0.9 %bitcast_bitcast_fusion.1 = bf16[8,32,128]{2,1,0:T(8,128)(2,1)S(1)} fusion(bf16[32,1024]{1,0:T(8,128)(2,1)} %param.6), kind=kLoop, calls=%fused_computation.26 | loop fusion | bytes 131072 | tf_op jit(solution)/shard_map/transpose | solution.py:51
  11.2 0.6 %gather_fusion = bf16[8,32,128]{2,1,0:T(8,128)(2,1)S(1)} fusion(bf16[8,32,128]{2,1,0:T(8,128)(2,1)S(1)} %bitcast_bitcast_fusion.1, s32[1024]{0:T(1024)S(1)} %pad_clamp_fusion.2), kind=kCustom, calls=%fused_computation | custom fusion | bytes 131104 | tf_op jit(solution)/shard_map/gather | solution.py:8
  11.7 0.0 copy-done
  11.8 0.2 convolution_convert_fusion
  12.0 0.7 %scatter_fusion = bf16[16,32,128]{2,1,0:T(8,128)(2,1)S(1)} fusion(bf16[16,32,128]{2,1,0:T(8,128)(2,1)S(1)} %broadcast_in_dim.18, s32[8]{0:T(128)S(1)} %fusion.22, bf16[8,32,128]{2,1,0:T(8,128)(2,1)S(1)} %convolution_convert_fusion), kind=kCustom, calls=%fused_computation.3 | custom fusion | bytes 196640 | tf_op jit(solution)/shard_map/scatter | solution.py:72
  12.7 4.1 %all-to-all-done = s32[8,2,128]{2,1,0:T(2,128)S(1)} async-done(((s32[8,2,128]{2,1,0:T(2,128)}), s32[8,2,128]{2,1,0:T(2,128)S(1)}, u32[]{:S(2)}, u32[]{:S(2)}) %all-to-all-start) | async-done | bytes 8224 | tf_op jit(solution)/shard_map/all_to_all | solution.py:74
  16.8 0.2 slice_reduce_fusion
  17.0 0.1 copy.30
  17.1 0.1 copy.31
  17.2 0.1 reshape.91
  17.3 1.3 %gather_fusion.1 = bf16[32,32,128]{2,1,0:T(8,128)(2,1)} fusion(bf16[24,32,128]{2,1,0:T(8,128)(2,1)S(1)} %pad_maximum_fusion, s32[1024]{0:T(1024)S(1)} %pad_clamp_fusion.1), kind=kCustom, calls=%fused_computation.1 | custom fusion | bytes 524416 | tf_op jit(solution)/shard_map/gather | solution.py:8
  18.6 3.4 %all-to-all-start.1 = ((bf16[8,4,32,128]{3,2,1,0:T(8,128)(2,1)}), bf16[8,4,32,128]{3,2,1,0:T(8,128)(2,1)S(1)}, u32[]{:S(2)}, u32[]{:S(2)}) async-start(bf16[8,4,32,128]{3,2,1,0:T(8,128)(2,1)} %bitcast.10), calls=%async_computation.1 | async-start | bytes 524288 | tf_op jit(solution)/shard_map/all_to_all | solution.py:79
  22.0 0.1 eq.103
  22.1 8.1 %all-to-all-done.1 = bf16[8,4,32,128]{3,2,1,0:T(8,128)(2,1)S(1)} async-done(((bf16[8,4,32,128]{3,2,1,0:T(8,128)(2,1)}), bf16[8,4,32,128]{3,2,1,0:T(8,128)(2,1)S(1)}, u32[]{:S(2)}, u32[]{:S(2)}) %all-to-all-start.1) | async-done | bytes 262176 | tf_op jit(solution)/shard_map/all_to_all | solution.py:79
  30.2 0.6 %gather_fusion.2 = bf16[8,32,128]{2,1,0:T(8,128)(2,1)S(1)} fusion(bf16[16,32,128]{2,1,0:T(8,128)(2,1)S(1)} %bitcast.72, s32[1024]{0:T(1024)S(1)} %pad_clamp_fusion), kind=kCustom, calls=%fused_computation.2 | custom fusion | bytes 131104 | tf_op jit(solution)/shard_map/gather | solution.py:8
  30.8 0.2 fusion.28
  31.0 0.3 fusion.12
  31.3 0.2 fusion
  31.5 0.1 collective-permute-start.2
  31.6 1.6 %collective-permute-start.1 = (bf16[32,1024]{1,0:T(8,128)(2,1)S(1)}, bf16[32,1024]{1,0:T(8,128)(2,1)S(1)}, u32[]{:S(2)}, u32[]{:S(2)}) collective-permute-start(bf16[32,1024]{1,0:T(8,128)(2,1)S(1)} %bitcast.74), channel_id=1, source_target_pairs={{0,2},{1,3},{2,0},{3,1},{4,6},{5,7},{6,4},{7,5},{8,10},{9,11},{10,... | collective-permute-start | bytes 196616 | tf_op jit(solution)/shard_map/ppermute | solution.py:25
  33.1 0.3 collective-permute-start
  33.4 0.0 copy-start.3
  33.4 2.5 %collective-permute-done.2 = bf16[32,1024]{1,0:T(8,128)(2,1)S(1)} collective-permute-done((bf16[32,1024]{1,0:T(8,128)(2,1)S(1)}, bf16[32,1024]{1,0:T(8,128)(2,1)S(1)}, u32[]{:S(2)}, u32[]{:S(2)}) %collective-permute-start.2) | collective-permute-done | bytes 65568 | tf_op jit(solution)/shard_map/ppermute | solution.py:25
  35.9 1.5 %collective-permute-done.1 = bf16[32,1024]{1,0:T(8,128)(2,1)S(1)} collective-permute-done((bf16[32,1024]{1,0:T(8,128)(2,1)S(1)}, bf16[32,1024]{1,0:T(8,128)(2,1)S(1)}, u32[]{:S(2)}, u32[]{:S(2)}) %collective-permute-start.1) | collective-permute-done | bytes 65568 | tf_op jit(solution)/shard_map/ppermute | solution.py:25
  37.3 0.0 collective-permute-done
  37.4 0.0 copy-done.3
  37.4 0.0 copy-start.2
  37.4 1.3 %multiply_convert_fusion.1 = (bf16[1024,256]{1,0:T(8,128)(2,1)}, f32[1024,256]{1,0:T(8,128)S(1)}) fusion(bf16[128,256]{1,0:T(8,128)(2,1)S(1)} %copy-done.3, bf16[32,1024]{1,0:T(8,128)(2,1)S(1)} %get-tuple-element.3, bf16[32,1024]{1,0:T(8,128)(2,1)S(1)} %get-tuple-element.4, bf16[32,1024]{1,0:T(8,128)(2,1)S(1)} %get-tuple-element.5, ...), kind=kOutput, calls=%fused_computation.8 | convolution fusion | flops 69468160 | bytes 1900544 | tf_op jit(solution)/shard_map/dot_general | solution.py:99
  38.7 0.0 copy-done.2
  38.7 0.5 %fusion.1 = f32[32,256]{1,0:T(8,128)S(1)} fusion(f32[1024,256]{1,0:T(8,128)S(1)} %get-tuple-element.14, bf16[1024,256]{1,0:T(8,128)(2,1)S(1)} %copy-done.2, bf16[4,8,8,128]{3,2,1,0:T(8,128)(2,1)S(1)} %bitcast.70), kind=kOutput, calls=%fused_computation.10 | convolution fusion | flops 19398656 | bytes 1671168 | tf_op jit(solution)/shard_map/dot_general | solution.py:107
  39.2 12.0 %all_to_all.15 = f32[8,32,256]{2,1,0:T(8,128)S(1)} all-to-all(f32[8,32,256]{2,1,0:T(8,128)S(1)} %broadcast_in_dim.36), channel_id=1, replica_groups=mesh['row'=8,'col'=4] {'row'}, dimensions={0} | all-to-all | bytes 524288 | tf_op jit(solution)/shard_map/all_to_all | solution.py:37
  51.3 0.6 %fusion.14 = f32[32,256]{1,0:T(8,128)} fusion(f32[8,32,256]{2,1,0:T(8,128)S(1)} %all_to_all.15), kind=kLoop, calls=%fused_computation.33 | loop fusion | flops 57344 | bytes 294912 | tf_op jit(solution)/shard_map/add | solution.py:40
  (16 shorter events, 0.2 us)
Async XLA Ops:
  0.6 11.1 %copy-start = (bf16[8,128,128]{2,1,0:T(8,128)(2,1)S(1)}, bf16[8,128,128]{2,1,0:T(8,128)(2,1)}, u32[]{:S(2)}) copy-start(bf16[8,128,128]{2,1,0:T(8,128)(2,1)} %param.7) | copy-start | bytes 786436
  0.7 0.7 %copy-start.4 = (s32[8,1]{0,1:T(1,128)S(1)}, s32[8,1]{0,1:T(1,128)}, u32[]{:S(2)}) copy-start(s32[8,1]{0,1:T(1,128)} %param.8) | copy-start | bytes 100
  1.5 0.7 %copy-start.1 = (s32[8,2]{0,1:T(2,128)S(1)}, s32[8,2]{0,1:T(2,128)}, u32[]{:S(2)}) copy-start(s32[8,2]{0,1:T(2,128)} %param.9) | copy-start | bytes 196
  3.0 13.8 %all-to-all-start = ((s32[8,2,128]{2,1,0:T(2,128)}), s32[8,2,128]{2,1,0:T(2,128)S(1)}, u32[]{:S(2)}, u32[]{:S(2)}) async-start(s32[8,2,128]{2,1,0:T(2,128)} %select_reduce_fusion), calls=%async_computation | async-start | bytes 16384 | tf_op jit(solution)/shard_map/all_to_all | solution.py:74
  18.6 11.6 %all-to-all-start.1 = ((bf16[8,4,32,128]{3,2,1,0:T(8,128)(2,1)}), bf16[8,4,32,128]{3,2,1,0:T(8,128)(2,1)S(1)}, u32[]{:S(2)}, u32[]{:S(2)}) async-start(bf16[8,4,32,128]{3,2,1,0:T(8,128)(2,1)} %bitcast.10), calls=%async_computation.1 | async-start | bytes 524288 | tf_op jit(solution)/shard_map/all_to_all | solution.py:79
  31.5 4.4 %collective-permute-start.2 = (bf16[32,1024]{1,0:T(8,128)(2,1)S(1)}, bf16[32,1024]{1,0:T(8,128)(2,1)S(1)}, u32[]{:S(2)}, u32[]{:S(2)}) collective-permute-start(bf16[32,1024]{1,0:T(8,128)(2,1)S(1)} %bitcast.73), channel_id=1, source_target_pairs={{0,3},{1,2},{2,1},{3,0},{4,7},{5,6},{6,5},{7,4},{8,11},{9,10},{10,... | collective-permute-start | bytes 196616 | tf_op jit(solution)/shard_map/ppermute | solution.py:25
  31.6 5.8 %collective-permute-start.1 = (bf16[32,1024]{1,0:T(8,128)(2,1)S(1)}, bf16[32,1024]{1,0:T(8,128)(2,1)S(1)}, u32[]{:S(2)}, u32[]{:S(2)}) collective-permute-start(bf16[32,1024]{1,0:T(8,128)(2,1)S(1)} %bitcast.74), channel_id=1, source_target_pairs={{0,2},{1,3},{2,0},{3,1},{4,6},{5,7},{6,4},{7,5},{8,10},{9,11},{10,... | collective-permute-start | bytes 196616 | tf_op jit(solution)/shard_map/ppermute | solution.py:25
  33.1 4.2 %collective-permute-start = (bf16[32,1024]{1,0:T(8,128)(2,1)S(1)}, bf16[32,1024]{1,0:T(8,128)(2,1)S(1)}, u32[]{:S(2)}, u32[]{:S(2)}) collective-permute-start(bf16[32,1024]{1,0:T(8,128)(2,1)S(1)} %bitcast.75), channel_id=1, source_target_pairs={{0,1},{1,0},{2,3},{3,2},{4,5},{5,4},{6,7},{7,6},{8,9},{9,8},{10,11... | collective-permute-start | bytes 196616 | tf_op jit(solution)/shard_map/ppermute | solution.py:25
  33.4 4.0 %copy-start.3 = (bf16[128,256]{1,0:T(8,128)(2,1)S(1)}, bf16[128,256]{1,0:T(8,128)(2,1)}, u32[]{:S(2)}) copy-start(bf16[128,256]{1,0:T(8,128)(2,1)} %param.10) | copy-start | bytes 196612
  37.4 1.3 %copy-start.2 = (bf16[1024,256]{1,0:T(8,128)(2,1)S(1)}, bf16[1024,256]{1,0:T(8,128)(2,1)}, u32[]{:S(2)}) copy-start(bf16[1024,256]{1,0:T(8,128)(2,1)} %param.11) | copy-start | bytes 1572868

commit v6 on v5

--- a/solution.py
+++ b/solution.py
@@ -99,13 +99,14 @@
     y_full = lax.dot_general(
         z_full, weight, (((0,), (0,)), ((), ())), preferred_element_type=jnp.float32
     )
-    act = jax.nn.silu(y_full).astype(jnp.bfloat16)
     sig = jax.nn.sigmoid(y_full)
     grad_y = (cotangent.astype(jnp.float32) * sig * (1.0 + y_full * (1.0 - sig))).astype(
         jnp.bfloat16
     )
     grad_part = jnp.dot(z_part, grad_y, preferred_element_type=jnp.float32)
+    y_late, grad_part = lax.optimization_barrier((y_full, grad_part))
     grad_w = sum_over_row(grad_part, n_row)
+    act = jax.nn.silu(y_late).astype(jnp.bfloat16)
     return (act, grad_w)
 
 

time: 52.3 us -> 53.6 us (1.025)
  blocking collectives: 12 us -> 0 us
  waiting for transfers between devices: 16.1 us -> 24.4 us
  starting transfers between devices: 12.6 us -> 16 us
  local copies, waits for them, and re-layouts: 6.08 us -> 7.49 us
  other arithmetic: 1.65 us -> 2.72 us
  matrix products: 2.63 us -> 1.69 us
    all_to_all x1 -> x0, blocking collectives: 12 us -> none  [sum_over_row(): lax.all_to_all(every, 'row', split_axis=0, concat_axis=0, tiled=True)]
    all_to_all x0 -> x1, waiting for transfers between devices: none -> 8.29 us  [sum_over_row(): lax.all_to_all(every, 'row', split_axis=0, concat_axis=0, tiled=True)]
    all_to_all x0 -> x1, starting transfers between devices: none -> 3.41 us  [sum_over_row(): lax.all_to_all(every, 'row', split_axis=0, concat_axis=0, tiled=True)]
    convert_element_type x0 -> x1, other arithmetic: none -> 1.07 us  [body(): act = jax.nn.silu(y_late).astype(jnp.bfloat16)]
    dot_general x1, matrix products: 1.27 us -> 0.32 us  [body(): lax.dot_general(z_full, weight, (((0,), (0,)), ((), ())), preferred_eleme...]
    unnamed x11, local copies, waits for them, and re-layouts: 1.39 us -> 2.09 us
    broadcast_in_dim x1, local copies, waits for them, and re-layouts: 0.02 us -> 0.72 us  [sum_over_row(): every = jnp.broadcast_to(x[None], (n_row,) + x.shape)]
  transfers between devices with their start and end apart: 5 -> 6, of which waited for: 4 -> 5; matrix products, arithmetic and copies ran while one was open for 5% -> 7% of each run, Pallas kernels for 0% -> 0%
where the time goes in v6:
time: 53.6 us; the launch traced here: 53.1 us
  waiting for transfers between devices  24.4 us (46%)
  starting transfers between devices  16 us (30%)
  local copies, waits for them, and re-layouts  7.49 us (14%)
  other arithmetic  2.72 us (5%)
  matrix products  1.69 us (3%)
  between operations  0.83 us (2%)
    all_to_all x1, waiting for transfers between devices, sum_over_row(): lax.all_to_all(every, 'row', split_axis=0, concat_axis=0, tiled=True)  8.29 us
    all_to_all x1, waiting for transfers between devices, body(): lax.all_to_all(payload, 'row', split_axis=0, concat_axis=0, tiled=True)  8.07 us
    all_to_all x1, starting transfers between devices, body(): lax.all_to_all(requests, 'row', split_axis=0, concat_axis=0, tiled=True)  7.28 us
    all_to_all x1, waiting for transfers between devices, body(): lax.all_to_all(requests, 'row', split_axis=0, concat_axis=0, tiled=True)  4.07 us
    ppermute x3, waiting for transfers between devices, gather_groups(): lax.ppermute(z_part, 'col', [(i, i ^ k) for i in range(n_col)])  3.93 us
    all_to_all x1, starting transfers between devices, body(): lax.all_to_all(payload, 'row', split_axis=0, concat_axis=0, tiled=True)  3.41 us
    all_to_all x1, starting transfers between devices, sum_over_row(): lax.all_to_all(every, 'row', split_axis=0, concat_axis=0, tiled=True)  3.41 us
    gather x3, local copies, waits for them, and re-layouts, rows_of(): return a.at[idx].get(mode='promise_in_bounds')  2.42 us
  transfers between devices with their start and end apart: 6, of which 5 were waited for; matrix products, arithmetic and copies ran while one was open for 7% of the time, Pallas kernels for 0%

profile of v6, /device:TPU:0, one launch (start us, length us, event | category | flops | bytes accessed | tf_op | source)
XLA Modules:
  0.0 53.1 jit_solution(13814651664698134297)
XLA Ops:
  0.6 0.0 copy-start
  0.7 0.0 copy-start.4
  0.7 0.7 %copy-done.4 = s32[8,1]{0,1:T(1,128)S(1)} copy-done((s32[8,1]{0,1:T(1,128)S(1)}, s32[8,1]{0,1:T(1,128)}, u32[]{:S(2)}) %copy-start.4) | copy-done | bytes 56
  1.4 0.2 convert_reduce_fusion
  1.5 0.0 copy-start.2
  1.6 0.7 %copy-done.2 = s32[8,2]{0,1:T(2,128)S(1)} copy-done((s32[8,2]{0,1:T(2,128)S(1)}, s32[8,2]{0,1:T(2,128)}, u32[]{:S(2)}) %copy-start.2) | copy-done | bytes 88
  2.2 0.1 copy.29
  2.3 0.7 %select_reduce_fusion = s32[8,2,128]{2,1,0:T(2,128)} fusion(s32[8]{0:T(128)S(1)} %get-tuple-element.16, s32[8,2]{1,0:T(8,128)S(1)} %copy.29, s32[8]{0:T(128)S(1)} %multiply_add_fusion.1), kind=kLoop, calls=%fused_computation.30 | loop fusion | flops 47104 | bytes 8320 | tf_op jit(solution)/shard_map/reduce_sum | solution.py:63
  3.0 7.3 %all-to-all-start = ((s32[8,2,128]{2,1,0:T(2,128)}), s32[8,2,128]{2,1,0:T(2,128)S(1)}, u32[]{:S(2)}, u32[]{:S(2)}) async-start(s32[8,2,128]{2,1,0:T(2,128)} %select_reduce_fusion), calls=%async_computation | async-start | bytes 16384 | tf_op jit(solution)/shard_map/all_to_all | solution.py:74
  10.3 0.9 %bitcast_bitcast_fusion.1 = bf16[8,32,128]{2,1,0:T(8,128)(2,1)S(1)} fusion(bf16[32,1024]{1,0:T(8,128)(2,1)} %param.6), kind=kLoop, calls=%fused_computation.25 | loop fusion | bytes 131072 | tf_op jit(solution)/shard_map/transpose | solution.py:51
  11.2 0.6 %gather_fusion = bf16[8,32,128]{2,1,0:T(8,128)(2,1)S(1)} fusion(bf16[8,32,128]{2,1,0:T(8,128)(2,1)S(1)} %bitcast_bitcast_fusion.1, s32[1024]{0:T(1024)S(1)} %pad_clamp_fusion.2), kind=kCustom, calls=%fused_computation | custom fusion | bytes 131104 | tf_op jit(solution)/shard_map/gather | solution.py:8
  11.7 0.0 copy-done
  11.8 0.2 convolution_convert_fusion
  12.0 0.7 %scatter_fusion = bf16[16,32,128]{2,1,0:T(8,128)(2,1)S(1)} fusion(bf16[16,32,128]{2,1,0:T(8,128)(2,1)S(1)} %broadcast_in_dim.18, s32[8]{0:T(128)S(1)} %fusion.22, bf16[8,32,128]{2,1,0:T(8,128)(2,1)S(1)} %convolution_convert_fusion), kind=kCustom, calls=%fused_computation.3 | custom fusion | bytes 196640 | tf_op jit(solution)/shard_map/scatter | solution.py:72
  12.7 4.1 %all-to-all-done = s32[8,2,128]{2,1,0:T(2,128)S(1)} async-done(((s32[8,2,128]{2,1,0:T(2,128)}), s32[8,2,128]{2,1,0:T(2,128)S(1)}, u32[]{:S(2)}, u32[]{:S(2)}) %all-to-all-start) | async-done | bytes 8224 | tf_op jit(solution)/shard_map/all_to_all | solution.py:74
  16.8 0.2 slice_reduce_fusion
  17.0 0.1 copy.30
  17.1 0.1 copy.31
  17.2 0.1 reshape.91
  17.3 1.3 %gather_fusion.1 = bf16[32,32,128]{2,1,0:T(8,128)(2,1)} fusion(bf16[24,32,128]{2,1,0:T(8,128)(2,1)S(1)} %pad_maximum_fusion, s32[1024]{0:T(1024)S(1)} %pad_clamp_fusion.1), kind=kCustom, calls=%fused_computation.1 | custom fusion | bytes 524416 | tf_op jit(solution)/shard_map/gather | solution.py:8
  18.6 3.4 %all-to-all-start.1 = ((bf16[8,4,32,128]{3,2,1,0:T(8,128)(2,1)}), bf16[8,4,32,128]{3,2,1,0:T(8,128)(2,1)S(1)}, u32[]{:S(2)}, u32[]{:S(2)}) async-start(bf16[8,4,32,128]{3,2,1,0:T(8,128)(2,1)} %bitcast.10), calls=%async_computation.1 | async-start | bytes 524288 | tf_op jit(solution)/shard_map/all_to_all | solution.py:79
  22.0 0.1 eq.103
  22.1 8.1 %all-to-all-done.1 = bf16[8,4,32,128]{3,2,1,0:T(8,128)(2,1)S(1)} async-done(((bf16[8,4,32,128]{3,2,1,0:T(8,128)(2,1)}), bf16[8,4,32,128]{3,2,1,0:T(8,128)(2,1)S(1)}, u32[]{:S(2)}, u32[]{:S(2)}) %all-to-all-start.1) | async-done | bytes 262176 | tf_op jit(solution)/shard_map/all_to_all | solution.py:79
  30.2 0.6 %gather_fusion.2 = bf16[8,32,128]{2,1,0:T(8,128)(2,1)S(1)} fusion(bf16[16,32,128]{2,1,0:T(8,128)(2,1)S(1)} %bitcast.72, s32[1024]{0:T(1024)S(1)} %pad_clamp_fusion), kind=kCustom, calls=%fused_computation.2 | custom fusion | bytes 131104 | tf_op jit(solution)/shard_map/gather | solution.py:8
  30.8 0.2 fusion.28
  31.0 0.3 fusion.12
  31.3 0.2 fusion
  31.5 0.1 collective-permute-start.2
  31.6 1.6 %collective-permute-start.1 = (bf16[32,1024]{1,0:T(8,128)(2,1)S(1)}, bf16[32,1024]{1,0:T(8,128)(2,1)S(1)}, u32[]{:S(2)}, u32[]{:S(2)}) collective-permute-start(bf16[32,1024]{1,0:T(8,128)(2,1)S(1)} %bitcast.74), channel_id=1, source_target_pairs={{0,2},{1,3},{2,0},{3,1},{4,6},{5,7},{6,4},{7,5},{8,10},{9,11},{10,... | collective-permute-start | bytes 196616 | tf_op jit(solution)/shard_map/ppermute | solution.py:25
  33.1 0.3 collective-permute-start
  33.4 0.0 copy-start.1
  33.4 2.5 %collective-permute-done.2 = bf16[32,1024]{1,0:T(8,128)(2,1)S(1)} collective-permute-done((bf16[32,1024]{1,0:T(8,128)(2,1)S(1)}, bf16[32,1024]{1,0:T(8,128)(2,1)S(1)}, u32[]{:S(2)}, u32[]{:S(2)}) %collective-permute-start.2) | collective-permute-done | bytes 65568 | tf_op jit(solution)/shard_map/ppermute | solution.py:25
  35.9 1.5 %collective-permute-done.1 = bf16[32,1024]{1,0:T(8,128)(2,1)S(1)} collective-permute-done((bf16[32,1024]{1,0:T(8,128)(2,1)S(1)}, bf16[32,1024]{1,0:T(8,128)(2,1)S(1)}, u32[]{:S(2)}, u32[]{:S(2)}) %collective-permute-start.1) | collective-permute-done | bytes 65568 | tf_op jit(solution)/shard_map/ppermute | solution.py:25
  37.3 0.0 collective-permute-done
  37.4 0.0 copy-done.1
  37.4 0.0 copy-start.3
  37.4 0.3 fusion.2
  37.7 0.7 %copy-done.3 = bf16[1024,256]{1,0:T(8,128)(2,1)S(1)} copy-done((bf16[1024,256]{1,0:T(8,128)(2,1)S(1)}, bf16[1024,256]{1,0:T(8,128)(2,1)}, u32[]{:S(2)}) %copy-start.3) | copy-done | bytes 524312
  38.4 0.5 fusion.1
  39.0 0.7 %broadcast_in_dim.36 = f32[8,32,256]{2,1,0:T(8,128)} broadcast(f32[32,256]{1,0:T(8,128)S(1)} %fusion.1), dimensions={1,2} | broadcast | bytes 294912 | tf_op jit(solution)/shard_map/broadcast_in_dim | solution.py:36
  39.7 3.4 %all-to-all-start.2 = ((f32[8,32,256]{2,1,0:T(8,128)}), f32[8,32,256]{2,1,0:T(8,128)S(1)}, u32[]{:S(2)}, u32[]{:S(2)}) async-start(f32[8,32,256]{2,1,0:T(8,128)} %broadcast_in_dim.36), calls=%async_computation.2 | async-start | bytes 524288 | tf_op jit(solution)/shard_map/all_to_all | solution.py:37
  43.1 1.1 %multiply_convert_fusion = bf16[1024,256]{1,0:T(8,128)(2,1)} fusion(f32[1024,256]{1,0:T(8,128)S(1)} %fusion.2), kind=kLoop, calls=%fused_computation.7 | loop fusion | flops 1310720 | bytes 1572864 | tf_op jit(solution)/shard_map/convert_element_type | solution.py:109
  44.2 8.3 %all-to-all-done.2 = f32[8,32,256]{2,1,0:T(8,128)S(1)} async-done(((f32[8,32,256]{2,1,0:T(8,128)}), f32[8,32,256]{2,1,0:T(8,128)S(1)}, u32[]{:S(2)}, u32[]{:S(2)}) %all-to-all-start.2) | async-done | bytes 262176 | tf_op jit(solution)/shard_map/all_to_all | solution.py:37
  52.5 0.6 %fusion.14 = f32[32,256]{1,0:T(8,128)} fusion(f32[8,32,256]{2,1,0:T(8,128)S(1)} %all-to-all-done.2), kind=kLoop, calls=%fused_computation.32 | loop fusion | flops 57344 | bytes 294912 | tf_op jit(solution)/shard_map/add | solution.py:40
  (15 shorter events, 0.2 us)
Async XLA Ops:
  0.6 11.1 %copy-start = (bf16[8,128,128]{2,1,0:T(8,128)(2,1)S(1)}, bf16[8,128,128]{2,1,0:T(8,128)(2,1)}, u32[]{:S(2)}) copy-start(bf16[8,128,128]{2,1,0:T(8,128)(2,1)} %param.7) | copy-start | bytes 786436
  0.7 0.7 %copy-start.4 = (s32[8,1]{0,1:T(1,128)S(1)}, s32[8,1]{0,1:T(1,128)}, u32[]{:S(2)}) copy-start(s32[8,1]{0,1:T(1,128)} %param.8) | copy-start | bytes 100
  1.5 0.7 %copy-start.2 = (s32[8,2]{0,1:T(2,128)S(1)}, s32[8,2]{0,1:T(2,128)}, u32[]{:S(2)}) copy-start(s32[8,2]{0,1:T(2,128)} %param.9) | copy-start | bytes 196
  3.0 13.8 %all-to-all-start = ((s32[8,2,128]{2,1,0:T(2,128)}), s32[8,2,128]{2,1,0:T(2,128)S(1)}, u32[]{:S(2)}, u32[]{:S(2)}) async-start(s32[8,2,128]{2,1,0:T(2,128)} %select_reduce_fusion), calls=%async_computation | async-start | bytes 16384 | tf_op jit(solution)/shard_map/all_to_all | solution.py:74
  18.6 11.6 %all-to-all-start.1 = ((bf16[8,4,32,128]{3,2,1,0:T(8,128)(2,1)}), bf16[8,4,32,128]{3,2,1,0:T(8,128)(2,1)S(1)}, u32[]{:S(2)}, u32[]{:S(2)}) async-start(bf16[8,4,32,128]{3,2,1,0:T(8,128)(2,1)} %bitcast.10), calls=%async_computation.1 | async-start | bytes 524288 | tf_op jit(solution)/shard_map/all_to_all | solution.py:79
  31.5 4.4 %collective-permute-start.2 = (bf16[32,1024]{1,0:T(8,128)(2,1)S(1)}, bf16[32,1024]{1,0:T(8,128)(2,1)S(1)}, u32[]{:S(2)}, u32[]{:S(2)}) collective-permute-start(bf16[32,1024]{1,0:T(8,128)(2,1)S(1)} %bitcast.73), channel_id=1, source_target_pairs={{0,3},{1,2},{2,1},{3,0},{4,7},{5,6},{6,5},{7,4},{8,11},{9,10},{10,... | collective-permute-start | bytes 196616 | tf_op jit(solution)/shard_map/ppermute | solution.py:25
  31.6 5.8 %collective-permute-start.1 = (bf16[32,1024]{1,0:T(8,128)(2,1)S(1)}, bf16[32,1024]{1,0:T(8,128)(2,1)S(1)}, u32[]{:S(2)}, u32[]{:S(2)}) collective-permute-start(bf16[32,1024]{1,0:T(8,128)(2,1)S(1)} %bitcast.74), channel_id=1, source_target_pairs={{0,2},{1,3},{2,0},{3,1},{4,6},{5,7},{6,4},{7,5},{8,10},{9,11},{10,... | collective-permute-start | bytes 196616 | tf_op jit(solution)/shard_map/ppermute | solution.py:25
  33.1 4.2 %collective-permute-start = (bf16[32,1024]{1,0:T(8,128)(2,1)S(1)}, bf16[32,1024]{1,0:T(8,128)(2,1)S(1)}, u32[]{:S(2)}, u32[]{:S(2)}) collective-permute-start(bf16[32,1024]{1,0:T(8,128)(2,1)S(1)} %bitcast.75), channel_id=1, source_target_pairs={{0,1},{1,0},{2,3},{3,2},{4,5},{5,4},{6,7},{7,6},{8,9},{9,8},{10,11... | collective-permute-start | bytes 196616 | tf_op jit(solution)/shard_map/ppermute | solution.py:25
  33.4 4.0 %copy-start.1 = (bf16[128,256]{1,0:T(8,128)(2,1)S(1)}, bf16[128,256]{1,0:T(8,128)(2,1)}, u32[]{:S(2)}) copy-start(bf16[128,256]{1,0:T(8,128)(2,1)} %param.10) | copy-start | bytes 196612
  37.4 1.0 %copy-start.3 = (bf16[1024,256]{1,0:T(8,128)(2,1)S(1)}, bf16[1024,256]{1,0:T(8,128)(2,1)}, u32[]{:S(2)}) copy-start(bf16[1024,256]{1,0:T(8,128)(2,1)} %param.11) | copy-start | bytes 1572868
  39.7 12.8 %all-to-all-start.2 = ((f32[8,32,256]{2,1,0:T(8,128)}), f32[8,32,256]{2,1,0:T(8,128)S(1)}, u32[]{:S(2)}, u32[]{:S(2)}) async-start(f32[8,32,256]{2,1,0:T(8,128)} %broadcast_in_dim.36), calls=%async_computation.2 | async-start | bytes 524288 | tf_op jit(solution)/shard_map/all_to_all | solution.py:37

commit v7 on v5

--- a/solution.py
+++ b/solution.py
@@ -1,6 +1,8 @@
 import jax
 import jax.numpy as jnp
 from jax import lax
+from jax.experimental import pallas as pl
+from jax.experimental.pallas import tpu as pltpu
 from jax.sharding import PartitionSpec as P
 
 
@@ -41,6 +43,40 @@
     return total
 
 
+def payload_kernel(ids_ref, slot_ref, xb_ref, mirror_ref, out_ref):
+    n_row, two_cap = out_ref.shape[0], out_ref.shape[1]
+    capacity = two_cap // 2
+    zero = jnp.zeros(out_ref.shape[2:], out_ref.dtype)
+
+    def fill(o, carry):
+        for k in range(capacity):
+            out_ref[o, k] = xb_ref[ids_ref[o, k, 0]]
+            out_ref[o, capacity + k] = zero
+        return carry
+
+    lax.fori_loop(0, n_row, fill, 0)
+    for t in range(mirror_ref.shape[0]):
+        s = slot_ref[t]
+        out_ref[s // capacity, capacity + s % capacity] = mirror_ref[t]
+
+
+def build_payload(ids, slot, xb, mirror_terms, n_row, capacity):
+    shape = (n_row, 2 * capacity) + xb.shape[1:]
+    nbytes = 2 * (n_row * 2 * capacity + xb.shape[0] + mirror_terms.shape[0]) * xb.shape[1] * xb.shape[2]
+    return pl.pallas_call(
+        payload_kernel,
+        out_shape=jax.ShapeDtypeStruct(shape, xb.dtype),
+        in_specs=[
+            pl.BlockSpec(memory_space=pltpu.SMEM),
+            pl.BlockSpec(memory_space=pltpu.SMEM),
+            pl.BlockSpec(memory_space=pltpu.VMEM),
+            pl.BlockSpec(memory_space=pltpu.VMEM),
+        ],
+        out_specs=pl.BlockSpec(memory_space=pltpu.VMEM),
+        cost_estimate=pl.CostEstimate(flops=0, transcendentals=0, bytes_accessed=nbytes),
+    )(ids, slot, xb, mirror_terms)
+
+
 def body(x_t, tiles, tile_owner, tile_local, weight, cotangent):
     n_row = lax.axis_size("row")
     n_col = lax.axis_size("col")
@@ -68,14 +104,9 @@
     mirror_terms = jnp.einsum(
         "tfi,tij->tfj", own_blocks, tiles, preferred_element_type=jnp.float32
     ).astype(jnp.bfloat16)
-    outgoing = jnp.zeros((n_row * capacity, feat_q, tile_dim), jnp.bfloat16)
-    outgoing = outgoing.at[slot].set(mirror_terms, mode="promise_in_bounds", unique_indices=True)
-    source = jnp.concatenate([xb, outgoing], axis=0)
     got_ids = lax.all_to_all(requests, "row", split_axis=0, concat_axis=0, tiled=True)
     block_ids = got_ids[:, :, 0]
-    mirror_rows = n_blocks + slot_range.reshape(n_row, capacity)
-    pick = jnp.concatenate([block_ids, mirror_rows], axis=1)
-    payload = rows_of(source, pick.reshape(-1)).reshape(n_row, 2 * capacity, feat_q, tile_dim)
+    payload = build_payload(got_ids, slot, xb, mirror_terms, n_row, capacity)
     both = lax.all_to_all(payload, "row", split_axis=0, concat_axis=0, tiled=True)
     fetched = both[:, :capacity].reshape(n_row * capacity, feat_q, tile_dim)
     incoming = both[:, capacity:]

time: 52.3 us -> 53.5 us (1.023)
  Pallas kernels: 0 us -> 1.69 us
  local copies, waits for them, and re-layouts: 6.08 us -> 4.92 us
  matrix products: 2.63 us -> 3.26 us
    pallas_call x0 -> x1, Pallas kernels: none -> 1.69 us  [build_payload(): pl.pallas_call(payload_kernel, out_shape=jax.ShapeDtypeStruct(shape, xb.d...]
    gather x3 -> x2, local copies, waits for them, and re-layouts: 2.42 us -> 1.13 us  [rows_of(): return a.at[idx].get(mode='promise_in_bounds')]
    unnamed x11 -> x19, local copies, waits for them, and re-layouts: 1.39 us -> 2.62 us
    scatter x1 -> x0, local copies, waits for them, and re-layouts: 0.73 us -> none  [body(): outgoing.at[slot]]
    dot_general x1, matrix products: 0.17 us -> 0.8 us  [body(): jnp.einsum('tfi,tij->tfj', own_blocks, tiles, preferred_element_type=jnp....]
where the time goes in v7:
time: 53.5 us; the launch traced here: 53 us
  waiting for transfers between devices  16 us (30%)
  starting transfers between devices  12.7 us (24%)
  blocking collectives  12 us (22%)
  local copies, waits for them, and re-layouts  4.92 us (9%)
  matrix products  3.26 us (6%)
  Pallas kernels  1.69 us (3%)
  other arithmetic  1.6 us (3%)
  between operations  0.8 us (1%)
    all_to_all x1, blocking collectives, sum_over_row(): lax.all_to_all(every, 'row', split_axis=0, concat_axis=0, tiled=True)  12 us
    all_to_all x1, waiting for transfers between devices, body(): lax.all_to_all(payload, 'row', split_axis=0, concat_axis=0, tiled=True)  7.83 us
    all_to_all x1, starting transfers between devices, body(): lax.all_to_all(requests, 'row', split_axis=0, concat_axis=0, tiled=True)  7.28 us
    all_to_all x1, waiting for transfers between devices, body(): lax.all_to_all(requests, 'row', split_axis=0, concat_axis=0, tiled=True)  4.23 us
    ppermute x3, waiting for transfers between devices, gather_groups(): lax.ppermute(z_part, 'col', [(i, i ^ k) for i in range(n_col)])  3.93 us
    all_to_all x1, starting transfers between devices, body(): lax.all_to_all(payload, 'row', split_axis=0, concat_axis=0, tiled=True)  3.54 us
    unnamed x19, local copies, waits for them, and re-layouts  2.62 us
    ppermute x3, starting transfers between devices, gather_groups(): lax.ppermute(z_part, 'col', [(i, i ^ k) for i in range(n_col)])  1.92 us
  transfers between devices with their start and end apart: 5, of which 4 were waited for; matrix products, arithmetic and copies ran while one was open for 5% of the time, Pallas kernels for 0%

profile of v7, /device:TPU:0, one launch (start us, length us, event | category | flops | bytes accessed | tf_op | source)
XLA Modules:
  0.0 53.0 jit_solution(17042229638588947878)
XLA Ops:
  0.6 0.0 copy-start
  0.7 0.0 copy-start.8
  0.7 0.7 %copy-done.8 = s32[8,1]{0,1:T(1,128)S(1)} copy-done((s32[8,1]{0,1:T(1,128)S(1)}, s32[8,1]{0,1:T(1,128)}, u32[]{:S(2)}) %copy-start.8) | copy-done | bytes 56
  1.4 0.2 convert_reduce_fusion
  1.5 0.0 copy-start.5
  1.6 0.7 %copy-done.5 = s32[8,2]{0,1:T(2,128)S(1)} copy-done((s32[8,2]{0,1:T(2,128)S(1)}, s32[8,2]{0,1:T(2,128)}, u32[]{:S(2)}) %copy-start.5) | copy-done | bytes 88
  2.2 0.0 copy-start.4
  2.2 0.6 %copy-done.4 = s32[8]{0:T(128)} copy-done((s32[8]{0:T(128)}, s32[8]{0:T(128)S(1)}, u32[]{:S(2)}) %copy-start.4) | copy-done | bytes 56
  2.8 0.7 %select_reduce_fusion = s32[8,2,128]{2,1,0:T(2,128)} fusion(s32[8]{0:T(128)S(1)} %get-tuple-element.10, s32[8,2]{1,0:T(8,128)S(1)} %multiply_add_fusion, s32[8]{0:T(128)S(1)} %multiply_add_fusion.1.slot_ref), kind=kLoop, calls=%fused_computation.28 | loop fusion | flops 47104 | bytes 8320 | tf_op jit(solution)/shard_map/reduce_sum | solution.py:99
  3.5 7.3 %all-to-all-start = ((s32[8,2,128]{2,1,0:T(2,128)}), s32[8,2,128]{2,1,0:T(2,128)S(1)}, u32[]{:S(2)}, u32[]{:S(2)}) async-start(s32[8,2,128]{2,1,0:T(2,128)} %select_reduce_fusion), calls=%async_computation | async-start | bytes 16384 | tf_op jit(solution)/shard_map/all_to_all | solution.py:107
  10.8 0.9 %bitcast_bitcast_fusion.1.xb_ref = bf16[8,32,128]{2,1,0:T(8,128)(2,1)S(1)} fusion(bf16[32,1024]{1,0:T(8,128)(2,1)} %param.6), kind=kLoop, calls=%fused_computation.23 | loop fusion | bytes 131072 | tf_op jit(solution)/shard_map/transpose | solution.py:87
  11.7 0.0 copy-start.1
  11.7 0.6 %gather_fusion = bf16[8,32,128]{2,1,0:T(8,128)(2,1)S(1)} fusion(bf16[8,32,128]{2,1,0:T(8,128)(2,1)S(1)} %bitcast_bitcast_fusion.1.xb_ref, s32[1024]{0:T(1024)S(1)} %pad_clamp_fusion.1), kind=kCustom, calls=%fused_computation | custom fusion | bytes 131104 | tf_op jit(solution)/shard_map/gather | solution.py:10
  12.2 0.0 copy-done.1
  12.3 0.0 copy-done
  12.3 0.8 %convolution_convert_fusion.mirror_ref = bf16[8,32,128]{2,1,0:T(8,128)(2,1)} fusion(bf16[8,32,128]{2,1,0:T(8,128)(2,1)S(1)} %gather_fusion, bf16[8,128,128]{2,1,0:T(8,128)(2,1)S(1)} %copy-done), kind=kOutput, calls=%fused_computation.4 | convolution fusion | flops 8421376 | bytes 393216 | tf_op jit(solution)/shard_map/tfi,tij->tfj/dot_general | solution.py:104
  13.1 4.2 %all-to-all-done.ids_ref = s32[8,2,128]{2,1,0:T(2,128)S(1)} async-done(((s32[8,2,128]{2,1,0:T(2,128)}), s32[8,2,128]{2,1,0:T(2,128)S(1)}, u32[]{:S(2)}, u32[]{:S(2)}) %all-to-all-start) | async-done | bytes 8224 | tf_op jit(solution)/shard_map/all_to_all | solution.py:107
  17.3 0.0 copy-start.2
  17.3 0.6 %copy-done.2 = s32[8,2,128]{2,1,0:T(2,128)} copy-done((s32[8,2,128]{2,1,0:T(2,128)}, s32[8,2,128]{2,1,0:T(2,128)S(1)}, u32[]{:S(2)}) %copy-start.2) | copy-done | bytes 8216
  17.9 1.7 %shard_map.77 = bf16[8,4,32,128]{3,2,1,0:T(8,128)(2,1)} custom-call(s32[8,2,128]{2,1,0:T(2,128)} %copy-done.2, s32[8]{0:T(128)} %copy-done.4, bf16[8,32,128]{2,1,0:T(8,128)(2,1)} %copy-done.1, bf16[8,32,128]{2,1,0:T(8,128)(2,1)} %convolution_convert_fusion.mirror_ref), custom_call_target="tpu_custom_call" | custom-call | bytes 393216 | tf_op jit(solution)/shard_map/pallas_call | solution.py:66
  19.6 0.0 copy-start.3
  19.6 3.5 %all-to-all-start.1 = ((bf16[8,4,32,128]{3,2,1,0:T(8,128)(2,1)}), bf16[8,4,32,128]{3,2,1,0:T(8,128)(2,1)S(1)}, u32[]{:S(2)}, u32[]{:S(2)}) async-start(bf16[8,4,32,128]{3,2,1,0:T(8,128)(2,1)} %shard_map.77), calls=%async_computation.1 | async-start | bytes 524288 | tf_op jit(solution)/shard_map/all_to_all | solution.py:110
  23.2 0.0 copy-done.3
  23.2 0.2 slice_reduce_fusion
  23.4 0.1 eq.100
  23.5 7.8 %all-to-all-done.1 = bf16[8,4,32,128]{3,2,1,0:T(8,128)(2,1)S(1)} async-done(((bf16[8,4,32,128]{3,2,1,0:T(8,128)(2,1)}), bf16[8,4,32,128]{3,2,1,0:T(8,128)(2,1)S(1)}, u32[]{:S(2)}, u32[]{:S(2)}) %all-to-all-start.1) | async-done | bytes 262176 | tf_op jit(solution)/shard_map/all_to_all | solution.py:110
  31.3 0.6 %gather_fusion.1 = bf16[8,32,128]{2,1,0:T(8,128)(2,1)S(1)} fusion(bf16[16,32,128]{2,1,0:T(8,128)(2,1)S(1)} %bitcast.67, s32[1024]{0:T(1024)S(1)} %pad_clamp_fusion), kind=kCustom, calls=%fused_computation.1 | custom fusion | bytes 131104 | tf_op jit(solution)/shard_map/gather | solution.py:10
  31.9 0.2 fusion.27
  32.1 0.3 fusion.12
  32.4 0.2 fusion
  32.6 0.1 collective-permute-start.2
  32.7 1.6 %collective-permute-start.1 = (bf16[32,1024]{1,0:T(8,128)(2,1)S(1)}, bf16[32,1024]{1,0:T(8,128)(2,1)S(1)}, u32[]{:S(2)}, u32[]{:S(2)}) collective-permute-start(bf16[32,1024]{1,0:T(8,128)(2,1)S(1)} %bitcast.69), channel_id=1, source_target_pairs={{0,2},{1,3},{2,0},{3,1},{4,6},{5,7},{6,4},{7,5},{8,10},{9,11},{10,... | collective-permute-start | bytes 196616 | tf_op jit(solution)/shard_map/ppermute | solution.py:27
  34.2 0.3 collective-permute-start
  34.5 0.0 copy-start.7
  34.5 2.5 %collective-permute-done.2 = bf16[32,1024]{1,0:T(8,128)(2,1)S(1)} collective-permute-done((bf16[32,1024]{1,0:T(8,128)(2,1)S(1)}, bf16[32,1024]{1,0:T(8,128)(2,1)S(1)}, u32[]{:S(2)}, u32[]{:S(2)}) %collective-permute-start.2) | collective-permute-done | bytes 65568 | tf_op jit(solution)/shard_map/ppermute | solution.py:27
  37.0 1.5 %collective-permute-done.1 = bf16[32,1024]{1,0:T(8,128)(2,1)S(1)} collective-permute-done((bf16[32,1024]{1,0:T(8,128)(2,1)S(1)}, bf16[32,1024]{1,0:T(8,128)(2,1)S(1)}, u32[]{:S(2)}, u32[]{:S(2)}) %collective-permute-start.1) | collective-permute-done | bytes 65568 | tf_op jit(solution)/shard_map/ppermute | solution.py:27
  38.5 0.0 collective-permute-done
  38.5 0.0 copy-done.7
  38.5 0.0 copy-start.6
  38.5 1.3 %multiply_convert_fusion.1 = (bf16[1024,256]{1,0:T(8,128)(2,1)}, f32[1024,256]{1,0:T(8,128)S(1)}) fusion(bf16[128,256]{1,0:T(8,128)(2,1)S(1)} %copy-done.7, bf16[32,1024]{1,0:T(8,128)(2,1)S(1)} %get-tuple-element.3, bf16[32,1024]{1,0:T(8,128)(2,1)S(1)} %get-tuple-element.4, bf16[32,1024]{1,0:T(8,128)(2,1)S(1)} %get-tuple-element.5, ...), kind=kOutput, calls=%fused_computation.6 | convolution fusion | flops 69468160 | bytes 1900544 | tf_op jit(solution)/shard_map/dot_general | solution.py:130
  39.8 0.0 copy-done.6
  39.8 0.5 fusion.1
  40.4 12.0 %all_to_all.15 = f32[8,32,256]{2,1,0:T(8,128)S(1)} all-to-all(f32[8,32,256]{2,1,0:T(8,128)S(1)} %broadcast_in_dim.30), channel_id=1, replica_groups=mesh['row'=8,'col'=4] {'row'}, dimensions={0} | all-to-all | bytes 524288 | tf_op jit(solution)/shard_map/all_to_all | solution.py:39
  52.4 0.6 %fusion.14 = f32[32,256]{1,0:T(8,128)} fusion(f32[8,32,256]{2,1,0:T(8,128)S(1)} %all_to_all.15), kind=kLoop, calls=%fused_computation.30 | loop fusion | flops 57344 | bytes 294912 | tf_op jit(solution)/shard_map/add | solution.py:42
  (10 shorter events, 0.1 us)
Async XLA Ops:
  0.6 11.7 %copy-start = (bf16[8,128,128]{2,1,0:T(8,128)(2,1)S(1)}, bf16[8,128,128]{2,1,0:T(8,128)(2,1)}, u32[]{:S(2)}) copy-start(bf16[8,128,128]{2,1,0:T(8,128)(2,1)} %param.7) | copy-start | bytes 786436
  0.7 0.7 %copy-start.8 = (s32[8,1]{0,1:T(1,128)S(1)}, s32[8,1]{0,1:T(1,128)}, u32[]{:S(2)}) copy-start(s32[8,1]{0,1:T(1,128)} %param.8) | copy-start | bytes 100
  1.5 0.7 %copy-start.5 = (s32[8,2]{0,1:T(2,128)S(1)}, s32[8,2]{0,1:T(2,128)}, u32[]{:S(2)}) copy-start(s32[8,2]{0,1:T(2,128)} %param.9) | copy-start | bytes 196
  2.2 0.6 %copy-start.4 = (s32[8]{0:T(128)}, s32[8]{0:T(128)S(1)}, u32[]{:S(2)}) copy-start(s32[8]{0:T(128)S(1)} %multiply_add_fusion.1.slot_ref) | copy-start | bytes 100
  3.5 13.8 %all-to-all-start = ((s32[8,2,128]{2,1,0:T(2,128)}), s32[8,2,128]{2,1,0:T(2,128)S(1)}, u32[]{:S(2)}, u32[]{:S(2)}) async-start(s32[8,2,128]{2,1,0:T(2,128)} %select_reduce_fusion), calls=%async_computation | async-start | bytes 16384 | tf_op jit(solution)/shard_map/all_to_all | solution.py:107
  11.7 0.6 %copy-start.1 = (bf16[8,32,128]{2,1,0:T(8,128)(2,1)}, bf16[8,32,128]{2,1,0:T(8,128)(2,1)S(1)}, u32[]{:S(2)}) copy-start(bf16[8,32,128]{2,1,0:T(8,128)(2,1)S(1)} %bitcast_bitcast_fusion.1.xb_ref) | copy-start | bytes 196612
  17.3 0.6 %copy-start.2 = (s32[8,2,128]{2,1,0:T(2,128)}, s32[8,2,128]{2,1,0:T(2,128)S(1)}, u32[]{:S(2)}) copy-start(s32[8,2,128]{2,1,0:T(2,128)S(1)} %all-to-all-done.ids_ref) | copy-start | bytes 24580
  19.6 3.6 %copy-start.3 = (s32[8,2,128]{2,1,0:T(2,128)S(1)}, s32[8,2,128]{2,1,0:T(2,128)}, u32[]{:S(2)}) copy-start(s32[8,2,128]{2,1,0:T(2,128)} %copy-done.2) | copy-start | bytes 24580
  19.6 11.7 %all-to-all-start.1 = ((bf16[8,4,32,128]{3,2,1,0:T(8,128)(2,1)}), bf16[8,4,32,128]{3,2,1,0:T(8,128)(2,1)S(1)}, u32[]{:S(2)}, u32[]{:S(2)}) async-start(bf16[8,4,32,128]{3,2,1,0:T(8,128)(2,1)} %shard_map.77), calls=%async_computation.1 | async-start | bytes 524288 | tf_op jit(solution)/shard_map/all_to_all | solution.py:110
  32.6 4.4 %collective-permute-start.2 = (bf16[32,1024]{1,0:T(8,128)(2,1)S(1)}, bf16[32,1024]{1,0:T(8,128)(2,1)S(1)}, u32[]{:S(2)}, u32[]{:S(2)}) collective-permute-start(bf16[32,1024]{1,0:T(8,128)(2,1)S(1)} %bitcast.68), channel_id=1, source_target_pairs={{0,3},{1,2},{2,1},{3,0},{4,7},{5,6},{6,5},{7,4},{8,11},{9,10},{10,... | collective-permute-start | bytes 196616 | tf_op jit(solution)/shard_map/ppermute | solution.py:27
  32.7 5.8 %collective-permute-start.1 = (bf16[32,1024]{1,0:T(8,128)(2,1)S(1)}, bf16[32,1024]{1,0:T(8,128)(2,1)S(1)}, u32[]{:S(2)}, u32[]{:S(2)}) collective-permute-start(bf16[32,1024]{1,0:T(8,128)(2,1)S(1)} %bitcast.69), channel_id=1, source_target_pairs={{0,2},{1,3},{2,0},{3,1},{4,6},{5,7},{6,4},{7,5},{8,10},{9,11},{10,... | collective-permute-start | bytes 196616 | tf_op jit(solution)/shard_map/ppermute | solution.py:27
  34.2 4.2 %collective-permute-start = (bf16[32,1024]{1,0:T(8,128)(2,1)S(1)}, bf16[32,1024]{1,0:T(8,128)(2,1)S(1)}, u32[]{:S(2)}, u32[]{:S(2)}) collective-permute-start(bf16[32,1024]{1,0:T(8,128)(2,1)S(1)} %bitcast.70), channel_id=1, source_target_pairs={{0,1},{1,0},{2,3},{3,2},{4,5},{5,4},{6,7},{7,6},{8,9},{9,8},{10,11... | collective-permute-start | bytes 196616 | tf_op jit(solution)/shard_map/ppermute | solution.py:27
  34.5 4.0 %copy-start.7 = (bf16[128,256]{1,0:T(8,128)(2,1)S(1)}, bf16[128,256]{1,0:T(8,128)(2,1)}, u32[]{:S(2)}) copy-start(bf16[128,256]{1,0:T(8,128)(2,1)} %param.10) | copy-start | bytes 196612
  38.5 1.3 %copy-start.6 = (bf16[1024,256]{1,0:T(8,128)(2,1)S(1)}, bf16[1024,256]{1,0:T(8,128)(2,1)}, u32[]{:S(2)}) copy-start(bf16[1024,256]{1,0:T(8,128)(2,1)} %param.11) | copy-start | bytes 1572868

commit v8 on v5

--- a/solution.py
+++ b/solution.py
@@ -50,9 +50,10 @@
     capacity = 2 * (n_tiles // n_row)
     xb = x_t.reshape(feat_q, n_blocks, tile_dim).transpose(1, 0, 2)
     flat_blocks = xb.reshape(n_blocks, feat_q * tile_dim)
-    owner = tile_owner[:, 0]
-    row_local = tile_local[:, 0]
-    col_local = tile_local[:, 1]
+    key = (tile_owner[:, 0] * n_blocks + tile_local[:, 1]) * n_blocks + tile_local[:, 0]
+    owner = key // (n_blocks * n_blocks)
+    col_local = (key // n_blocks) % n_blocks
+    row_local = key % n_blocks
     tile_ids = jnp.arange(n_tiles, dtype=jnp.int32)
     same = owner[:, None] == owner[None, :]
     rank = jnp.sum((same & (tile_ids[None, :] < tile_ids[:, None])).astype(jnp.int32), axis=1)

time: 52.3 us -> 51.7 us (0.989)
  local copies, waits for them, and re-layouts: 6.08 us -> 5.43 us
    unnamed x11, local copies, waits for them, and re-layouts: 1.39 us -> 0.73 us
where the time goes in v8:
time: 51.7 us; the launch traced here: 51.3 us
  waiting for transfers between devices  16.1 us (31%)
  starting transfers between devices  12.6 us (24%)
  blocking collectives  12 us (23%)
  local copies, waits for them, and re-layouts  5.43 us (11%)
  matrix products  2.63 us (5%)
  other arithmetic  1.7 us (3%)
  between operations  0.84 us (2%)
    all_to_all x1, blocking collectives, sum_over_row(): lax.all_to_all(every, 'row', split_axis=0, concat_axis=0, tiled=True)  12 us
    all_to_all x1, waiting for transfers between devices, body(): lax.all_to_all(payload, 'row', split_axis=0, concat_axis=0, tiled=True)  8.07 us
    all_to_all x1, starting transfers between devices, body(): lax.all_to_all(requests, 'row', split_axis=0, concat_axis=0, tiled=True)  7.28 us
    all_to_all x1, waiting for transfers between devices, body(): lax.all_to_all(requests, 'row', split_axis=0, concat_axis=0, tiled=True)  4.07 us
    ppermute x3, waiting for transfers between devices, gather_groups(): lax.ppermute(z_part, 'col', [(i, i ^ k) for i in range(n_col)])  3.93 us
    all_to_all x1, starting transfers between devices, body(): lax.all_to_all(payload, 'row', split_axis=0, concat_axis=0, tiled=True)  3.41 us
    gather x3, local copies, waits for them, and re-layouts, rows_of(): return a.at[idx].get(mode='promise_in_bounds')  2.42 us
    ppermute x3, starting transfers between devices, gather_groups(): lax.ppermute(z_part, 'col', [(i, i ^ k) for i in range(n_col)])  1.92 us
  transfers between devices with their start and end apart: 5, of which 4 were waited for; matrix products, arithmetic and copies ran while one was open for 5% of the time, Pallas kernels for 0%

profile of v8, /device:TPU:0, one launch (start us, length us, event | category | flops | bytes accessed | tf_op | source)
XLA Modules:
  0.0 51.3 jit_solution(4327513298363373138)
XLA Ops:
  0.6 0.0 copy-start
  0.6 0.0 copy-start.1
  0.7 0.0 copy-start.2
  0.7 0.7 %copy-done.1 = s32[8,2]{0,1:T(2,128)S(1)} copy-done((s32[8,2]{0,1:T(2,128)S(1)}, s32[8,2]{0,1:T(2,128)}, u32[]{:S(2)}) %copy-start.1) | copy-done | bytes 88
  1.4 0.0 copy-done.2
  1.4 0.2 convert_reduce_fusion
  1.6 0.1 copy.29
  1.7 0.7 %select_reduce_fusion = s32[8,2,128]{2,1,0:T(2,128)} fusion(s32[8]{0:T(128)S(1)} %get-tuple-element.2, s32[8,2]{1,0:T(8,128)S(1)} %copy.29, s32[8]{0:T(128)S(1)} %multiply_add_fusion.1), kind=kLoop, calls=%fused_computation.31 | loop fusion | flops 47104 | bytes 8320 | tf_op jit(solution)/shard_map/reduce_sum | solution.py:64
  2.4 7.3 %all-to-all-start = ((s32[8,2,128]{2,1,0:T(2,128)}), s32[8,2,128]{2,1,0:T(2,128)S(1)}, u32[]{:S(2)}, u32[]{:S(2)}) async-start(s32[8,2,128]{2,1,0:T(2,128)} %select_reduce_fusion), calls=%async_computation | async-start | bytes 16384 | tf_op jit(solution)/shard_map/all_to_all | solution.py:75
  9.7 0.9 %bitcast_bitcast_fusion.1 = bf16[8,32,128]{2,1,0:T(8,128)(2,1)S(1)} fusion(bf16[32,1024]{1,0:T(8,128)(2,1)} %param.6), kind=kLoop, calls=%fused_computation.26 | loop fusion | bytes 131072 | tf_op jit(solution)/shard_map/transpose | solution.py:51
  10.6 0.6 %gather_fusion = bf16[8,32,128]{2,1,0:T(8,128)(2,1)S(1)} fusion(bf16[8,32,128]{2,1,0:T(8,128)(2,1)S(1)} %bitcast_bitcast_fusion.1, s32[1024]{0:T(1024)S(1)} %pad_clamp_fusion.2), kind=kCustom, calls=%fused_computation | custom fusion | bytes 131104 | tf_op jit(solution)/shard_map/gather | solution.py:8
  11.1 0.0 copy-done
  11.2 0.2 convolution_convert_fusion
  11.4 0.7 %scatter_fusion = bf16[16,32,128]{2,1,0:T(8,128)(2,1)S(1)} fusion(bf16[16,32,128]{2,1,0:T(8,128)(2,1)S(1)} %broadcast_in_dim.16, s32[8]{0:T(128)S(1)} %fusion.23, bf16[8,32,128]{2,1,0:T(8,128)(2,1)S(1)} %convolution_convert_fusion), kind=kCustom, calls=%fused_computation.3 | custom fusion | bytes 196640 | tf_op jit(solution)/shard_map/scatter | solution.py:73
  12.1 4.1 %all-to-all-done = s32[8,2,128]{2,1,0:T(2,128)S(1)} async-done(((s32[8,2,128]{2,1,0:T(2,128)}), s32[8,2,128]{2,1,0:T(2,128)S(1)}, u32[]{:S(2)}, u32[]{:S(2)}) %all-to-all-start) | async-done | bytes 8224 | tf_op jit(solution)/shard_map/all_to_all | solution.py:75
  16.2 0.2 slice_reduce_fusion
  16.4 0.1 copy.30
  16.5 0.1 copy.31
  16.6 0.1 reshape.183
  16.7 1.3 %gather_fusion.1 = bf16[32,32,128]{2,1,0:T(8,128)(2,1)} fusion(bf16[24,32,128]{2,1,0:T(8,128)(2,1)S(1)} %pad_maximum_fusion, s32[1024]{0:T(1024)S(1)} %pad_clamp_fusion.1), kind=kCustom, calls=%fused_computation.1 | custom fusion | bytes 524416 | tf_op jit(solution)/shard_map/gather | solution.py:8
  18.0 3.4 %all-to-all-start.1 = ((bf16[8,4,32,128]{3,2,1,0:T(8,128)(2,1)}), bf16[8,4,32,128]{3,2,1,0:T(8,128)(2,1)S(1)}, u32[]{:S(2)}, u32[]{:S(2)}) async-start(bf16[8,4,32,128]{3,2,1,0:T(8,128)(2,1)} %bitcast.10), calls=%async_computation.1 | async-start | bytes 524288 | tf_op jit(solution)/shard_map/all_to_all | solution.py:80
  21.4 0.1 eq.106
  21.5 8.1 %all-to-all-done.1 = bf16[8,4,32,128]{3,2,1,0:T(8,128)(2,1)S(1)} async-done(((bf16[8,4,32,128]{3,2,1,0:T(8,128)(2,1)}), bf16[8,4,32,128]{3,2,1,0:T(8,128)(2,1)S(1)}, u32[]{:S(2)}, u32[]{:S(2)}) %all-to-all-start.1) | async-done | bytes 262176 | tf_op jit(solution)/shard_map/all_to_all | solution.py:80
  29.6 0.6 %gather_fusion.2 = bf16[8,32,128]{2,1,0:T(8,128)(2,1)S(1)} fusion(bf16[16,32,128]{2,1,0:T(8,128)(2,1)S(1)} %bitcast.85, s32[1024]{0:T(1024)S(1)} %pad_clamp_fusion), kind=kCustom, calls=%fused_computation.2 | custom fusion | bytes 131104 | tf_op jit(solution)/shard_map/gather | solution.py:8
  30.2 0.2 fusion.29
  30.4 0.3 fusion.12
  30.7 0.2 fusion
  30.9 0.1 collective-permute-start.2
  31.0 1.6 %collective-permute-start.1 = (bf16[32,1024]{1,0:T(8,128)(2,1)S(1)}, bf16[32,1024]{1,0:T(8,128)(2,1)S(1)}, u32[]{:S(2)}, u32[]{:S(2)}) collective-permute-start(bf16[32,1024]{1,0:T(8,128)(2,1)S(1)} %bitcast.87), channel_id=1, source_target_pairs={{0,2},{1,3},{2,0},{3,1},{4,6},{5,7},{6,4},{7,5},{8,10},{9,11},{10,... | collective-permute-start | bytes 196616 | tf_op jit(solution)/shard_map/ppermute | solution.py:25
  32.5 0.3 collective-permute-start
  32.8 0.0 copy-start.4
  32.8 2.5 %collective-permute-done.2 = bf16[32,1024]{1,0:T(8,128)(2,1)S(1)} collective-permute-done((bf16[32,1024]{1,0:T(8,128)(2,1)S(1)}, bf16[32,1024]{1,0:T(8,128)(2,1)S(1)}, u32[]{:S(2)}, u32[]{:S(2)}) %collective-permute-start.2) | collective-permute-done | bytes 65568 | tf_op jit(solution)/shard_map/ppermute | solution.py:25
  35.3 1.5 %collective-permute-done.1 = bf16[32,1024]{1,0:T(8,128)(2,1)S(1)} collective-permute-done((bf16[32,1024]{1,0:T(8,128)(2,1)S(1)}, bf16[32,1024]{1,0:T(8,128)(2,1)S(1)}, u32[]{:S(2)}, u32[]{:S(2)}) %collective-permute-start.1) | collective-permute-done | bytes 65568 | tf_op jit(solution)/shard_map/ppermute | solution.py:25
  36.7 0.0 collective-permute-done
  36.8 0.0 copy-done.4
  36.8 0.0 copy-start.3
  36.8 1.3 %multiply_convert_fusion.1 = (bf16[1024,256]{1,0:T(8,128)(2,1)}, f32[1024,256]{1,0:T(8,128)S(1)}) fusion(bf16[128,256]{1,0:T(8,128)(2,1)S(1)} %copy-done.4, bf16[32,1024]{1,0:T(8,128)(2,1)S(1)} %get-tuple-element.7, bf16[32,1024]{1,0:T(8,128)(2,1)S(1)} %get-tuple-element.8, bf16[32,1024]{1,0:T(8,128)(2,1)S(1)} %get-tuple-element.9, ...), kind=kOutput, calls=%fused_computation.8 | convolution fusion | flops 69468160 | bytes 1900544 | tf_op jit(solution)/shard_map/dot_general | solution.py:100
  38.1 0.0 copy-done.3
  38.1 0.5 %fusion.1 = f32[32,256]{1,0:T(8,128)S(1)} fusion(f32[1024,256]{1,0:T(8,128)S(1)} %get-tuple-element.16, bf16[1024,256]{1,0:T(8,128)(2,1)S(1)} %copy-done.3, bf16[4,8,8,128]{3,2,1,0:T(8,128)(2,1)S(1)} %bitcast.83), kind=kOutput, calls=%fused_computation.10 | convolution fusion | flops 19398656 | bytes 1671168 | tf_op jit(solution)/shard_map/dot_general | solution.py:108
  38.6 12.0 %all_to_all.15 = f32[8,32,256]{2,1,0:T(8,128)S(1)} all-to-all(f32[8,32,256]{2,1,0:T(8,128)S(1)} %broadcast_in_dim.19), channel_id=1, replica_groups=mesh['row'=8,'col'=4] {'row'}, dimensions={0} | all-to-all | bytes 524288 | tf_op jit(solution)/shard_map/all_to_all | solution.py:37
  50.7 0.6 %fusion.14 = f32[32,256]{1,0:T(8,128)} fusion(f32[8,32,256]{2,1,0:T(8,128)S(1)} %all_to_all.15), kind=kLoop, calls=%fused_computation.33 | loop fusion | flops 57344 | bytes 294912 | tf_op jit(solution)/shard_map/add | solution.py:40
  (18 shorter events, 0.3 us)
Async XLA Ops:
  0.6 10.5 %copy-start = (bf16[8,128,128]{2,1,0:T(8,128)(2,1)S(1)}, bf16[8,128,128]{2,1,0:T(8,128)(2,1)}, u32[]{:S(2)}) copy-start(bf16[8,128,128]{2,1,0:T(8,128)(2,1)} %param.7) | copy-start | bytes 786436
  0.6 0.7 %copy-start.1 = (s32[8,2]{0,1:T(2,128)S(1)}, s32[8,2]{0,1:T(2,128)}, u32[]{:S(2)}) copy-start(s32[8,2]{0,1:T(2,128)} %param.9) | copy-start | bytes 196
  0.7 0.7 %copy-start.2 = (s32[8,1]{0,1:T(1,128)S(1)}, s32[8,1]{0,1:T(1,128)}, u32[]{:S(2)}) copy-start(s32[8,1]{0,1:T(1,128)} %param.8) | copy-start | bytes 100
  2.4 13.8 %all-to-all-start = ((s32[8,2,128]{2,1,0:T(2,128)}), s32[8,2,128]{2,1,0:T(2,128)S(1)}, u32[]{:S(2)}, u32[]{:S(2)}) async-start(s32[8,2,128]{2,1,0:T(2,128)} %select_reduce_fusion), calls=%async_computation | async-start | bytes 16384 | tf_op jit(solution)/shard_map/all_to_all | solution.py:75
  18.0 11.6 %all-to-all-start.1 = ((bf16[8,4,32,128]{3,2,1,0:T(8,128)(2,1)}), bf16[8,4,32,128]{3,2,1,0:T(8,128)(2,1)S(1)}, u32[]{:S(2)}, u32[]{:S(2)}) async-start(bf16[8,4,32,128]{3,2,1,0:T(8,128)(2,1)} %bitcast.10), calls=%async_computation.1 | async-start | bytes 524288 | tf_op jit(solution)/shard_map/all_to_all | solution.py:80
  30.9 4.4 %collective-permute-start.2 = (bf16[32,1024]{1,0:T(8,128)(2,1)S(1)}, bf16[32,1024]{1,0:T(8,128)(2,1)S(1)}, u32[]{:S(2)}, u32[]{:S(2)}) collective-permute-start(bf16[32,1024]{1,0:T(8,128)(2,1)S(1)} %bitcast.86), channel_id=1, source_target_pairs={{0,3},{1,2},{2,1},{3,0},{4,7},{5,6},{6,5},{7,4},{8,11},{9,10},{10,... | collective-permute-start | bytes 196616 | tf_op jit(solution)/shard_map/ppermute | solution.py:25
  31.0 5.8 %collective-permute-start.1 = (bf16[32,1024]{1,0:T(8,128)(2,1)S(1)}, bf16[32,1024]{1,0:T(8,128)(2,1)S(1)}, u32[]{:S(2)}, u32[]{:S(2)}) collective-permute-start(bf16[32,1024]{1,0:T(8,128)(2,1)S(1)} %bitcast.87), channel_id=1, source_target_pairs={{0,2},{1,3},{2,0},{3,1},{4,6},{5,7},{6,4},{7,5},{8,10},{9,11},{10,... | collective-permute-start | bytes 196616 | tf_op jit(solution)/shard_map/ppermute | solution.py:25
  32.5 4.2 %collective-permute-start = (bf16[32,1024]{1,0:T(8,128)(2,1)S(1)}, bf16[32,1024]{1,0:T(8,128)(2,1)S(1)}, u32[]{:S(2)}, u32[]{:S(2)}) collective-permute-start(bf16[32,1024]{1,0:T(8,128)(2,1)S(1)} %bitcast.88), channel_id=1, source_target_pairs={{0,1},{1,0},{2,3},{3,2},{4,5},{5,4},{6,7},{7,6},{8,9},{9,8},{10,11... | collective-permute-start | bytes 196616 | tf_op jit(solution)/shard_map/ppermute | solution.py:25
  32.8 4.0 %copy-start.4 = (bf16[128,256]{1,0:T(8,128)(2,1)S(1)}, bf16[128,256]{1,0:T(8,128)(2,1)}, u32[]{:S(2)}) copy-start(bf16[128,256]{1,0:T(8,128)(2,1)} %param.10) | copy-start | bytes 196612
  36.8 1.3 %copy-start.3 = (bf16[1024,256]{1,0:T(8,128)(2,1)S(1)}, bf16[1024,256]{1,0:T(8,128)(2,1)}, u32[]{:S(2)}) copy-start(bf16[1024,256]{1,0:T(8,128)(2,1)} %param.11) | copy-start | bytes 1572868

commit v9 on v8

--- a/solution.py
+++ b/solution.py
@@ -71,12 +71,14 @@
     ).astype(jnp.bfloat16)
     outgoing = jnp.zeros((n_row * capacity, feat_q, tile_dim), jnp.bfloat16)
     outgoing = outgoing.at[slot].set(mirror_terms, mode="promise_in_bounds", unique_indices=True)
-    source = jnp.concatenate([xb, outgoing], axis=0)
+    base = jnp.concatenate(
+        [jnp.zeros_like(outgoing), outgoing], axis=0
+    ).reshape(2, n_row, capacity, feat_q, tile_dim).transpose(1, 0, 2, 3, 4)
+    base = base.reshape(n_row, 2 * capacity, feat_q, tile_dim)
     got_ids = lax.all_to_all(requests, "row", split_axis=0, concat_axis=0, tiled=True)
     block_ids = got_ids[:, :, 0]
-    mirror_rows = n_blocks + slot_range.reshape(n_row, capacity)
-    pick = jnp.concatenate([block_ids, mirror_rows], axis=1)
-    payload = rows_of(source, pick.reshape(-1)).reshape(n_row, 2 * capacity, feat_q, tile_dim)
+    asked = rows_of(xb, block_ids.reshape(-1)).reshape(n_row, capacity, feat_q, tile_dim)
+    payload = lax.dynamic_update_slice(base, asked, (0, 0, 0, 0))
     both = lax.all_to_all(payload, "row", split_axis=0, concat_axis=0, tiled=True)
     fetched = both[:, :capacity].reshape(n_row * capacity, feat_q, tile_dim)
     incoming = both[:, capacity:]

time: 51.7 us -> 51.4 us (level)
  other arithmetic: 1.7 us -> 2.42 us
  waiting for transfers between devices: 16.1 us -> 15.4 us
    select_n x1, other arithmetic: 0.02 us -> 0.78 us  [body(): col_local = key // n_blocks % n_blocks]
    transpose x0 -> x1, local copies, waits for them, and re-layouts: none -> 0.72 us  [body(): base = jnp.concatenate([jnp.zeros_like(outgoing), outgoing], axis=0).resh...]
    gather x3, local copies, waits for them, and re-layouts: 2.42 us -> 1.7 us  [rows_of(): return a.at[idx].get(mode='promise_in_bounds')]
    all_to_all x1, waiting for transfers between devices: 4.07 us -> 3.36 us  [body(): lax.all_to_all(requests, 'row', split_axis=0, concat_axis=0, tiled=True)]
    unnamed x11 -> x7, local copies, waits for them, and re-layouts: 0.73 us -> 0.03 us
    dynamic_update_slice x0 -> x1, local copies, waits for them, and re-layouts: none -> 0.68 us  [body(): payload = lax.dynamic_update_slice(base, asked, (0, 0, 0, 0))]
  transfers between devices with their start and end apart: 5 -> 5, of which waited for: 4 -> 4; matrix products, arithmetic and copies ran while one was open for 5% -> 6% of each run, Pallas kernels for 0% -> 0%
where the time goes in v9:
time: 51.4 us; the launch traced here: 51.1 us
  waiting for transfers between devices  15.4 us (30%)
  starting transfers between devices  12.6 us (25%)
  blocking collectives  12 us (23%)
  local copies, waits for them, and re-layouts  5.18 us (10%)
  matrix products  2.63 us (5%)
  other arithmetic  2.42 us (5%)
  between operations  0.82 us (2%)
    all_to_all x1, blocking collectives, sum_over_row(): lax.all_to_all(every, 'row', split_axis=0, concat_axis=0, tiled=True)  12 us
    all_to_all x1, waiting for transfers between devices, body(): lax.all_to_all(payload, 'row', split_axis=0, concat_axis=0, tiled=True)  8.07 us
    all_to_all x1, starting transfers between devices, body(): lax.all_to_all(requests, 'row', split_axis=0, concat_axis=0, tiled=True)  7.28 us
    ppermute x3, waiting for transfers between devices, gather_groups(): lax.ppermute(z_part, 'col', [(i, i ^ k) for i in range(n_col)])  3.93 us
    all_to_all x1, starting transfers between devices, body(): lax.all_to_all(payload, 'row', split_axis=0, concat_axis=0, tiled=True)  3.41 us
    all_to_all x1, waiting for transfers between devices, body(): lax.all_to_all(requests, 'row', split_axis=0, concat_axis=0, tiled=True)  3.36 us
    ppermute x3, starting transfers between devices, gather_groups(): lax.ppermute(z_part, 'col', [(i, i ^ k) for i in range(n_col)])  1.92 us
    gather x3, local copies, waits for them, and re-layouts, rows_of(): return a.at[idx].get(mode='promise_in_bounds')  1.7 us
  transfers between devices with their start and end apart: 5, of which 4 were waited for; matrix products, arithmetic and copies ran while one was open for 6% of the time, Pallas kernels for 0%

profile of v9, /device:TPU:0, one launch (start us, length us, event | category | flops | bytes accessed | tf_op | source)
XLA Modules:
  0.0 51.1 jit_solution(5363154278988607474)
XLA Ops:
  0.6 0.0 copy-start
  0.6 0.8 %and_select_fusion = (s32[8]{0:T(128)S(1)}, s32[8,1]{0,1:T(1,128)S(1)}) fusion(s32[8,2]{0,1:T(2,128)} %param.9, s32[8,1]{0,1:T(1,128)} %param.8), kind=kLoop, calls=%fused_computation.58 | loop fusion | flops 240 | bytes 160 | tf_op jit(solution)/shard_map/jit(remainder)/select_n | solution.py:55
  1.5 0.2 convert_reduce_fusion
  1.7 0.7 %select_reduce_fusion = s32[8,2,128]{2,1,0:T(2,128)} fusion(s32[8]{0:T(128)S(1)} %get-tuple-element.2, s32[8,2]{1,0:T(8,128)S(1)} %multiply_add_fusion, s32[8]{0:T(128)S(1)} %multiply_add_fusion.1), kind=kLoop, calls=%fused_computation.30 | loop fusion | flops 47104 | bytes 8320 | tf_op jit(solution)/shard_map/reduce_sum | solution.py:64
  2.4 7.3 %all-to-all-start = ((s32[8,2,128]{2,1,0:T(2,128)}), s32[8,2,128]{2,1,0:T(2,128)S(1)}, u32[]{:S(2)}, u32[]{:S(2)}) async-start(s32[8,2,128]{2,1,0:T(2,128)} %select_reduce_fusion), calls=%async_computation | async-start | bytes 16384 | tf_op jit(solution)/shard_map/all_to_all | solution.py:78
  9.7 0.9 %bitcast_bitcast_fusion.1 = bf16[8,32,128]{2,1,0:T(8,128)(2,1)S(1)} fusion(bf16[32,1024]{1,0:T(8,128)(2,1)} %param.6), kind=kLoop, calls=%fused_computation.25 | loop fusion | bytes 131072 | tf_op jit(solution)/shard_map/transpose | solution.py:51
  10.5 0.6 %gather_fusion = bf16[8,32,128]{2,1,0:T(8,128)(2,1)S(1)} fusion(bf16[8,32,128]{2,1,0:T(8,128)(2,1)S(1)} %bitcast_bitcast_fusion.1, s32[1024]{0:T(1024)S(1)} %pad_clamp_fusion.2), kind=kCustom, calls=%fused_computation | custom fusion | bytes 131104 | tf_op jit(solution)/shard_map/gather | solution.py:8
  11.1 0.0 copy-done
  11.1 0.2 convolution_convert_fusion
  11.3 0.7 %scatter_fusion = bf16[16,32,128]{2,1,0:T(8,128)(2,1)S(1)} fusion(bf16[16,32,128]{2,1,0:T(8,128)(2,1)S(1)} %broadcast.240, s32[8]{0:T(128)S(1)} %fusion.23, bf16[8,32,128]{2,1,0:T(8,128)(2,1)S(1)} %convolution_convert_fusion), kind=kCustom, calls=%fused_computation.3 | custom fusion | bytes 196640 | tf_op jit(solution)/shard_map/scatter | solution.py:73
  12.1 0.7 %copy.18 = bf16[8,2,2,32,128]{4,3,2,1,0:T(8,128)(2,1)} copy(bf16[8,2,2,32,128]{4,3,2,0,1:T(8,128)(2,1)S(1)} %bitcast.84) | data formatting | bytes 524288 | tf_op jit(solution)/shard_map/transpose | solution.py:76
  12.8 3.4 %all-to-all-done = s32[8,2,128]{2,1,0:T(2,128)S(1)} async-done(((s32[8,2,128]{2,1,0:T(2,128)}), s32[8,2,128]{2,1,0:T(2,128)S(1)}, u32[]{:S(2)}, u32[]{:S(2)}) %all-to-all-start) | async-done | bytes 8224 | tf_op jit(solution)/shard_map/all_to_all | solution.py:78
  16.2 0.2 slice_reduce_fusion
  16.4 0.1 reshape_squeeze.3
  16.5 0.6 %gather_fusion.1 = bf16[16,32,128]{2,1,0:T(8,128)(2,1)S(1)} fusion(bf16[8,32,128]{2,1,0:T(8,128)(2,1)S(1)} %bitcast_bitcast_fusion.1, s32[1024]{0:T(1024)S(1)} %pad_clamp_fusion.1), kind=kCustom, calls=%fused_computation.1 | custom fusion | bytes 262208 | tf_op jit(solution)/shard_map/gather | solution.py:8
  17.1 0.7 %constant_dynamic-update-slice_fusion = bf16[8,4,32,128]{3,2,1,0:T(8,128)(2,1)} fusion(bf16[8,4,32,128]{3,2,1,0:T(8,128)(2,1)} %bitcast.10, bf16[8,2,32,128]{3,2,1,0:T(8,128)(2,1)S(1)} %bitcast.89), kind=kLoop, calls=%fused_computation.80 | loop fusion | bytes 262144 | tf_op jit(solution)/shard_map/dynamic_update_slice | solution.py:81
  17.8 3.4 %all-to-all-start.1 = ((bf16[8,4,32,128]{3,2,1,0:T(8,128)(2,1)}), bf16[8,4,32,128]{3,2,1,0:T(8,128)(2,1)S(1)}, u32[]{:S(2)}, u32[]{:S(2)}) async-start(bf16[8,4,32,128]{3,2,1,0:T(8,128)(2,1)} %constant_dynamic-update-slice_fusion), calls=%async_computation.1 | async-start | bytes 524288 | tf_op jit(solution)/shard_map/all_to_all | solution.py:82
  21.2 0.1 eq.106
  21.3 8.1 %all-to-all-done.1 = bf16[8,4,32,128]{3,2,1,0:T(8,128)(2,1)S(1)} async-done(((bf16[8,4,32,128]{3,2,1,0:T(8,128)(2,1)}), bf16[8,4,32,128]{3,2,1,0:T(8,128)(2,1)S(1)}, u32[]{:S(2)}, u32[]{:S(2)}) %all-to-all-start.1) | async-done | bytes 262176 | tf_op jit(solution)/shard_map/all_to_all | solution.py:82
  29.4 0.6 %gather_fusion.2 = bf16[8,32,128]{2,1,0:T(8,128)(2,1)S(1)} fusion(bf16[16,32,128]{2,1,0:T(8,128)(2,1)S(1)} %bitcast.90, s32[1024]{0:T(1024)S(1)} %pad_clamp_fusion), kind=kCustom, calls=%fused_computation.2 | custom fusion | bytes 131104 | tf_op jit(solution)/shard_map/gather | solution.py:8
  29.9 0.2 fusion.29
  30.2 0.3 fusion.12
  30.4 0.2 fusion
  30.6 0.1 collective-permute-start.2
  30.7 1.6 %collective-permute-start.1 = (bf16[32,1024]{1,0:T(8,128)(2,1)S(1)}, bf16[32,1024]{1,0:T(8,128)(2,1)S(1)}, u32[]{:S(2)}, u32[]{:S(2)}) collective-permute-start(bf16[32,1024]{1,0:T(8,128)(2,1)S(1)} %bitcast.92), channel_id=1, source_target_pairs={{0,2},{1,3},{2,0},{3,1},{4,6},{5,7},{6,4},{7,5},{8,10},{9,11},{10,... | collective-permute-start | bytes 196616 | tf_op jit(solution)/shard_map/ppermute | solution.py:25
  32.3 0.3 collective-permute-start
  32.6 0.0 copy-start.2
  32.6 2.5 %collective-permute-done.2 = bf16[32,1024]{1,0:T(8,128)(2,1)S(1)} collective-permute-done((bf16[32,1024]{1,0:T(8,128)(2,1)S(1)}, bf16[32,1024]{1,0:T(8,128)(2,1)S(1)}, u32[]{:S(2)}, u32[]{:S(2)}) %collective-permute-start.2) | collective-permute-done | bytes 65568 | tf_op jit(solution)/shard_map/ppermute | solution.py:25
  35.0 1.5 %collective-permute-done.1 = bf16[32,1024]{1,0:T(8,128)(2,1)S(1)} collective-permute-done((bf16[32,1024]{1,0:T(8,128)(2,1)S(1)}, bf16[32,1024]{1,0:T(8,128)(2,1)S(1)}, u32[]{:S(2)}, u32[]{:S(2)}) %collective-permute-start.1) | collective-permute-done | bytes 65568 | tf_op jit(solution)/shard_map/ppermute | solution.py:25
  36.5 0.0 collective-permute-done
  36.5 0.0 copy-done.2
  36.6 0.0 copy-start.1
  36.6 1.3 %multiply_convert_fusion.1 = (bf16[1024,256]{1,0:T(8,128)(2,1)}, f32[1024,256]{1,0:T(8,128)S(1)}) fusion(bf16[128,256]{1,0:T(8,128)(2,1)S(1)} %copy-done.2, bf16[32,1024]{1,0:T(8,128)(2,1)S(1)} %get-tuple-element.7, bf16[32,1024]{1,0:T(8,128)(2,1)S(1)} %get-tuple-element.8, bf16[32,1024]{1,0:T(8,128)(2,1)S(1)} %get-tuple-element.9, ...), kind=kOutput, calls=%fused_computation.8 | convolution fusion | flops 69468160 | bytes 1900544 | tf_op jit(solution)/shard_map/dot_general | solution.py:102
  37.8 0.0 copy-done.1
  37.8 0.5 %fusion.1 = f32[32,256]{1,0:T(8,128)S(1)} fusion(f32[1024,256]{1,0:T(8,128)S(1)} %get-tuple-element.14, bf16[1024,256]{1,0:T(8,128)(2,1)S(1)} %copy-done.1, bf16[4,8,8,128]{3,2,1,0:T(8,128)(2,1)S(1)} %bitcast.87), kind=kOutput, calls=%fused_computation.10 | convolution fusion | flops 19398656 | bytes 1671168 | tf_op jit(solution)/shard_map/dot_general | solution.py:110
  38.4 12.0 %all_to_all.15 = f32[8,32,256]{2,1,0:T(8,128)S(1)} all-to-all(f32[8,32,256]{2,1,0:T(8,128)S(1)} %broadcast_in_dim.16), channel_id=1, replica_groups=mesh['row'=8,'col'=4] {'row'}, dimensions={0} | all-to-all | bytes 524288 | tf_op jit(solution)/shard_map/all_to_all | solution.py:37
  50.4 0.6 %fusion.14 = f32[32,256]{1,0:T(8,128)} fusion(f32[8,32,256]{2,1,0:T(8,128)S(1)} %all_to_all.15), kind=kLoop, calls=%fused_computation.32 | loop fusion | flops 57344 | bytes 294912 | tf_op jit(solution)/shard_map/add | solution.py:40
  (15 shorter events, 0.2 us)
Async XLA Ops:
  0.6 10.5 %copy-start = (bf16[8,128,128]{2,1,0:T(8,128)(2,1)S(1)}, bf16[8,128,128]{2,1,0:T(8,128)(2,1)}, u32[]{:S(2)}) copy-start(bf16[8,128,128]{2,1,0:T(8,128)(2,1)} %param.7) | copy-start | bytes 786436
  2.4 13.8 %all-to-all-start = ((s32[8,2,128]{2,1,0:T(2,128)}), s32[8,2,128]{2,1,0:T(2,128)S(1)}, u32[]{:S(2)}, u32[]{:S(2)}) async-start(s32[8,2,128]{2,1,0:T(2,128)} %select_reduce_fusion), calls=%async_computation | async-start | bytes 16384 | tf_op jit(solution)/shard_map/all_to_all | solution.py:78
  17.8 11.6 %all-to-all-start.1 = ((bf16[8,4,32,128]{3,2,1,0:T(8,128)(2,1)}), bf16[8,4,32,128]{3,2,1,0:T(8,128)(2,1)S(1)}, u32[]{:S(2)}, u32[]{:S(2)}) async-start(bf16[8,4,32,128]{3,2,1,0:T(8,128)(2,1)} %constant_dynamic-update-slice_fusion), calls=%async_computation.1 | async-start | bytes 524288 | tf_op jit(solution)/shard_map/all_to_all | solution.py:82
  30.6 4.4 %collective-permute-start.2 = (bf16[32,1024]{1,0:T(8,128)(2,1)S(1)}, bf16[32,1024]{1,0:T(8,128)(2,1)S(1)}, u32[]{:S(2)}, u32[]{:S(2)}) collective-permute-start(bf16[32,1024]{1,0:T(8,128)(2,1)S(1)} %bitcast.91), channel_id=1, source_target_pairs={{0,3},{1,2},{2,1},{3,0},{4,7},{5,6},{6,5},{7,4},{8,11},{9,10},{10,... | collective-permute-start | bytes 196616 | tf_op jit(solution)/shard_map/ppermute | solution.py:25
  30.7 5.8 %collective-permute-start.1 = (bf16[32,1024]{1,0:T(8,128)(2,1)S(1)}, bf16[32,1024]{1,0:T(8,128)(2,1)S(1)}, u32[]{:S(2)}, u32[]{:S(2)}) collective-permute-start(bf16[32,1024]{1,0:T(8,128)(2,1)S(1)} %bitcast.92), channel_id=1, source_target_pairs={{0,2},{1,3},{2,0},{3,1},{4,6},{5,7},{6,4},{7,5},{8,10},{9,11},{10,... | collective-permute-start | bytes 196616 | tf_op jit(solution)/shard_map/ppermute | solution.py:25
  32.3 4.2 %collective-permute-start = (bf16[32,1024]{1,0:T(8,128)(2,1)S(1)}, bf16[32,1024]{1,0:T(8,128)(2,1)S(1)}, u32[]{:S(2)}, u32[]{:S(2)}) collective-permute-start(bf16[32,1024]{1,0:T(8,128)(2,1)S(1)} %bitcast.93), channel_id=1, source_target_pairs={{0,1},{1,0},{2,3},{3,2},{4,5},{5,4},{6,7},{7,6},{8,9},{9,8},{10,11... | collective-permute-start | bytes 196616 | tf_op jit(solution)/shard_map/ppermute | solution.py:25
  32.6 4.0 %copy-start.2 = (bf16[128,256]{1,0:T(8,128)(2,1)S(1)}, bf16[128,256]{1,0:T(8,128)(2,1)}, u32[]{:S(2)}) copy-start(bf16[128,256]{1,0:T(8,128)(2,1)} %param.10) | copy-start | bytes 196612
  36.6 1.3 %copy-start.1 = (bf16[1024,256]{1,0:T(8,128)(2,1)S(1)}, bf16[1024,256]{1,0:T(8,128)(2,1)}, u32[]{:S(2)}) copy-start(bf16[1024,256]{1,0:T(8,128)(2,1)} %param.11) | copy-start | bytes 1572868

commit v10 on v9

--- a/solution.py
+++ b/solution.py
@@ -81,23 +81,20 @@
     payload = lax.dynamic_update_slice(base, asked, (0, 0, 0, 0))
     both = lax.all_to_all(payload, "row", split_axis=0, concat_axis=0, tiled=True)
     fetched = both[:, :capacity].reshape(n_row * capacity, feat_q, tile_dim)
-    incoming = both[:, capacity:]
-    fetched_tiles = rows_of(fetched, slot)
+    incoming = both[:, capacity:].reshape(n_row * capacity, feat_q, tile_dim)
+    tile_of_slot = jnp.sum(jnp.where(slot_hot, tile_ids[None, :], 0), axis=1)
+    slot_used = jnp.any(slot_hot, axis=1)
+    tiles_by_slot = jnp.where(slot_used[:, None, None], rows_of(tiles, tile_of_slot), 0)
+    row_of_slot = jnp.where(slot_used, rows_of(row_local, tile_of_slot), -1)
     forward_terms = jnp.einsum(
-        "tfj,tij->tfi", fetched_tiles, tiles, preferred_element_type=jnp.float32
+        "sfj,sij->sfi", fetched, tiles_by_slot, preferred_element_type=jnp.float32
     )
     block_range = jnp.arange(n_blocks, dtype=jnp.int32)
-    row_hot = (row_local[:, None] == block_range[None, :]).astype(jnp.float32)
-    local_sum = jnp.einsum("tfi,tb->fbi", forward_terms, row_hot, precision=lax.Precision.HIGHEST)
-    in_hot = (block_ids.reshape(-1)[:, None] == block_range[None, :]).astype(jnp.bfloat16)
-    mirror_sum = jnp.einsum(
-        "sk,sb->bk",
-        incoming.reshape(n_row * capacity, feat_q * tile_dim),
-        in_hot,
-        preferred_element_type=jnp.float32,
-    )
-    mirror_sum = mirror_sum.reshape(n_blocks, feat_q, tile_dim).transpose(1, 0, 2)
-    z_part = (local_sum + mirror_sum).reshape(feat_q, rows).astype(jnp.bfloat16)
+    terms = jnp.concatenate([forward_terms, incoming.astype(jnp.float32)], axis=0)
+    targets = jnp.concatenate([row_of_slot, block_ids.reshape(-1)], axis=0)
+    target_hot = (targets[:, None] == block_range[None, :]).astype(jnp.float32)
+    z_sum = jnp.einsum("sfi,sb->fbi", terms, target_hot, precision=lax.Precision.HIGHEST)
+    z_part = z_sum.reshape(feat_q, rows).astype(jnp.bfloat16)
     z_full = gather_groups(z_part, n_col)
     y_full = lax.dot_general(
         z_full, weight, (((0,), (0,)), ((), ())), preferred_element_type=jnp.float32

time: 51.4 us -> 51.3 us (level)
  waiting for transfers between devices: 15.4 us -> 13.8 us
  local copies, waits for them, and re-layouts: 5.18 us -> 5.92 us
    all_to_all x1, waiting for transfers between devices: 8.07 us -> 6.58 us  [body(): lax.all_to_all(payload, 'row', split_axis=0, concat_axis=0, tiled=True)]
    select_n x1 -> x2, other arithmetic: 0.01 us -> 0.78 us  [the longest x1 0.77 us: body(): row_local = key % n_blocks]
    select_n x1, other arithmetic: 0.78 us -> 0.02 us  [body(): col_local = key // n_blocks % n_blocks]
    gather x3 -> x4, local copies, waits for them, and re-layouts: 1.7 us -> 2.45 us  [rows_of(): return a.at[idx].get(mode='promise_in_bounds')]
  transfers between devices with their start and end apart: 5 -> 5, of which waited for: 4 -> 4; matrix products, arithmetic and copies ran while one was open for 6% -> 9% of each run, Pallas kernels for 0% -> 0%
where the time goes in v10:
time: 51.3 us; the launch traced here: 50.9 us
  waiting for transfers between devices  13.8 us (27%)
  starting transfers between devices  12.6 us (25%)
  blocking collectives  12 us (23%)
  local copies, waits for them, and re-layouts  5.92 us (12%)
  matrix products  2.99 us (6%)
  other arithmetic  2.74 us (5%)
  between operations  0.84 us (2%)
    all_to_all x1, blocking collectives, sum_over_row(): lax.all_to_all(every, 'row', split_axis=0, concat_axis=0, tiled=True)  12 us
    all_to_all x1, starting transfers between devices, body(): lax.all_to_all(requests, 'row', split_axis=0, concat_axis=0, tiled=True)  7.28 us
    all_to_all x1, waiting for transfers between devices, body(): lax.all_to_all(payload, 'row', split_axis=0, concat_axis=0, tiled=True)  6.58 us
    ppermute x3, waiting for transfers between devices, gather_groups(): lax.ppermute(z_part, 'col', [(i, i ^ k) for i in range(n_col)])  3.93 us
    all_to_all x1, starting transfers between devices, body(): lax.all_to_all(payload, 'row', split_axis=0, concat_axis=0, tiled=True)  3.41 us
    all_to_all x1, waiting for transfers between devices, body(): lax.all_to_all(requests, 'row', split_axis=0, concat_axis=0, tiled=True)  3.27 us
    gather x4, local copies, waits for them, and re-layouts, rows_of(): return a.at[idx].get(mode='promise_in_bounds')  2.45 us
    ppermute x3, starting transfers between devices, gather_groups(): lax.ppermute(z_part, 'col', [(i, i ^ k) for i in range(n_col)])  1.92 us
  transfers between devices with their start and end apart: 5, of which 4 were waited for; matrix products, arithmetic and copies ran while one was open for 9% of the time, Pallas kernels for 0%

profile of v10, /device:TPU:0, one launch (start us, length us, event | category | flops | bytes accessed | tf_op | source)
XLA Modules:
  0.0 50.9 jit_solution(1601058927814330728)
XLA Ops:
  0.6 0.0 copy-start
  0.6 0.8 %and_select_fusion.3 = (s32[8]{0:T(128)S(1)}, s32[8,1]{0,1:T(1,128)S(1)}) fusion(s32[8,2]{0,1:T(2,128)} %param.9, s32[8,1]{0,1:T(1,128)} %param.8), kind=kLoop, calls=%fused_computation.64 | loop fusion | flops 120 | bytes 160 | tf_op jit(solution)/shard_map/jit(remainder)/select_n | solution.py:56
  1.5 0.2 convert_reduce_fusion
  1.7 0.7 %select_reduce_fusion = s32[8,2,128]{2,1,0:T(2,128)} fusion(s32[8]{0:T(128)S(1)} %get-tuple-element.10, s32[8,2]{1,0:T(8,128)S(1)} %multiply_add_fusion, s32[8]{0:T(128)S(1)} %multiply_add_fusion.1), kind=kLoop, calls=%fused_computation.32 | loop fusion | flops 47104 | bytes 8320 | tf_op jit(solution)/shard_map/reduce_sum | solution.py:64
  2.4 7.3 %all-to-all-start = ((s32[8,2,128]{2,1,0:T(2,128)}), s32[8,2,128]{2,1,0:T(2,128)S(1)}, u32[]{:S(2)}, u32[]{:S(2)}) async-start(s32[8,2,128]{2,1,0:T(2,128)} %select_reduce_fusion), calls=%async_computation | async-start | bytes 16384 | tf_op jit(solution)/shard_map/all_to_all | solution.py:78
  9.7 0.1 select_reduce_fusion.1
  9.8 0.9 %bitcast_bitcast_fusion = bf16[8,32,128]{2,1,0:T(8,128)(2,1)S(1)} fusion(bf16[32,1024]{1,0:T(8,128)(2,1)} %param.6), kind=kLoop, calls=%fused_computation.27 | loop fusion | bytes 131072 | tf_op jit(solution)/shard_map/transpose | solution.py:51
  10.6 0.6 %gather_fusion.1 = bf16[8,32,128]{2,1,0:T(8,128)(2,1)S(1)} fusion(bf16[8,32,128]{2,1,0:T(8,128)(2,1)S(1)} %bitcast_bitcast_fusion, s32[1024]{0:T(1024)S(1)} %pad_clamp_fusion.1), kind=kCustom, calls=%fused_computation.1 | custom fusion | bytes 131104 | tf_op jit(solution)/shard_map/gather | solution.py:8
  11.2 0.0 copy-done
  11.2 0.2 convolution_convert_fusion.1
  11.4 0.7 %scatter_fusion = bf16[16,32,128]{2,1,0:T(8,128)(2,1)S(1)} fusion(bf16[16,32,128]{2,1,0:T(8,128)(2,1)S(1)} %broadcast.288, s32[8]{0:T(128)S(1)} %fusion.22, bf16[8,32,128]{2,1,0:T(8,128)(2,1)S(1)} %convolution_convert_fusion.1), kind=kCustom, calls=%fused_computation.4 | custom fusion | bytes 196640 | tf_op jit(solution)/shard_map/scatter | solution.py:73
  12.2 0.7 %copy.16 = bf16[8,2,2,32,128]{4,3,2,1,0:T(8,128)(2,1)} copy(bf16[8,2,2,32,128]{4,3,2,0,1:T(8,128)(2,1)S(1)} %bitcast.81) | data formatting | bytes 524288 | tf_op jit(solution)/shard_map/transpose | solution.py:76
  12.9 3.3 %all-to-all-done = s32[8,2,128]{2,1,0:T(2,128)S(1)} async-done(((s32[8,2,128]{2,1,0:T(2,128)}), s32[8,2,128]{2,1,0:T(2,128)S(1)}, u32[]{:S(2)}, u32[]{:S(2)}) %all-to-all-start) | async-done | bytes 8224 | tf_op jit(solution)/shard_map/all_to_all | solution.py:78
  16.2 0.2 slice_reduce_fusion
  16.4 0.1 reshape_squeeze.7
  16.5 0.6 %gather_fusion.2 = bf16[16,32,128]{2,1,0:T(8,128)(2,1)S(1)} fusion(bf16[8,32,128]{2,1,0:T(8,128)(2,1)S(1)} %bitcast_bitcast_fusion, s32[1024]{0:T(1024)S(1)} %pad_clamp_fusion), kind=kCustom, calls=%fused_computation.2 | custom fusion | bytes 262208 | tf_op jit(solution)/shard_map/gather | solution.py:8
  17.1 0.7 %constant_dynamic-update-slice_fusion = bf16[8,4,32,128]{3,2,1,0:T(8,128)(2,1)} fusion(bf16[8,4,32,128]{3,2,1,0:T(8,128)(2,1)} %bitcast.11, bf16[8,2,32,128]{3,2,1,0:T(8,128)(2,1)S(1)} %bitcast.86), kind=kLoop, calls=%fused_computation.88 | loop fusion | bytes 262144 | tf_op jit(solution)/shard_map/dynamic_update_slice | solution.py:81
  17.7 3.4 %all-to-all-start.1 = ((bf16[8,4,32,128]{3,2,1,0:T(8,128)(2,1)}), bf16[8,4,32,128]{3,2,1,0:T(8,128)(2,1)S(1)}, u32[]{:S(2)}, u32[]{:S(2)}) async-start(bf16[8,4,32,128]{3,2,1,0:T(8,128)(2,1)} %constant_dynamic-update-slice_fusion), calls=%async_computation.1 | async-start | bytes 524288 | tf_op jit(solution)/shard_map/all_to_all | solution.py:82
  21.2 0.6 %gather_fusion.3 = bf16[16,128,128]{2,1,0:T(8,128)(2,1)S(1)} fusion(bf16[8,128,128]{2,1,0:T(8,128)(2,1)S(1)} %copy-done, s32[1024]{0:T(1024)S(1)} %pad_clamp_fusion.2), kind=kCustom, calls=%fused_computation.3 | custom fusion | bytes 1048640 | tf_op jit(solution)/shard_map/gather | solution.py:8
  21.8 0.7 %gather_fusion = s32[16]{0:T(128)S(1)} fusion(s32[8]{0:T(128)S(1)} %get-tuple-element.2, s32[1024]{0:T(1024)S(1)} %pad_clamp_fusion.2), kind=kCustom, calls=%fused_computation | custom fusion | bytes 192 | tf_op jit(solution)/shard_map/gather | solution.py:8
  22.5 0.1 fusion.15
  22.6 0.1 reshape_squeeze.6
  22.7 0.1 pad_add_fusion
  22.8 6.6 %all-to-all-done.1 = bf16[8,4,32,128]{3,2,1,0:T(8,128)(2,1)S(1)} async-done(((bf16[8,4,32,128]{3,2,1,0:T(8,128)(2,1)}), bf16[8,4,32,128]{3,2,1,0:T(8,128)(2,1)S(1)}, u32[]{:S(2)}, u32[]{:S(2)}) %all-to-all-start.1) | async-done | bytes 262176 | tf_op jit(solution)/shard_map/all_to_all | solution.py:82
  29.4 0.4 fusion.1
  29.9 0.6 %convolution_convert_fusion = bf16[8,32,128]{2,0,1:T(8,128)(2,1)S(1)} fusion(f32[32,32,128]{2,1,0:T(8,128)S(1)} %pad_maximum_fusion, s32[32]{0:T(128)S(1)} %pad_add_fusion), kind=kOutput, calls=%fused_computation.5 | convolution fusion | flops 12615936 | bytes 589952 | tf_op jit(solution)/shard_map/sfi,sb->fbi/dot_general | solution.py:96
  30.5 0.1 collective-permute-start.2
  30.6 1.6 %collective-permute-start.1 = (bf16[32,1024]{1,0:T(8,128)(2,1)S(1)}, bf16[32,1024]{1,0:T(8,128)(2,1)S(1)}, u32[]{:S(2)}, u32[]{:S(2)}) collective-permute-start(bf16[32,1024]{1,0:T(8,128)(2,1)S(1)} %bitcast.88), channel_id=1, source_target_pairs={{0,2},{1,3},{2,0},{3,1},{4,6},{5,7},{6,4},{7,5},{8,10},{9,11},{10,... | collective-permute-start | bytes 196616 | tf_op jit(solution)/shard_map/ppermute | solution.py:25
  32.1 0.3 collective-permute-start
  32.4 0.0 copy-start.2
  32.4 2.5 %collective-permute-done.2 = bf16[32,1024]{1,0:T(8,128)(2,1)S(1)} collective-permute-done((bf16[32,1024]{1,0:T(8,128)(2,1)S(1)}, bf16[32,1024]{1,0:T(8,128)(2,1)S(1)}, u32[]{:S(2)}, u32[]{:S(2)}) %collective-permute-start.2) | collective-permute-done | bytes 65568 | tf_op jit(solution)/shard_map/ppermute | solution.py:25
  34.9 1.5 %collective-permute-done.1 = bf16[32,1024]{1,0:T(8,128)(2,1)S(1)} collective-permute-done((bf16[32,1024]{1,0:T(8,128)(2,1)S(1)}, bf16[32,1024]{1,0:T(8,128)(2,1)S(1)}, u32[]{:S(2)}, u32[]{:S(2)}) %collective-permute-start.1) | collective-permute-done | bytes 65568 | tf_op jit(solution)/shard_map/ppermute | solution.py:25
  36.4 0.0 collective-permute-done
  36.4 0.0 copy-done.2
  36.4 0.0 copy-start.1
  36.4 1.3 %multiply_convert_fusion.1 = (bf16[1024,256]{1,0:T(8,128)(2,1)}, f32[1024,256]{1,0:T(8,128)S(1)}) fusion(bf16[128,256]{1,0:T(8,128)(2,1)S(1)} %copy-done.2, bf16[32,1024]{1,0:T(8,128)(2,1)S(1)} %get-tuple-element.5, bf16[32,1024]{1,0:T(8,128)(2,1)S(1)} %get-tuple-element.6, bf16[32,1024]{1,0:T(8,128)(2,1)S(1)} %get-tuple-element.7, ...), kind=kOutput, calls=%fused_computation.8 | convolution fusion | flops 69468160 | bytes 1900544 | tf_op jit(solution)/shard_map/dot_general | solution.py:99
  37.7 0.0 copy-done.1
  37.7 0.5 %fusion.4 = f32[32,256]{1,0:T(8,128)S(1)} fusion(f32[1024,256]{1,0:T(8,128)S(1)} %get-tuple-element.15, bf16[1024,256]{1,0:T(8,128)(2,1)S(1)} %copy-done.1, bf16[4,8,8,128]{3,2,1,0:T(8,128)(2,1)S(1)} %bitcast.84), kind=kOutput, calls=%fused_computation.15 | convolution fusion | flops 19398656 | bytes 1671168 | tf_op jit(solution)/shard_map/dot_general | solution.py:107
  38.3 12.0 %all_to_all.15 = f32[8,32,256]{2,1,0:T(8,128)S(1)} all-to-all(f32[8,32,256]{2,1,0:T(8,128)S(1)} %broadcast_in_dim.70), channel_id=1, replica_groups=mesh['row'=8,'col'=4] {'row'}, dimensions={0} | all-to-all | bytes 524288 | tf_op jit(solution)/shard_map/all_to_all | solution.py:37
  50.3 0.6 %fusion.14 = f32[32,256]{1,0:T(8,128)} fusion(f32[8,32,256]{2,1,0:T(8,128)S(1)} %all_to_all.15), kind=kLoop, calls=%fused_computation.34 | loop fusion | flops 57344 | bytes 294912 | tf_op jit(solution)/shard_map/add | solution.py:40
  (19 shorter events, 0.3 us)
Async XLA Ops:
  0.6 10.5 %copy-start = (bf16[8,128,128]{2,1,0:T(8,128)(2,1)S(1)}, bf16[8,128,128]{2,1,0:T(8,128)(2,1)}, u32[]{:S(2)}) copy-start(bf16[8,128,128]{2,1,0:T(8,128)(2,1)} %param.7) | copy-start | bytes 786436
  2.4 13.8 %all-to-all-start = ((s32[8,2,128]{2,1,0:T(2,128)}), s32[8,2,128]{2,1,0:T(2,128)S(1)}, u32[]{:S(2)}, u32[]{:S(2)}) async-start(s32[8,2,128]{2,1,0:T(2,128)} %select_reduce_fusion), calls=%async_computation | async-start | bytes 16384 | tf_op jit(solution)/shard_map/all_to_all | solution.py:78
  17.7 11.6 %all-to-all-start.1 = ((bf16[8,4,32,128]{3,2,1,0:T(8,128)(2,1)}), bf16[8,4,32,128]{3,2,1,0:T(8,128)(2,1)S(1)}, u32[]{:S(2)}, u32[]{:S(2)}) async-start(bf16[8,4,32,128]{3,2,1,0:T(8,128)(2,1)} %constant_dynamic-update-slice_fusion), calls=%async_computation.1 | async-start | bytes 524288 | tf_op jit(solution)/shard_map/all_to_all | solution.py:82
  30.5 4.4 %collective-permute-start.2 = (bf16[32,1024]{1,0:T(8,128)(2,1)S(1)}, bf16[32,1024]{1,0:T(8,128)(2,1)S(1)}, u32[]{:S(2)}, u32[]{:S(2)}) collective-permute-start(bf16[32,1024]{1,0:T(8,128)(2,1)S(1)} %bitcast.87), channel_id=1, source_target_pairs={{0,3},{1,2},{2,1},{3,0},{4,7},{5,6},{6,5},{7,4},{8,11},{9,10},{10,... | collective-permute-start | bytes 196616 | tf_op jit(solution)/shard_map/ppermute | solution.py:25
  30.6 5.8 %collective-permute-start.1 = (bf16[32,1024]{1,0:T(8,128)(2,1)S(1)}, bf16[32,1024]{1,0:T(8,128)(2,1)S(1)}, u32[]{:S(2)}, u32[]{:S(2)}) collective-permute-start(bf16[32,1024]{1,0:T(8,128)(2,1)S(1)} %bitcast.88), channel_id=1, source_target_pairs={{0,2},{1,3},{2,0},{3,1},{4,6},{5,7},{6,4},{7,5},{8,10},{9,11},{10,... | collective-permute-start | bytes 196616 | tf_op jit(solution)/shard_map/ppermute | solution.py:25
  32.1 4.2 %collective-permute-start = (bf16[32,1024]{1,0:T(8,128)(2,1)S(1)}, bf16[32,1024]{1,0:T(8,128)(2,1)S(1)}, u32[]{:S(2)}, u32[]{:S(2)}) collective-permute-start(bf16[32,1024]{1,0:T(8,128)(2,1)S(1)} %bitcast.89), channel_id=1, source_target_pairs={{0,1},{1,0},{2,3},{3,2},{4,5},{5,4},{6,7},{7,6},{8,9},{9,8},{10,11... | collective-permute-start | bytes 196616 | tf_op jit(solution)/shard_map/ppermute | solution.py:25
  32.4 4.0 %copy-start.2 = (bf16[128,256]{1,0:T(8,128)(2,1)S(1)}, bf16[128,256]{1,0:T(8,128)(2,1)}, u32[]{:S(2)}) copy-start(bf16[128,256]{1,0:T(8,128)(2,1)} %param.10) | copy-start | bytes 196612
  36.4 1.3 %copy-start.1 = (bf16[1024,256]{1,0:T(8,128)(2,1)S(1)}, bf16[1024,256]{1,0:T(8,128)(2,1)}, u32[]{:S(2)}) copy-start(bf16[1024,256]{1,0:T(8,128)(2,1)} %param.11) | copy-start | bytes 1572868

commit v11 on v10

--- a/solution.py
+++ b/solution.py
@@ -54,6 +54,10 @@
     owner = key // (n_blocks * n_blocks)
     col_local = (key // n_blocks) % n_blocks
     row_local = key % n_blocks
+    if n_col > 1:
+        late_local = lax.ppermute(tile_local, "col", [(i, i ^ 1) for i in range(n_col)])
+    else:
+        late_local = tile_local
     tile_ids = jnp.arange(n_tiles, dtype=jnp.int32)
     same = owner[:, None] == owner[None, :]
     rank = jnp.sum((same & (tile_ids[None, :] < tile_ids[:, None])).astype(jnp.int32), axis=1)
@@ -85,7 +89,7 @@
     tile_of_slot = jnp.sum(jnp.where(slot_hot, tile_ids[None, :], 0), axis=1)
     slot_used = jnp.any(slot_hot, axis=1)
     tiles_by_slot = jnp.where(slot_used[:, None, None], rows_of(tiles, tile_of_slot), 0)
-    row_of_slot = jnp.where(slot_used, rows_of(row_local, tile_of_slot), -1)
+    row_of_slot = jnp.where(slot_used, rows_of(late_local[:, 0], tile_of_slot), -1)
     forward_terms = jnp.einsum(
         "sfj,sij->sfi", fetched, tiles_by_slot, preferred_element_type=jnp.float32
     )

time: 51.3 us -> 52 us (1.014)
  waiting for transfers between devices: 13.8 us -> 14.9 us
  local copies, waits for them, and re-layouts: 5.92 us -> 5.09 us
    all_to_all x1, waiting for transfers between devices: 6.58 us -> 7.6 us  [body(): lax.all_to_all(payload, 'row', split_axis=0, concat_axis=0, tiled=True)]
    transpose x1, local copies, waits for them, and re-layouts: 0.85 us -> 0.01 us  [body(): xb = x_t.reshape(feat_q, n_blocks, tile_dim).transpose(1, 0, 2)]
    select_n x2, other arithmetic: 0.78 us -> 0.02 us  [the longest x1 0.01 us: body(): owner = key // (n_blocks * n_blocks)]
    select_n x1, other arithmetic: 0.02 us -> 0.77 us  [body(): col_local = key // n_blocks % n_blocks]
  transfers between devices with their start and end apart: 5 -> 6, of which waited for: 4 -> 4; matrix products, arithmetic and copies ran while one was open for 9% -> 14% of each run, Pallas kernels for 0% -> 0%
where the time goes in v11:
time: 52 us; the launch traced here: 51.7 us
  waiting for transfers between devices  14.9 us (29%)
  starting transfers between devices  12.7 us (24%)
  blocking collectives  12.4 us (24%)
  local copies, waits for them, and re-layouts  5.09 us (10%)
  matrix products  2.99 us (6%)
  other arithmetic  2.76 us (5%)
  between operations  0.87 us (2%)
    all_to_all x1, blocking collectives, sum_over_row(): lax.all_to_all(every, 'row', split_axis=0, concat_axis=0, tiled=True)  12.4 us
    all_to_all x1, waiting for transfers between devices, body(): lax.all_to_all(payload, 'row', split_axis=0, concat_axis=0, tiled=True)  7.6 us
    all_to_all x1, starting transfers between devices, body(): lax.all_to_all(requests, 'row', split_axis=0, concat_axis=0, tiled=True)  6.84 us
    ppermute x3, waiting for transfers between devices, gather_groups(): lax.ppermute(z_part, 'col', [(i, i ^ k) for i in range(n_col)])  3.93 us
    all_to_all x1, starting transfers between devices, body(): lax.all_to_all(payload, 'row', split_axis=0, concat_axis=0, tiled=True)  3.41 us
    all_to_all x1, waiting for transfers between devices, body(): lax.all_to_all(requests, 'row', split_axis=0, concat_axis=0, tiled=True)  3.34 us
    gather x4, local copies, waits for them, and re-layouts, rows_of(): return a.at[idx].get(mode='promise_in_bounds')  2.45 us
    ppermute x3, starting transfers between devices, gather_groups(): lax.ppermute(z_part, 'col', [(i, i ^ k) for i in range(n_col)])  1.92 us
  transfers between devices with their start and end apart: 6, of which 4 were waited for; matrix products, arithmetic and copies ran while one was open for 14% of the time, Pallas kernels for 0%

profile of v11, /device:TPU:0, one launch (start us, length us, event | category | flops | bytes accessed | tf_op | source)
XLA Modules:
  0.0 51.7 jit_solution(2523337311125123284)
XLA Ops:
  0.6 0.0 copy-start
  0.6 0.0 copy-start.1
  0.7 0.5 %collective-permute-start = (s32[8,2]{0,1:T(2,128)}, s32[8,2]{0,1:T(2,128)S(1)}, u32[]{:S(2)}, u32[]{:S(2)}) collective-permute-start(s32[8,2]{0,1:T(2,128)} %param.9), channel_id=1, source_target_pairs={{0,1},{1,0},{2,3},{3,2},{4,5},{5,4},{6,7},{7,6},{8,9},{9,8},{10,11... | collective-permute-start | bytes 200 | tf_op jit(solution)/shard_map/ppermute | solution.py:58
  1.2 0.8 %and_select_fusion.1 = (s32[8]{0:T(128)S(1)}, s32[8,1]{0,1:T(1,128)S(1)}) fusion(s32[8,2]{0,1:T(2,128)} %param.9, s32[8,1]{0,1:T(1,128)} %param.8), kind=kLoop, calls=%fused_computation.62 | loop fusion | flops 240 | bytes 160 | tf_op jit(solution)/shard_map/jit(remainder)/select_n | solution.py:55
  2.0 0.2 convert_reduce_fusion
  2.2 0.7 %select_reduce_fusion = s32[8,2,128]{2,1,0:T(2,128)} fusion(s32[8]{0:T(128)S(1)} %get-tuple-element.2, s32[8,2]{1,0:T(8,128)S(1)} %multiply_add_fusion, s32[8]{0:T(128)S(1)} %multiply_add_fusion.1), kind=kLoop, calls=%fused_computation.32 | loop fusion | flops 47104 | bytes 8320 | tf_op jit(solution)/shard_map/reduce_sum | solution.py:68
  2.9 6.8 %all-to-all-start = ((s32[8,2,128]{2,1,0:T(2,128)}), s32[8,2,128]{2,1,0:T(2,128)S(1)}, u32[]{:S(2)}, u32[]{:S(2)}) async-start(s32[8,2,128]{2,1,0:T(2,128)} %select_reduce_fusion), calls=%async_computation | async-start | bytes 16384 | tf_op jit(solution)/shard_map/all_to_all | solution.py:82
  9.8 0.1 fusion.15
  9.8 0.1 select_reduce_fusion.1
  9.9 0.0 copy-done.1
  10.0 0.6 %gather_fusion.1 = bf16[8,32,128]{2,1,0:T(8,128)(2,1)S(1)} fusion(bf16[8,32,128]{2,1,0:T(8,128)(2,1)S(1)} %bitcast_bitcast_fusion, s32[1024]{0:T(1024)S(1)} %pad_clamp_fusion.1), kind=kCustom, calls=%fused_computation.1 | custom fusion | bytes 131104 | tf_op jit(solution)/shard_map/gather | solution.py:8
  10.5 0.0 copy-done
  10.5 0.2 convolution_convert_fusion.1
  10.8 0.7 %scatter_fusion = bf16[16,32,128]{2,1,0:T(8,128)(2,1)S(1)} fusion(bf16[16,32,128]{2,1,0:T(8,128)(2,1)S(1)} %broadcast.286, s32[8]{0:T(128)S(1)} %fusion.22, bf16[8,32,128]{2,1,0:T(8,128)(2,1)S(1)} %convolution_convert_fusion.1), kind=kCustom, calls=%fused_computation.4 | custom fusion | bytes 196640 | tf_op jit(solution)/shard_map/scatter | solution.py:77
  11.5 0.7 %copy.16 = bf16[8,2,2,32,128]{4,3,2,1,0:T(8,128)(2,1)} copy(bf16[8,2,2,32,128]{4,3,2,0,1:T(8,128)(2,1)S(1)} %bitcast.74) | data formatting | bytes 524288 | tf_op jit(solution)/shard_map/transpose | solution.py:80
  12.3 0.6 %gather_fusion.3 = bf16[16,128,128]{2,1,0:T(8,128)(2,1)S(1)} fusion(bf16[8,128,128]{2,1,0:T(8,128)(2,1)S(1)} %copy-done, s32[1024]{0:T(1024)S(1)} %pad_clamp_fusion.2), kind=kCustom, calls=%fused_computation.3 | custom fusion | bytes 1048640 | tf_op jit(solution)/shard_map/gather | solution.py:8
  12.9 3.3 %all-to-all-done = s32[8,2,128]{2,1,0:T(2,128)S(1)} async-done(((s32[8,2,128]{2,1,0:T(2,128)}), s32[8,2,128]{2,1,0:T(2,128)S(1)}, u32[]{:S(2)}, u32[]{:S(2)}) %all-to-all-start) | async-done | bytes 8224 | tf_op jit(solution)/shard_map/all_to_all | solution.py:82
  16.3 0.2 slice_reduce_fusion
  16.5 0.1 reshape_squeeze.7
  16.6 0.6 %gather_fusion.2 = bf16[16,32,128]{2,1,0:T(8,128)(2,1)S(1)} fusion(bf16[8,32,128]{2,1,0:T(8,128)(2,1)S(1)} %bitcast_bitcast_fusion, s32[1024]{0:T(1024)S(1)} %pad_clamp_fusion), kind=kCustom, calls=%fused_computation.2 | custom fusion | bytes 262208 | tf_op jit(solution)/shard_map/gather | solution.py:8
  17.2 0.7 %constant_dynamic-update-slice_fusion = bf16[8,4,32,128]{3,2,1,0:T(8,128)(2,1)} fusion(bf16[8,4,32,128]{3,2,1,0:T(8,128)(2,1)} %bitcast.12, bf16[8,2,32,128]{3,2,1,0:T(8,128)(2,1)S(1)} %bitcast.79), kind=kLoop, calls=%fused_computation.87 | loop fusion | bytes 262144 | tf_op jit(solution)/shard_map/dynamic_update_slice | solution.py:85
  17.8 3.4 %all-to-all-start.1 = ((bf16[8,4,32,128]{3,2,1,0:T(8,128)(2,1)}), bf16[8,4,32,128]{3,2,1,0:T(8,128)(2,1)S(1)}, u32[]{:S(2)}, u32[]{:S(2)}) async-start(bf16[8,4,32,128]{3,2,1,0:T(8,128)(2,1)} %constant_dynamic-update-slice_fusion), calls=%async_computation.1 | async-start | bytes 524288 | tf_op jit(solution)/shard_map/all_to_all | solution.py:86
  21.3 0.0 collective-permute-done
  21.3 0.7 %gather_fusion = s32[16]{0:T(128)S(1)} fusion(s32[8]{0:T(128)S(1)} %slice_bitcast_fusion, s32[1024]{0:T(1024)S(1)} %pad_clamp_fusion.2), kind=kCustom, calls=%fused_computation | custom fusion | bytes 192 | tf_op jit(solution)/shard_map/gather | solution.py:8
  22.0 0.1 reshape_squeeze.6
  22.0 0.1 pad_add_fusion
  22.1 7.6 %all-to-all-done.1 = bf16[8,4,32,128]{3,2,1,0:T(8,128)(2,1)S(1)} async-done(((bf16[8,4,32,128]{3,2,1,0:T(8,128)(2,1)}), bf16[8,4,32,128]{3,2,1,0:T(8,128)(2,1)S(1)}, u32[]{:S(2)}, u32[]{:S(2)}) %all-to-all-start.1) | async-done | bytes 262176 | tf_op jit(solution)/shard_map/all_to_all | solution.py:86
  29.8 0.4 fusion.1
  30.3 0.6 %convolution_convert_fusion = bf16[8,32,128]{2,0,1:T(8,128)(2,1)S(1)} fusion(f32[32,32,128]{2,1,0:T(8,128)S(1)} %pad_maximum_fusion, s32[32]{0:T(128)S(1)} %pad_add_fusion), kind=kOutput, calls=%fused_computation.5 | convolution fusion | flops 12615936 | bytes 589952 | tf_op jit(solution)/shard_map/sfi,sb->fbi/dot_general | solution.py:100
  30.9 0.1 collective-permute-start.3
  31.0 1.6 %collective-permute-start.2 = (bf16[32,1024]{1,0:T(8,128)(2,1)S(1)}, bf16[32,1024]{1,0:T(8,128)(2,1)S(1)}, u32[]{:S(2)}, u32[]{:S(2)}) collective-permute-start(bf16[32,1024]{1,0:T(8,128)(2,1)S(1)} %bitcast.81), channel_id=1, source_target_pairs={{0,2},{1,3},{2,0},{3,1},{4,6},{5,7},{6,4},{7,5},{8,10},{9,11},{10,... | collective-permute-start | bytes 196616 | tf_op jit(solution)/shard_map/ppermute | solution.py:25
  32.5 0.3 collective-permute-start.1
  32.8 0.0 copy-start.3
  32.8 2.5 %collective-permute-done.3 = bf16[32,1024]{1,0:T(8,128)(2,1)S(1)} collective-permute-done((bf16[32,1024]{1,0:T(8,128)(2,1)S(1)}, bf16[32,1024]{1,0:T(8,128)(2,1)S(1)}, u32[]{:S(2)}, u32[]{:S(2)}) %collective-permute-start.3) | collective-permute-done | bytes 65568 | tf_op jit(solution)/shard_map/ppermute | solution.py:25
  35.3 1.5 %collective-permute-done.2 = bf16[32,1024]{1,0:T(8,128)(2,1)S(1)} collective-permute-done((bf16[32,1024]{1,0:T(8,128)(2,1)S(1)}, bf16[32,1024]{1,0:T(8,128)(2,1)S(1)}, u32[]{:S(2)}, u32[]{:S(2)}) %collective-permute-start.2) | collective-permute-done | bytes 65568 | tf_op jit(solution)/shard_map/ppermute | solution.py:25
  36.7 0.0 collective-permute-done.1
  36.8 0.0 copy-done.3
  36.8 0.0 copy-start.2
  36.8 1.3 %multiply_convert_fusion.1 = (bf16[1024,256]{1,0:T(8,128)(2,1)}, f32[1024,256]{1,0:T(8,128)S(1)}) fusion(bf16[128,256]{1,0:T(8,128)(2,1)S(1)} %copy-done.3, bf16[32,1024]{1,0:T(8,128)(2,1)S(1)} %get-tuple-element.5, bf16[32,1024]{1,0:T(8,128)(2,1)S(1)} %get-tuple-element.6, bf16[32,1024]{1,0:T(8,128)(2,1)S(1)} %get-tuple-element.7, ...), kind=kOutput, calls=%fused_computation.8 | convolution fusion | flops 69468160 | bytes 1900544 | tf_op jit(solution)/shard_map/dot_general | solution.py:103
  38.1 0.0 copy-done.2
  38.1 0.5 %fusion.4 = f32[32,256]{1,0:T(8,128)S(1)} fusion(f32[1024,256]{1,0:T(8,128)S(1)} %get-tuple-element.13, bf16[1024,256]{1,0:T(8,128)(2,1)S(1)} %copy-done.2, bf16[4,8,8,128]{3,2,1,0:T(8,128)(2,1)S(1)} %bitcast.77), kind=kOutput, calls=%fused_computation.15 | convolution fusion | flops 19398656 | bytes 1671168 | tf_op jit(solution)/shard_map/dot_general | solution.py:111
  38.6 12.4 %all_to_all.15 = f32[8,32,256]{2,1,0:T(8,128)S(1)} all-to-all(f32[8,32,256]{2,1,0:T(8,128)S(1)} %broadcast_in_dim.70), channel_id=1, replica_groups=mesh['row'=8,'col'=4] {'row'}, dimensions={0} | all-to-all | bytes 524288 | tf_op jit(solution)/shard_map/all_to_all | solution.py:37
  51.1 0.6 %fusion.14 = f32[32,256]{1,0:T(8,128)} fusion(f32[8,32,256]{2,1,0:T(8,128)S(1)} %all_to_all.15), kind=kLoop, calls=%fused_computation.34 | loop fusion | flops 57344 | bytes 294912 | tf_op jit(solution)/shard_map/add | solution.py:40
  (21 shorter events, 0.3 us)
Async XLA Ops:
  0.6 9.9 %copy-start = (bf16[8,128,128]{2,1,0:T(8,128)(2,1)S(1)}, bf16[8,128,128]{2,1,0:T(8,128)(2,1)}, u32[]{:S(2)}) copy-start(bf16[8,128,128]{2,1,0:T(8,128)(2,1)} %param.7) | copy-start | bytes 786436
  0.6 9.3 %copy-start.1 = (bf16[32,1024]{1,0:T(8,128)(2,1)S(1)}, bf16[32,1024]{1,0:T(8,128)(2,1)}, u32[]{:S(2)}) copy-start(bf16[32,1024]{1,0:T(8,128)(2,1)} %param.6) | copy-start | bytes 196612
  0.7 20.6 %collective-permute-start = (s32[8,2]{0,1:T(2,128)}, s32[8,2]{0,1:T(2,128)S(1)}, u32[]{:S(2)}, u32[]{:S(2)}) collective-permute-start(s32[8,2]{0,1:T(2,128)} %param.9), channel_id=1, source_target_pairs={{0,1},{1,0},{2,3},{3,2},{4,5},{5,4},{6,7},{7,6},{8,9},{9,8},{10,11... | collective-permute-start | bytes 200 | tf_op jit(solution)/shard_map/ppermute | solution.py:58
  2.9 13.4 %all-to-all-start = ((s32[8,2,128]{2,1,0:T(2,128)}), s32[8,2,128]{2,1,0:T(2,128)S(1)}, u32[]{:S(2)}, u32[]{:S(2)}) async-start(s32[8,2,128]{2,1,0:T(2,128)} %select_reduce_fusion), calls=%async_computation | async-start | bytes 16384 | tf_op jit(solution)/shard_map/all_to_all | solution.py:82
  17.8 11.9 %all-to-all-start.1 = ((bf16[8,4,32,128]{3,2,1,0:T(8,128)(2,1)}), bf16[8,4,32,128]{3,2,1,0:T(8,128)(2,1)S(1)}, u32[]{:S(2)}, u32[]{:S(2)}) async-start(bf16[8,4,32,128]{3,2,1,0:T(8,128)(2,1)} %constant_dynamic-update-slice_fusion), calls=%async_computation.1 | async-start | bytes 524288 | tf_op jit(solution)/shard_map/all_to_all | solution.py:86
  30.9 4.4 %collective-permute-start.3 = (bf16[32,1024]{1,0:T(8,128)(2,1)S(1)}, bf16[32,1024]{1,0:T(8,128)(2,1)S(1)}, u32[]{:S(2)}, u32[]{:S(2)}) collective-permute-start(bf16[32,1024]{1,0:T(8,128)(2,1)S(1)} %bitcast.80), channel_id=1, source_target_pairs={{0,3},{1,2},{2,1},{3,0},{4,7},{5,6},{6,5},{7,4},{8,11},{9,10},{10,... | collective-permute-start | bytes 196616 | tf_op jit(solution)/shard_map/ppermute | solution.py:25
  31.0 5.8 %collective-permute-start.2 = (bf16[32,1024]{1,0:T(8,128)(2,1)S(1)}, bf16[32,1024]{1,0:T(8,128)(2,1)S(1)}, u32[]{:S(2)}, u32[]{:S(2)}) collective-permute-start(bf16[32,1024]{1,0:T(8,128)(2,1)S(1)} %bitcast.81), channel_id=1, source_target_pairs={{0,2},{1,3},{2,0},{3,1},{4,6},{5,7},{6,4},{7,5},{8,10},{9,11},{10,... | collective-permute-start | bytes 196616 | tf_op jit(solution)/shard_map/ppermute | solution.py:25
  32.5 4.2 %collective-permute-start.1 = (bf16[32,1024]{1,0:T(8,128)(2,1)S(1)}, bf16[32,1024]{1,0:T(8,128)(2,1)S(1)}, u32[]{:S(2)}, u32[]{:S(2)}) collective-permute-start(bf16[32,1024]{1,0:T(8,128)(2,1)S(1)} %bitcast.82), channel_id=1, source_target_pairs={{0,1},{1,0},{2,3},{3,2},{4,5},{5,4},{6,7},{7,6},{8,9},{9,8},{10,11... | collective-permute-start | bytes 196616 | tf_op jit(solution)/shard_map/ppermute | solution.py:25
  32.8 4.0 %copy-start.3 = (bf16[128,256]{1,0:T(8,128)(2,1)S(1)}, bf16[128,256]{1,0:T(8,128)(2,1)}, u32[]{:S(2)}) copy-start(bf16[128,256]{1,0:T(8,128)(2,1)} %param.10) | copy-start | bytes 196612
  36.8 1.3 %copy-start.2 = (bf16[1024,256]{1,0:T(8,128)(2,1)S(1)}, bf16[1024,256]{1,0:T(8,128)(2,1)}, u32[]{:S(2)}) copy-start(bf16[1024,256]{1,0:T(8,128)(2,1)} %param.11) | copy-start | bytes 1572868

commit v12 on v10

--- a/solution.py
+++ b/solution.py
@@ -1,6 +1,8 @@
 import jax
 import jax.numpy as jnp
 from jax import lax
+from jax.experimental import pallas as pl
+from jax.experimental.pallas import tpu as pltpu
 from jax.sharding import PartitionSpec as P
 
 
@@ -39,6 +41,34 @@
     for i in range(1, n_row):
         total = total + parts[i]
     return total
+
+
+def tail_kernel(z_full_ref, w_ref, cot_ref, z_part_ref, act_ref, grad_ref):
+    y = lax.dot_general(
+        z_full_ref[...], w_ref[...], (((0,), (0,)), ((), ())), preferred_element_type=jnp.float32
+    )
+    sig = 1.0 / (1.0 + jnp.exp(-y))
+    act_ref[...] = (y * sig).astype(act_ref.dtype)
+    grad_y = (cot_ref[...].astype(jnp.float32) * sig * (1.0 + y * (1.0 - sig))).astype(jnp.bfloat16)
+    grad_ref[...] = jnp.dot(z_part_ref[...], grad_y, preferred_element_type=jnp.float32)
+
+
+def layer_tail(z_full, weight, cotangent, z_part):
+    nodes, hid = cotangent.shape
+    feat, feat_q = z_full.shape[0], z_part.shape[0]
+    flops = 2 * nodes * hid * (feat + feat_q) + 12 * nodes * hid
+    nbytes = 2 * (z_full.size + weight.size + cotangent.size + z_part.size + nodes * hid) + 4 * feat_q * hid
+    vmem = pl.BlockSpec(memory_space=pltpu.VMEM)
+    return pl.pallas_call(
+        tail_kernel,
+        out_shape=(
+            jax.ShapeDtypeStruct((nodes, hid), jnp.bfloat16),
+            jax.ShapeDtypeStruct((feat_q, hid), jnp.float32),
+        ),
+        in_specs=[vmem] * 4,
+        out_specs=(vmem, vmem),
+        cost_estimate=pl.CostEstimate(flops=flops, transcendentals=nodes * hid, bytes_accessed=nbytes),
+    )(z_full, weight, cotangent, z_part)
 
 
 def body(x_t, tiles, tile_owner, tile_local, weight, cotangent):
@@ -96,15 +126,7 @@
     z_sum = jnp.einsum("sfi,sb->fbi", terms, target_hot, precision=lax.Precision.HIGHEST)
     z_part = z_sum.reshape(feat_q, rows).astype(jnp.bfloat16)
     z_full = gather_groups(z_part, n_col)
-    y_full = lax.dot_general(
-        z_full, weight, (((0,), (0,)), ((), ())), preferred_element_type=jnp.float32
-    )
-    act = jax.nn.silu(y_full).astype(jnp.bfloat16)
-    sig = jax.nn.sigmoid(y_full)
-    grad_y = (cotangent.astype(jnp.float32) * sig * (1.0 + y_full * (1.0 - sig))).astype(
-        jnp.bfloat16
-    )
-    grad_part = jnp.dot(z_part, grad_y, preferred_element_type=jnp.float32)
+    act, grad_part = layer_tail(z_full, weight, cotangent, z_part)
     grad_w = sum_over_row(grad_part, n_row)
     return (act, grad_w)
 

time: 51.3 us -> 53.5 us (1.043)
  Pallas kernels: 0 us -> 2.57 us
  matrix products: 2.99 us -> 1.2 us
  local copies, waits for them, and re-layouts: 5.92 us -> 6.67 us
  other arithmetic: 2.74 us -> 3.46 us
    pallas_call x0 -> x1, Pallas kernels: none -> 2.57 us  [layer_tail(): pl.pallas_call(tail_kernel, out_shape=(jax.ShapeDtypeStruct((nodes, hid),...]
    dot_general x2 -> x0, matrix products: 1.79 us -> none  [the longest x1 1.27 us: body(): lax.dot_general(z_full, weight, (((0,), (0,)), ((), ())), preferred_eleme...]
    broadcast_in_dim x1, local copies, waits for them, and re-layouts: 0.02 us -> 0.78 us  [sum_over_row(): every = jnp.broadcast_to(x[None], (n_row,) + x.shape)]
    concatenate x0 -> x1, other arithmetic: none -> 0.71 us  [gather_groups(): return jnp.concatenate(groups, axis=0)]
where the time goes in v12:
time: 53.5 us; the launch traced here: 53.1 us
  waiting for transfers between devices  13.6 us (25%)
  starting transfers between devices  12.6 us (24%)
  blocking collectives  12.1 us (23%)
  local copies, waits for them, and re-layouts  6.67 us (12%)
  other arithmetic  3.46 us (6%)
  Pallas kernels  2.57 us (5%)
  matrix products  1.2 us (2%)
  between operations  0.83 us (2%)
    all_to_all x1, blocking collectives, sum_over_row(): lax.all_to_all(every, 'row', split_axis=0, concat_axis=0, tiled=True)  12.1 us
    all_to_all x1, starting transfers between devices, body(): lax.all_to_all(requests, 'row', split_axis=0, concat_axis=0, tiled=True)  7.28 us
    all_to_all x1, waiting for transfers between devices, body(): lax.all_to_all(payload, 'row', split_axis=0, concat_axis=0, tiled=True)  6.58 us
    ppermute x3, waiting for transfers between devices, gather_groups(): lax.ppermute(z_part, 'col', [(i, i ^ k) for i in range(n_col)])  3.74 us
    all_to_all x1, starting transfers between devices, body(): lax.all_to_all(payload, 'row', split_axis=0, concat_axis=0, tiled=True)  3.41 us
    all_to_all x1, waiting for transfers between devices, body(): lax.all_to_all(requests, 'row', split_axis=0, concat_axis=0, tiled=True)  3.26 us
    pallas_call x1, Pallas kernels, layer_tail(): pl.pallas_call(tail_kernel, out_shape=(jax.ShapeDtypeStruct((nodes, hid),...  2.57 us
    gather x4, local copies, waits for them, and re-layouts, rows_of(): return a.at[idx].get(mode='promise_in_bounds')  2.45 us
  transfers between devices with their start and end apart: 5, of which 4 were waited for; matrix products, arithmetic and copies ran while one was open for 9% of the time, Pallas kernels for 0%

profile of v12, /device:TPU:0, one launch (start us, length us, event | category | flops | bytes accessed | tf_op | source)
XLA Modules:
  0.0 53.1 jit_solution(6065187742278338212)
XLA Ops:
  0.6 0.0 copy-start
  0.6 0.8 %and_select_fusion.3 = (s32[8]{0:T(128)S(1)}, s32[8,1]{0,1:T(1,128)S(1)}) fusion(s32[8,2]{0,1:T(2,128)} %param.9, s32[8,1]{0,1:T(1,128)} %param.8), kind=kLoop, calls=%fused_computation.53 | loop fusion | flops 120 | bytes 160 | tf_op jit(solution)/shard_map/jit(remainder)/select_n | solution.py:86
  1.5 0.2 convert_reduce_fusion
  1.7 0.7 %select_reduce_fusion = s32[8,2,128]{2,1,0:T(2,128)} fusion(s32[8]{0:T(128)S(1)} %get-tuple-element.14, s32[8,2]{1,0:T(8,128)S(1)} %multiply_add_fusion, s32[8]{0:T(128)S(1)} %multiply_add_fusion.1), kind=kLoop, calls=%fused_computation.21 | loop fusion | flops 47104 | bytes 8320 | tf_op jit(solution)/shard_map/reduce_sum | solution.py:94
  2.4 7.3 %all-to-all-start = ((s32[8,2,128]{2,1,0:T(2,128)}), s32[8,2,128]{2,1,0:T(2,128)S(1)}, u32[]{:S(2)}, u32[]{:S(2)}) async-start(s32[8,2,128]{2,1,0:T(2,128)} %select_reduce_fusion), calls=%async_computation | async-start | bytes 16384 | tf_op jit(solution)/shard_map/all_to_all | solution.py:108
  9.7 0.1 select_reduce_fusion.1
  9.7 0.9 %bitcast_bitcast_fusion = bf16[8,32,128]{2,1,0:T(8,128)(2,1)S(1)} fusion(bf16[32,1024]{1,0:T(8,128)(2,1)} %param.6), kind=kLoop, calls=%fused_computation.16 | loop fusion | bytes 131072 | tf_op jit(solution)/shard_map/transpose | solution.py:81
  10.6 0.6 %gather_fusion.1 = bf16[8,32,128]{2,1,0:T(8,128)(2,1)S(1)} fusion(bf16[8,32,128]{2,1,0:T(8,128)(2,1)S(1)} %bitcast_bitcast_fusion, s32[1024]{0:T(1024)S(1)} %pad_clamp_fusion.1), kind=kCustom, calls=%fused_computation.1 | custom fusion | bytes 131104 | tf_op jit(solution)/shard_map/gather | solution.py:10
  11.2 0.0 copy-done
  11.2 0.2 convolution_convert_fusion.1
  11.4 0.7 %scatter_fusion = bf16[16,32,128]{2,1,0:T(8,128)(2,1)S(1)} fusion(bf16[16,32,128]{2,1,0:T(8,128)(2,1)S(1)} %broadcast.285, s32[8]{0:T(128)S(1)} %fusion.13, bf16[8,32,128]{2,1,0:T(8,128)(2,1)S(1)} %convolution_convert_fusion.1), kind=kCustom, calls=%fused_computation.4 | custom fusion | bytes 196640 | tf_op jit(solution)/shard_map/scatter | solution.py:103
  12.2 0.7 %copy.16 = bf16[8,2,2,32,128]{4,3,2,1,0:T(8,128)(2,1)} copy(bf16[8,2,2,32,128]{4,3,2,0,1:T(8,128)(2,1)S(1)} %bitcast.78) | data formatting | bytes 524288 | tf_op jit(solution)/shard_map/transpose | solution.py:106
  12.9 3.3 %all-to-all-done = s32[8,2,128]{2,1,0:T(2,128)S(1)} async-done(((s32[8,2,128]{2,1,0:T(2,128)}), s32[8,2,128]{2,1,0:T(2,128)S(1)}, u32[]{:S(2)}, u32[]{:S(2)}) %all-to-all-start) | async-done | bytes 8224 | tf_op jit(solution)/shard_map/all_to_all | solution.py:108
  16.2 0.2 slice_reduce_fusion
  16.4 0.1 reshape_squeeze.7
  16.5 0.6 %gather_fusion.2 = bf16[16,32,128]{2,1,0:T(8,128)(2,1)S(1)} fusion(bf16[8,32,128]{2,1,0:T(8,128)(2,1)S(1)} %bitcast_bitcast_fusion, s32[1024]{0:T(1024)S(1)} %pad_clamp_fusion), kind=kCustom, calls=%fused_computation.2 | custom fusion | bytes 262208 | tf_op jit(solution)/shard_map/gather | solution.py:10
  17.1 0.7 %constant_dynamic-update-slice_fusion = bf16[8,4,32,128]{3,2,1,0:T(8,128)(2,1)} fusion(bf16[8,4,32,128]{3,2,1,0:T(8,128)(2,1)} %bitcast.11, bf16[8,2,32,128]{3,2,1,0:T(8,128)(2,1)S(1)} %bitcast.82), kind=kLoop, calls=%fused_computation.77 | loop fusion | bytes 262144 | tf_op jit(solution)/shard_map/dynamic_update_slice | solution.py:111
  17.7 3.4 %all-to-all-start.1 = ((bf16[8,4,32,128]{3,2,1,0:T(8,128)(2,1)}), bf16[8,4,32,128]{3,2,1,0:T(8,128)(2,1)S(1)}, u32[]{:S(2)}, u32[]{:S(2)}) async-start(bf16[8,4,32,128]{3,2,1,0:T(8,128)(2,1)} %constant_dynamic-update-slice_fusion), calls=%async_computation.1 | async-start | bytes 524288 | tf_op jit(solution)/shard_map/all_to_all | solution.py:112
  21.2 0.6 %gather_fusion.3 = bf16[16,128,128]{2,1,0:T(8,128)(2,1)S(1)} fusion(bf16[8,128,128]{2,1,0:T(8,128)(2,1)S(1)} %copy-done, s32[1024]{0:T(1024)S(1)} %pad_clamp_fusion.2), kind=kCustom, calls=%fused_computation.3 | custom fusion | bytes 1048640 | tf_op jit(solution)/shard_map/gather | solution.py:10
  21.8 0.7 %gather_fusion = s32[16]{0:T(128)S(1)} fusion(s32[8]{0:T(128)S(1)} %get-tuple-element.6, s32[1024]{0:T(1024)S(1)} %pad_clamp_fusion.2), kind=kCustom, calls=%fused_computation | custom fusion | bytes 192 | tf_op jit(solution)/shard_map/gather | solution.py:10
  22.5 0.1 fusion.6
  22.6 0.1 reshape_squeeze.6
  22.7 0.1 pad_add_fusion
  22.8 6.6 %all-to-all-done.1 = bf16[8,4,32,128]{3,2,1,0:T(8,128)(2,1)S(1)} async-done(((bf16[8,4,32,128]{3,2,1,0:T(8,128)(2,1)}), bf16[8,4,32,128]{3,2,1,0:T(8,128)(2,1)S(1)}, u32[]{:S(2)}, u32[]{:S(2)}) %all-to-all-start.1) | async-done | bytes 262176 | tf_op jit(solution)/shard_map/all_to_all | solution.py:112
  29.4 0.4 fusion.1
  29.9 0.6 %convolution_convert_fusion = bf16[8,32,128]{2,0,1:T(8,128)(2,1)S(1)} fusion(f32[32,32,128]{2,1,0:T(8,128)S(1)} %pad_maximum_fusion, s32[32]{0:T(128)S(1)} %pad_add_fusion), kind=kOutput, calls=%fused_computation.5 | convolution fusion | flops 12615936 | bytes 589952 | tf_op jit(solution)/shard_map/sfi,sb->fbi/dot_general | solution.py:126
  30.5 0.0 copy-start.1
  30.5 0.1 collective-permute-start
  30.6 1.6 %collective-permute-start.1 = (bf16[32,1024]{1,0:T(8,128)(2,1)S(1)}, bf16[32,1024]{1,0:T(8,128)(2,1)S(1)}, u32[]{:S(2)}, u32[]{:S(2)}) collective-permute-start(bf16[32,1024]{1,0:T(8,128)(2,1)S(1)} %bitcast.84), channel_id=1, source_target_pairs={{0,2},{1,3},{2,0},{3,1},{4,6},{5,7},{6,4},{7,5},{8,10},{9,11},{10,... | collective-permute-start | bytes 196616 | tf_op jit(solution)/shard_map/ppermute | solution.py:27
  32.1 0.3 collective-permute-start.2
  32.4 0.0 collective-permute-done
  32.5 2.6 %collective-permute-done.1 = bf16[32,1024]{1,0:T(8,128)(2,1)S(1)} collective-permute-done((bf16[32,1024]{1,0:T(8,128)(2,1)S(1)}, bf16[32,1024]{1,0:T(8,128)(2,1)S(1)}, u32[]{:S(2)}, u32[]{:S(2)}) %collective-permute-start.1) | collective-permute-done | bytes 65568 | tf_op jit(solution)/shard_map/ppermute | solution.py:27
  35.1 1.1 %collective-permute-done.2 = bf16[32,1024]{1,0:T(8,128)(2,1)S(1)} collective-permute-done((bf16[32,1024]{1,0:T(8,128)(2,1)S(1)}, bf16[32,1024]{1,0:T(8,128)(2,1)S(1)}, u32[]{:S(2)}, u32[]{:S(2)}) %collective-permute-start.2) | collective-permute-done | bytes 65568 | tf_op jit(solution)/shard_map/ppermute | solution.py:27
  36.2 0.0 copy-done.1
  36.2 0.7 %pad_maximum_fusion.1.z_full_ref = bf16[128,1024]{1,0:T(8,128)(2,1)} fusion(bf16[32,1024]{1,0:T(8,128)(2,1)S(1)} %get-tuple-element.9, bf16[32,1024]{1,0:T(8,128)(2,1)S(1)} %get-tuple-element.10, bf16[32,1024]{1,0:T(8,128)(2,1)S(1)} %get-tuple-element.11, bf16[32,1024]{1,0:T(8,128)(2,1)S(1)} %get-tuple-element.8), kind=kLoop, calls=%fused_computation.12 | loop fusion | flops 1048576 | bytes 524288 | tf_op jit(solution)/shard_map/concatenate | solution.py:34
  37.0 2.6 %shard_map.77 = (bf16[1024,256]{1,0:T(8,128)(2,1)}, f32[32,256]{1,0:T(8,128)}) custom-call(bf16[128,1024]{1,0:T(8,128)(2,1)} %pad_maximum_fusion.1.z_full_ref, bf16[128,256]{1,0:T(8,128)(2,1)} %w_ref.1, bf16[1024,256]{1,0:T(8,128)(2,1)} %cot_ref.1, bf16[32,1024]{1,0:T(8,128)(2,1)} %bitcast.86), custom_call_target="tpu_custom_call" | custom-call | flops 87031808 | bytes 1474560 | tf_op jit(solution)/shard_map/pallas_call | solution.py:62
  39.5 0.8 %broadcast_in_dim.70 = f32[8,32,256]{2,1,0:T(8,128)S(1)} broadcast(f32[32,256]{1,0:T(8,128)} %get-tuple-element.5), dimensions={1,2} | broadcast | bytes 294912 | tf_op jit(solution)/shard_map/broadcast_in_dim | solution.py:38
  40.3 12.1 %all_to_all.15 = f32[8,32,256]{2,1,0:T(8,128)S(1)} all-to-all(f32[8,32,256]{2,1,0:T(8,128)S(1)} %broadcast_in_dim.70), channel_id=1, replica_groups=mesh['row'=8,'col'=4] {'row'}, dimensions={0} | all-to-all | bytes 524288 | tf_op jit(solution)/shard_map/all_to_all | solution.py:39
  52.5 0.6 %fusion.5 = f32[32,256]{1,0:T(8,128)} fusion(f32[8,32,256]{2,1,0:T(8,128)S(1)} %all_to_all.15), kind=kLoop, calls=%fused_computation.23 | loop fusion | flops 57344 | bytes 294912 | tf_op jit(solution)/shard_map/add | solution.py:42
  (18 shorter events, 0.3 us)
Async XLA Ops:
  0.6 10.6 %copy-start = (bf16[8,128,128]{2,1,0:T(8,128)(2,1)S(1)}, bf16[8,128,128]{2,1,0:T(8,128)(2,1)}, u32[]{:S(2)}) copy-start(bf16[8,128,128]{2,1,0:T(8,128)(2,1)} %param.7) | copy-start | bytes 786436
  2.4 13.8 %all-to-all-start = ((s32[8,2,128]{2,1,0:T(2,128)}), s32[8,2,128]{2,1,0:T(2,128)S(1)}, u32[]{:S(2)}, u32[]{:S(2)}) async-start(s32[8,2,128]{2,1,0:T(2,128)} %select_reduce_fusion), calls=%async_computation | async-start | bytes 16384 | tf_op jit(solution)/shard_map/all_to_all | solution.py:108
  17.7 11.6 %all-to-all-start.1 = ((bf16[8,4,32,128]{3,2,1,0:T(8,128)(2,1)}), bf16[8,4,32,128]{3,2,1,0:T(8,128)(2,1)S(1)}, u32[]{:S(2)}, u32[]{:S(2)}) async-start(bf16[8,4,32,128]{3,2,1,0:T(8,128)(2,1)} %constant_dynamic-update-slice_fusion), calls=%async_computation.1 | async-start | bytes 524288 | tf_op jit(solution)/shard_map/all_to_all | solution.py:112
  30.5 5.7 %copy-start.1 = (bf16[4,8,8,128]{3,1,2,0:T(8,128)(2,1)}, bf16[4,8,8,128]{3,1,2,0:T(8,128)(2,1)S(1)}, u32[]{:S(2)}) copy-start(bf16[4,8,8,128]{3,1,2,0:T(8,128)(2,1)S(1)} %copy.32) | copy-start | bytes 196612
  30.5 1.9 %collective-permute-start = (bf16[32,1024]{1,0:T(8,128)(2,1)S(1)}, bf16[32,1024]{1,0:T(8,128)(2,1)S(1)}, u32[]{:S(2)}, u32[]{:S(2)}) collective-permute-start(bf16[32,1024]{1,0:T(8,128)(2,1)S(1)} %bitcast.83), channel_id=1, source_target_pairs={{0,1},{1,0},{2,3},{3,2},{4,5},{5,4},{6,7},{7,6},{8,9},{9,8},{10,11... | collective-permute-start | bytes 196616 | tf_op jit(solution)/shard_map/ppermute | solution.py:27
  30.6 4.5 %collective-permute-start.1 = (bf16[32,1024]{1,0:T(8,128)(2,1)S(1)}, bf16[32,1024]{1,0:T(8,128)(2,1)S(1)}, u32[]{:S(2)}, u32[]{:S(2)}) collective-permute-start(bf16[32,1024]{1,0:T(8,128)(2,1)S(1)} %bitcast.84), channel_id=1, source_target_pairs={{0,2},{1,3},{2,0},{3,1},{4,6},{5,7},{6,4},{7,5},{8,10},{9,11},{10,... | collective-permute-start | bytes 196616 | tf_op jit(solution)/shard_map/ppermute | solution.py:27
  32.1 4.0 %collective-permute-start.2 = (bf16[32,1024]{1,0:T(8,128)(2,1)S(1)}, bf16[32,1024]{1,0:T(8,128)(2,1)S(1)}, u32[]{:S(2)}, u32[]{:S(2)}) collective-permute-start(bf16[32,1024]{1,0:T(8,128)(2,1)S(1)} %bitcast.85), channel_id=1, source_target_pairs={{0,3},{1,2},{2,1},{3,0},{4,7},{5,6},{6,5},{7,4},{8,11},{9,10},{10,... | collective-permute-start | bytes 196616 | tf_op jit(solution)/shard_map/ppermute | solution.py:27

commit v13 on v10

--- a/solution.py
+++ b/solution.py
@@ -20,9 +20,15 @@
         order = (me - jnp.arange(n_col, dtype=jnp.int32)) % n_col
         full = rows_of(jnp.stack(parts), order)
         return full.reshape(n_col * z_part.shape[0], z_part.shape[1])
-    parts = [z_part]
-    for k in range(1, n_col):
-        parts.append(lax.ppermute(z_part, "col", [(i, i ^ k) for i in range(n_col)]))
+    if n_col == 4:
+        across = lax.ppermute(z_part, "col", [(i, i ^ 2) for i in range(n_col)])
+        beside = lax.ppermute(z_part, "col", [(i, i ^ 1) for i in range(n_col)])
+        corner = lax.ppermute(across, "col", [(i, i ^ 1) for i in range(n_col)])
+        parts = [z_part, beside, across, corner]
+    else:
+        parts = [z_part]
+        for k in range(1, n_col):
+            parts.append(lax.ppermute(z_part, "col", [(i, i ^ k) for i in range(n_col)]))
     groups = []
     for j in range(n_col):
         pick = parts[n_col - 1]

time: 51.3 us -> 51.1 us (level)
  no operation moved by 1% of the time
where the time goes in v13:
time: 51.1 us; the launch traced here: 50.7 us
  waiting for transfers between devices  13.9 us (27%)
  starting transfers between devices  12.3 us (24%)
  blocking collectives  12.1 us (24%)
  local copies, waits for them, and re-layouts  5.92 us (12%)
  matrix products  2.99 us (6%)
  other arithmetic  2.74 us (5%)
  between operations  0.83 us (2%)
    all_to_all x1, blocking collectives, sum_over_row(): lax.all_to_all(every, 'row', split_axis=0, concat_axis=0, tiled=True)  12.1 us
    all_to_all x1, starting transfers between devices, body(): lax.all_to_all(requests, 'row', split_axis=0, concat_axis=0, tiled=True)  7.28 us
    all_to_all x1, waiting for transfers between devices, body(): lax.all_to_all(payload, 'row', split_axis=0, concat_axis=0, tiled=True)  6.58 us
    all_to_all x1, starting transfers between devices, body(): lax.all_to_all(payload, 'row', split_axis=0, concat_axis=0, tiled=True)  3.41 us
    all_to_all x1, waiting for transfers between devices, body(): lax.all_to_all(requests, 'row', split_axis=0, concat_axis=0, tiled=True)  3.27 us
    ppermute x1, waiting for transfers between devices, gather_groups(): across = lax.ppermute(z_part, 'col', [(i, i ^ 2) for i in range(n_col)])  2.77 us
    gather x4, local copies, waits for them, and re-layouts, rows_of(): return a.at[idx].get(mode='promise_in_bounds')  2.45 us
    ppermute x1, starting transfers between devices, gather_groups(): across = lax.ppermute(z_part, 'col', [(i, i ^ 2) for i in range(n_col)])  1.56 us
  transfers between devices with their start and end apart: 5, of which 4 were waited for; matrix products, arithmetic and copies ran while one was open for 9% of the time, Pallas kernels for 0%

profile of v13, /device:TPU:0, one launch (start us, length us, event | category | flops | bytes accessed | tf_op | source)
XLA Modules:
  0.0 50.7 jit_solution(801939434981657362)
XLA Ops:
  0.6 0.0 copy-start
  0.6 0.8 %and_select_fusion.3 = (s32[8]{0:T(128)S(1)}, s32[8,1]{0,1:T(1,128)S(1)}) fusion(s32[8,2]{0,1:T(2,128)} %param.9, s32[8,1]{0,1:T(1,128)} %param.8), kind=kLoop, calls=%fused_computation.64 | loop fusion | flops 120 | bytes 160 | tf_op jit(solution)/shard_map/jit(remainder)/select_n | solution.py:62
  1.5 0.2 convert_reduce_fusion
  1.7 0.7 %select_reduce_fusion = s32[8,2,128]{2,1,0:T(2,128)} fusion(s32[8]{0:T(128)S(1)} %get-tuple-element.10, s32[8,2]{1,0:T(8,128)S(1)} %multiply_add_fusion, s32[8]{0:T(128)S(1)} %multiply_add_fusion.1), kind=kLoop, calls=%fused_computation.32 | loop fusion | flops 47104 | bytes 8320 | tf_op jit(solution)/shard_map/reduce_sum | solution.py:70
  2.4 7.3 %all-to-all-start = ((s32[8,2,128]{2,1,0:T(2,128)}), s32[8,2,128]{2,1,0:T(2,128)S(1)}, u32[]{:S(2)}, u32[]{:S(2)}) async-start(s32[8,2,128]{2,1,0:T(2,128)} %select_reduce_fusion), calls=%async_computation | async-start | bytes 16384 | tf_op jit(solution)/shard_map/all_to_all | solution.py:84
  9.7 0.1 select_reduce_fusion.1
  9.8 0.9 %bitcast_bitcast_fusion = bf16[8,32,128]{2,1,0:T(8,128)(2,1)S(1)} fusion(bf16[32,1024]{1,0:T(8,128)(2,1)} %param.6), kind=kLoop, calls=%fused_computation.27 | loop fusion | bytes 131072 | tf_op jit(solution)/shard_map/transpose | solution.py:57
  10.6 0.6 %gather_fusion.1 = bf16[8,32,128]{2,1,0:T(8,128)(2,1)S(1)} fusion(bf16[8,32,128]{2,1,0:T(8,128)(2,1)S(1)} %bitcast_bitcast_fusion, s32[1024]{0:T(1024)S(1)} %pad_clamp_fusion.1), kind=kCustom, calls=%fused_computation.1 | custom fusion | bytes 131104 | tf_op jit(solution)/shard_map/gather | solution.py:8
  11.2 0.0 copy-done
  11.2 0.2 convolution_convert_fusion.1
  11.4 0.7 %scatter_fusion = bf16[16,32,128]{2,1,0:T(8,128)(2,1)S(1)} fusion(bf16[16,32,128]{2,1,0:T(8,128)(2,1)S(1)} %broadcast.288, s32[8]{0:T(128)S(1)} %fusion.22, bf16[8,32,128]{2,1,0:T(8,128)(2,1)S(1)} %convolution_convert_fusion.1), kind=kCustom, calls=%fused_computation.4 | custom fusion | bytes 196640 | tf_op jit(solution)/shard_map/scatter | solution.py:79
  12.2 0.7 %copy.16 = bf16[8,2,2,32,128]{4,3,2,1,0:T(8,128)(2,1)} copy(bf16[8,2,2,32,128]{4,3,2,0,1:T(8,128)(2,1)S(1)} %bitcast.81) | data formatting | bytes 524288 | tf_op jit(solution)/shard_map/transpose | solution.py:82
  12.9 3.3 %all-to-all-done = s32[8,2,128]{2,1,0:T(2,128)S(1)} async-done(((s32[8,2,128]{2,1,0:T(2,128)}), s32[8,2,128]{2,1,0:T(2,128)S(1)}, u32[]{:S(2)}, u32[]{:S(2)}) %all-to-all-start) | async-done | bytes 8224 | tf_op jit(solution)/shard_map/all_to_all | solution.py:84
  16.2 0.2 slice_reduce_fusion
  16.4 0.1 reshape_squeeze.7
  16.5 0.6 %gather_fusion.2 = bf16[16,32,128]{2,1,0:T(8,128)(2,1)S(1)} fusion(bf16[8,32,128]{2,1,0:T(8,128)(2,1)S(1)} %bitcast_bitcast_fusion, s32[1024]{0:T(1024)S(1)} %pad_clamp_fusion), kind=kCustom, calls=%fused_computation.2 | custom fusion | bytes 262208 | tf_op jit(solution)/shard_map/gather | solution.py:8
  17.1 0.7 %constant_dynamic-update-slice_fusion = bf16[8,4,32,128]{3,2,1,0:T(8,128)(2,1)} fusion(bf16[8,4,32,128]{3,2,1,0:T(8,128)(2,1)} %bitcast.11, bf16[8,2,32,128]{3,2,1,0:T(8,128)(2,1)S(1)} %bitcast.86), kind=kLoop, calls=%fused_computation.88 | loop fusion | bytes 262144 | tf_op jit(solution)/shard_map/dynamic_update_slice | solution.py:87
  17.7 3.4 %all-to-all-start.1 = ((bf16[8,4,32,128]{3,2,1,0:T(8,128)(2,1)}), bf16[8,4,32,128]{3,2,1,0:T(8,128)(2,1)S(1)}, u32[]{:S(2)}, u32[]{:S(2)}) async-start(bf16[8,4,32,128]{3,2,1,0:T(8,128)(2,1)} %constant_dynamic-update-slice_fusion), calls=%async_computation.1 | async-start | bytes 524288 | tf_op jit(solution)/shard_map/all_to_all | solution.py:88
  21.2 0.6 %gather_fusion.3 = bf16[16,128,128]{2,1,0:T(8,128)(2,1)S(1)} fusion(bf16[8,128,128]{2,1,0:T(8,128)(2,1)S(1)} %copy-done, s32[1024]{0:T(1024)S(1)} %pad_clamp_fusion.2), kind=kCustom, calls=%fused_computation.3 | custom fusion | bytes 1048640 | tf_op jit(solution)/shard_map/gather | solution.py:8
  21.8 0.7 %gather_fusion = s32[16]{0:T(128)S(1)} fusion(s32[8]{0:T(128)S(1)} %get-tuple-element.2, s32[1024]{0:T(1024)S(1)} %pad_clamp_fusion.2), kind=kCustom, calls=%fused_computation | custom fusion | bytes 192 | tf_op jit(solution)/shard_map/gather | solution.py:8
  22.5 0.1 fusion.15
  22.6 0.1 reshape_squeeze.6
  22.7 0.1 pad_add_fusion
  22.8 6.6 %all-to-all-done.1 = bf16[8,4,32,128]{3,2,1,0:T(8,128)(2,1)S(1)} async-done(((bf16[8,4,32,128]{3,2,1,0:T(8,128)(2,1)}), bf16[8,4,32,128]{3,2,1,0:T(8,128)(2,1)S(1)}, u32[]{:S(2)}, u32[]{:S(2)}) %all-to-all-start.1) | async-done | bytes 262176 | tf_op jit(solution)/shard_map/all_to_all | solution.py:88
  29.4 0.4 fusion.1
  29.9 0.6 %convolution_convert_fusion = bf16[8,32,128]{2,0,1:T(8,128)(2,1)S(1)} fusion(f32[32,32,128]{2,1,0:T(8,128)S(1)} %pad_maximum_fusion, s32[32]{0:T(128)S(1)} %pad_add_fusion), kind=kOutput, calls=%fused_computation.5 | convolution fusion | flops 12615936 | bytes 589952 | tf_op jit(solution)/shard_map/sfi,sb->fbi/dot_general | solution.py:102
  30.5 1.6 %collective-permute-start.1 = (bf16[32,1024]{1,0:T(8,128)(2,1)S(1)}, bf16[32,1024]{1,0:T(8,128)(2,1)S(1)}, u32[]{:S(2)}, u32[]{:S(2)}) collective-permute-start(bf16[32,1024]{1,0:T(8,128)(2,1)S(1)} %bitcast.87), channel_id=1, source_target_pairs={{0,2},{1,3},{2,0},{3,1},{4,6},{5,7},{6,4},{7,5},{8,10},{9,11},{10,... | collective-permute-start | bytes 196616 | tf_op jit(solution)/shard_map/ppermute | solution.py:24
  32.1 0.0 collective-permute-start
  32.1 2.8 %collective-permute-done.1 = bf16[32,1024]{1,0:T(8,128)(2,1)S(1)} collective-permute-done((bf16[32,1024]{1,0:T(8,128)(2,1)S(1)}, bf16[32,1024]{1,0:T(8,128)(2,1)S(1)}, u32[]{:S(2)}, u32[]{:S(2)}) %collective-permute-start.1) | collective-permute-done | bytes 65568 | tf_op jit(solution)/shard_map/ppermute | solution.py:24
  34.8 0.0 collective-permute-start.2
  34.8 0.0 copy-start.2
  34.8 0.0 collective-permute-done
  34.8 1.2 %collective-permute-done.2 = bf16[32,1024]{1,0:T(8,128)(2,1)S(1)} collective-permute-done((bf16[32,1024]{1,0:T(8,128)(2,1)S(1)}, bf16[32,1024]{1,0:T(8,128)(2,1)S(1)}, u32[]{:S(2)}, u32[]{:S(2)}) %collective-permute-start.2) | collective-permute-done | bytes 65568 | tf_op jit(solution)/shard_map/ppermute | solution.py:26
  36.1 0.0 copy-done.2
  36.1 0.0 copy-start.1
  36.1 1.3 %multiply_convert_fusion.1 = (bf16[1024,256]{1,0:T(8,128)(2,1)}, f32[1024,256]{1,0:T(8,128)S(1)}) fusion(bf16[128,256]{1,0:T(8,128)(2,1)S(1)} %copy-done.2, bf16[32,1024]{1,0:T(8,128)(2,1)S(1)} %get-tuple-element.5, bf16[32,1024]{1,0:T(8,128)(2,1)S(1)} %get-tuple-element.6, bf16[32,1024]{1,0:T(8,128)(2,1)S(1)} %get-tuple-element.7, ...), kind=kOutput, calls=%fused_computation.8 | convolution fusion | flops 69468160 | bytes 1900544 | tf_op jit(solution)/shard_map/dot_general | solution.py:105
  37.4 0.0 copy-done.1
  37.4 0.5 %fusion.4 = f32[32,256]{1,0:T(8,128)S(1)} fusion(f32[1024,256]{1,0:T(8,128)S(1)} %get-tuple-element.15, bf16[1024,256]{1,0:T(8,128)(2,1)S(1)} %copy-done.1, bf16[4,8,8,128]{3,2,1,0:T(8,128)(2,1)S(1)} %bitcast.84), kind=kOutput, calls=%fused_computation.15 | convolution fusion | flops 19398656 | bytes 1671168 | tf_op jit(solution)/shard_map/dot_general | solution.py:113
  38.0 12.1 %all_to_all.15 = f32[8,32,256]{2,1,0:T(8,128)S(1)} all-to-all(f32[8,32,256]{2,1,0:T(8,128)S(1)} %broadcast_in_dim.70), channel_id=1, replica_groups=mesh['row'=8,'col'=4] {'row'}, dimensions={0} | all-to-all | bytes 524288 | tf_op jit(solution)/shard_map/all_to_all | solution.py:43
  50.1 0.6 %fusion.14 = f32[32,256]{1,0:T(8,128)} fusion(f32[8,32,256]{2,1,0:T(8,128)S(1)} %all_to_all.15), kind=kLoop, calls=%fused_computation.34 | loop fusion | flops 57344 | bytes 294912 | tf_op jit(solution)/shard_map/add | solution.py:46
  (19 shorter events, 0.3 us)
Async XLA Ops:
  0.6 10.5 %copy-start = (bf16[8,128,128]{2,1,0:T(8,128)(2,1)S(1)}, bf16[8,128,128]{2,1,0:T(8,128)(2,1)}, u32[]{:S(2)}) copy-start(bf16[8,128,128]{2,1,0:T(8,128)(2,1)} %param.7) | copy-start | bytes 786436
  2.4 13.8 %all-to-all-start = ((s32[8,2,128]{2,1,0:T(2,128)}), s32[8,2,128]{2,1,0:T(2,128)S(1)}, u32[]{:S(2)}, u32[]{:S(2)}) async-start(s32[8,2,128]{2,1,0:T(2,128)} %select_reduce_fusion), calls=%async_computation | async-start | bytes 16384 | tf_op jit(solution)/shard_map/all_to_all | solution.py:84
  17.7 11.6 %all-to-all-start.1 = ((bf16[8,4,32,128]{3,2,1,0:T(8,128)(2,1)}), bf16[8,4,32,128]{3,2,1,0:T(8,128)(2,1)S(1)}, u32[]{:S(2)}, u32[]{:S(2)}) async-start(bf16[8,4,32,128]{3,2,1,0:T(8,128)(2,1)} %constant_dynamic-update-slice_fusion), calls=%async_computation.1 | async-start | bytes 524288 | tf_op jit(solution)/shard_map/all_to_all | solution.py:88
  30.5 4.3 %collective-permute-start.1 = (bf16[32,1024]{1,0:T(8,128)(2,1)S(1)}, bf16[32,1024]{1,0:T(8,128)(2,1)S(1)}, u32[]{:S(2)}, u32[]{:S(2)}) collective-permute-start(bf16[32,1024]{1,0:T(8,128)(2,1)S(1)} %bitcast.87), channel_id=1, source_target_pairs={{0,2},{1,3},{2,0},{3,1},{4,6},{5,7},{6,4},{7,5},{8,10},{9,11},{10,... | collective-permute-start | bytes 196616 | tf_op jit(solution)/shard_map/ppermute | solution.py:24
  32.1 2.8 %collective-permute-start = (bf16[32,1024]{1,0:T(8,128)(2,1)S(1)}, bf16[32,1024]{1,0:T(8,128)(2,1)S(1)}, u32[]{:S(2)}, u32[]{:S(2)}) collective-permute-start(bf16[32,1024]{1,0:T(8,128)(2,1)S(1)} %bitcast.88), channel_id=1, source_target_pairs={{0,1},{1,0},{2,3},{3,2},{4,5},{5,4},{6,7},{7,6},{8,9},{9,8},{10,11... | collective-permute-start | bytes 196616 | tf_op jit(solution)/shard_map/ppermute | solution.py:25
  34.8 1.3 %collective-permute-start.2 = (bf16[32,1024]{1,0:T(8,128)(2,1)S(1)}, bf16[32,1024]{1,0:T(8,128)(2,1)S(1)}, u32[]{:S(2)}, u32[]{:S(2)}) collective-permute-start(bf16[32,1024]{1,0:T(8,128)(2,1)S(1)} %collective-permute-done.1), channel_id=1, source_target_pairs={{0,1},{1,0},{2,3},{3,2},{4,5},{5,4},{6,7},{7,6},{8,9},{9,8},{10,11... | collective-permute-start | bytes 196616 | tf_op jit(solution)/shard_map/ppermute | solution.py:26
  34.8 1.3 %copy-start.2 = (bf16[128,256]{1,0:T(8,128)(2,1)S(1)}, bf16[128,256]{1,0:T(8,128)(2,1)}, u32[]{:S(2)}) copy-start(bf16[128,256]{1,0:T(8,128)(2,1)} %param.10) | copy-start | bytes 196612
  36.1 1.3 %copy-start.1 = (bf16[1024,256]{1,0:T(8,128)(2,1)S(1)}, bf16[1024,256]{1,0:T(8,128)(2,1)}, u32[]{:S(2)}) copy-start(bf16[1024,256]{1,0:T(8,128)(2,1)} %param.11) | copy-start | bytes 1572868

commit v14 on v13

--- a/solution.py
+++ b/solution.py
@@ -66,11 +66,14 @@
     slot = owner * capacity + rank
     slot_range = jnp.arange(n_row * capacity, dtype=jnp.int32)
     slot_hot = slot[None, :] == slot_range[:, None]
-    lane_slots = jnp.broadcast_to(slot_range.reshape(n_row, capacity, 1), (n_row, capacity, 128))
-    requests = jnp.sum(
-        jnp.where(slot[None, None, None, :] == lane_slots[..., None], col_local[None, None, None, :], 0),
-        axis=-1,
-    )
+    pad_rows = 8
+    row_slot = jnp.arange(n_row * pad_rows, dtype=jnp.int32)
+    row_slot = (row_slot // pad_rows) * capacity + row_slot % pad_rows
+    row_used = (jnp.arange(n_row * pad_rows, dtype=jnp.int32) % pad_rows) < capacity
+    pick_hot = ((slot[None, :] == row_slot[:, None]) & row_used[:, None]).astype(jnp.bfloat16)
+    lane_local = jnp.broadcast_to(col_local[:, None], (n_tiles, 128)).astype(jnp.bfloat16)
+    requests = jnp.dot(pick_hot, lane_local, preferred_element_type=jnp.float32).astype(jnp.int32)
+    requests = requests.reshape(n_row, pad_rows, 128)
     own_blocks = rows_of(xb, row_local)
     mirror_terms = jnp.einsum(
         "tfi,tij->tfj", own_blocks, tiles, preferred_element_type=jnp.float32
@@ -82,7 +85,7 @@
     ).reshape(2, n_row, capacity, feat_q, tile_dim).transpose(1, 0, 2, 3, 4)
     base = base.reshape(n_row, 2 * capacity, feat_q, tile_dim)
     got_ids = lax.all_to_all(requests, "row", split_axis=0, concat_axis=0, tiled=True)
-    block_ids = got_ids[:, :, 0]
+    block_ids = got_ids[:, :capacity, 0]
     asked = rows_of(xb, block_ids.reshape(-1)).reshape(n_row, capacity, feat_q, tile_dim)
     payload = lax.dynamic_update_slice(base, asked, (0, 0, 0, 0))
     both = lax.all_to_all(payload, "row", split_axis=0, concat_axis=0, tiled=True)

time: 51.1 us -> 51.5 us (level)
  other arithmetic: 2.74 us -> 1.29 us
  waiting for transfers between devices: 13.9 us -> 14.9 us
  matrix products: 2.99 us -> 3.81 us
    all_to_all x1, waiting for transfers between devices: 3.27 us -> 4.27 us  [body(): lax.all_to_all(requests, 'row', split_axis=0, concat_axis=0, tiled=True)]
    transpose x1, local copies, waits for them, and re-layouts: 0.85 us -> 0.01 us  [body(): xb = x_t.reshape(feat_q, n_blocks, tile_dim).transpose(1, 0, 2)]
    dot_general x0 -> x1, matrix products: none -> 0.82 us  [body(): jnp.dot(pick_hot, lane_local, preferred_element_type=jnp.float32)]
    select_n x1, other arithmetic: 0.77 us -> 0.01 us  [body(): row_local = key % n_blocks]
    reduce_sum x1 -> x0, other arithmetic: 0.71 us -> none  [body(): jnp.sum(jnp.where(slot[None, None, None, :] == lane_slots[..., None], col...]
    unnamed x7 -> x13, local copies, waits for them, and re-layouts: 0.03 us -> 0.73 us
  transfers between devices with their start and end apart: 5 -> 5, of which waited for: 4 -> 4; matrix products, arithmetic and copies ran while one was open for 9% -> 8% of each run, Pallas kernels for 0% -> 0%
where the time goes in v14:
time: 51.5 us; the launch traced here: 51.1 us
  waiting for transfers between devices  14.9 us (29%)
  starting transfers between devices  12.4 us (24%)
  blocking collectives  12.1 us (23%)
  local copies, waits for them, and re-layouts  5.78 us (11%)
  matrix products  3.81 us (7%)
  other arithmetic  1.29 us (3%)
  between operations  0.86 us (2%)
    all_to_all x1, blocking collectives, sum_over_row(): lax.all_to_all(every, 'row', split_axis=0, concat_axis=0, tiled=True)  12.1 us
    all_to_all x1, starting transfers between devices, body(): lax.all_to_all(requests, 'row', split_axis=0, concat_axis=0, tiled=True)  7.41 us
    all_to_all x1, waiting for transfers between devices, body(): lax.all_to_all(payload, 'row', split_axis=0, concat_axis=0, tiled=True)  6.58 us
    all_to_all x1, waiting for transfers between devices, body(): lax.all_to_all(requests, 'row', split_axis=0, concat_axis=0, tiled=True)  4.27 us
    all_to_all x1, starting transfers between devices, body(): lax.all_to_all(payload, 'row', split_axis=0, concat_axis=0, tiled=True)  3.41 us
    ppermute x1, waiting for transfers between devices, gather_groups(): across = lax.ppermute(z_part, 'col', [(i, i ^ 2) for i in range(n_col)])  2.77 us
    gather x4, local copies, waits for them, and re-layouts, rows_of(): return a.at[idx].get(mode='promise_in_bounds')  2.45 us
    ppermute x1, starting transfers between devices, gather_groups(): across = lax.ppermute(z_part, 'col', [(i, i ^ 2) for i in range(n_col)])  1.56 us
  transfers between devices with their start and end apart: 5, of which 4 were waited for; matrix products, arithmetic and copies ran while one was open for 8% of the time, Pallas kernels for 0%

profile of v14, /device:TPU:0, one launch (start us, length us, event | category | flops | bytes accessed | tf_op | source)
XLA Modules:
  0.0 51.1 jit_solution(8193123010046605685)
XLA Ops:
  0.6 0.0 copy-start
  0.7 0.0 copy-start.2
  0.7 0.0 copy-start.3
  0.7 0.7 %copy-done.2 = s32[8,2]{0,1:T(2,128)S(1)} copy-done((s32[8,2]{0,1:T(2,128)S(1)}, s32[8,2]{0,1:T(2,128)}, u32[]{:S(2)}) %copy-start.2) | copy-done | bytes 88
  1.4 0.0 copy-done.3
  1.4 0.2 convert_reduce_fusion
  1.6 0.8 %fusion = s32[8,8,128]{2,1,0:T(8,128)} fusion(s32[8]{0:T(128)S(1)} %multiply_add_fusion, s32[64]{0:T(128)S(1)} %fusion.28, pred[64]{0:T(512)(128)(4,1)S(1)} %broadcast_compare_fusion, bf16[8]{0:T(256)(128)(2,1)S(1)} %get-tuple-element.10), kind=kOutput, calls=%fused_computation.8 | convolution fusion | flops 140288 | bytes 33136 | tf_op jit(solution)/shard_map/dot_general | solution.py:75
  2.5 0.0 copy-start.1
  2.5 7.4 %all-to-all-start = ((s32[8,8,128]{2,1,0:T(8,128)}), s32[8,8,128]{2,1,0:T(8,128)S(1)}, u32[]{:S(2)}, u32[]{:S(2)}) async-start(s32[8,8,128]{2,1,0:T(8,128)} %fusion), calls=%async_computation | async-start | bytes 65536 | tf_op jit(solution)/shard_map/all_to_all | solution.py:87
  9.9 0.1 select_reduce_fusion
  10.0 0.0 copy-done.1
  10.0 0.6 %gather_fusion.1 = bf16[8,32,128]{2,1,0:T(8,128)(2,1)S(1)} fusion(bf16[8,32,128]{2,1,0:T(8,128)(2,1)S(1)} %bitcast_bitcast_fusion, s32[1024]{0:T(1024)S(1)} %pad_clamp_fusion.1), kind=kCustom, calls=%fused_computation.1 | custom fusion | bytes 131104 | tf_op jit(solution)/shard_map/gather | solution.py:8
  10.6 0.0 copy-done
  10.6 0.2 convolution_convert_fusion.1
  10.8 0.7 %scatter_fusion = bf16[16,32,128]{2,1,0:T(8,128)(2,1)S(1)} fusion(bf16[16,32,128]{2,1,0:T(8,128)(2,1)S(1)} %broadcast.288, s32[8]{0:T(128)S(1)} %fusion.33, bf16[8,32,128]{2,1,0:T(8,128)(2,1)S(1)} %convolution_convert_fusion.1), kind=kCustom, calls=%fused_computation.4 | custom fusion | bytes 196640 | tf_op jit(solution)/shard_map/scatter | solution.py:82
  11.6 0.7 %copy.19 = bf16[8,2,2,32,128]{4,3,2,1,0:T(8,128)(2,1)} copy(bf16[8,2,2,32,128]{4,3,2,0,1:T(8,128)(2,1)S(1)} %bitcast.74) | data formatting | bytes 524288 | tf_op jit(solution)/shard_map/transpose | solution.py:85
  12.3 4.3 %all-to-all-done = s32[8,8,128]{2,1,0:T(8,128)S(1)} async-done(((s32[8,8,128]{2,1,0:T(8,128)}), s32[8,8,128]{2,1,0:T(8,128)S(1)}, u32[]{:S(2)}, u32[]{:S(2)}) %all-to-all-start) | async-done | bytes 32800 | tf_op jit(solution)/shard_map/all_to_all | solution.py:87
  16.6 0.2 slice_reduce_fusion
  16.8 0.1 reshape_squeeze.7
  16.9 0.6 %gather_fusion.2 = bf16[16,32,128]{2,1,0:T(8,128)(2,1)S(1)} fusion(bf16[8,32,128]{2,1,0:T(8,128)(2,1)S(1)} %bitcast_bitcast_fusion, s32[1024]{0:T(1024)S(1)} %pad_clamp_fusion), kind=kCustom, calls=%fused_computation.2 | custom fusion | bytes 262208 | tf_op jit(solution)/shard_map/gather | solution.py:8
  17.5 0.7 %constant_dynamic-update-slice_fusion = bf16[8,4,32,128]{3,2,1,0:T(8,128)(2,1)} fusion(bf16[8,4,32,128]{3,2,1,0:T(8,128)(2,1)} %bitcast.13, bf16[8,2,32,128]{3,2,1,0:T(8,128)(2,1)S(1)} %bitcast.79), kind=kLoop, calls=%fused_computation.104 | loop fusion | bytes 262144 | tf_op jit(solution)/shard_map/dynamic_update_slice | solution.py:90
  18.1 3.4 %all-to-all-start.1 = ((bf16[8,4,32,128]{3,2,1,0:T(8,128)(2,1)}), bf16[8,4,32,128]{3,2,1,0:T(8,128)(2,1)S(1)}, u32[]{:S(2)}, u32[]{:S(2)}) async-start(bf16[8,4,32,128]{3,2,1,0:T(8,128)(2,1)} %constant_dynamic-update-slice_fusion), calls=%async_computation.1 | async-start | bytes 524288 | tf_op jit(solution)/shard_map/all_to_all | solution.py:91
  21.6 0.6 %gather_fusion.3 = bf16[16,128,128]{2,1,0:T(8,128)(2,1)S(1)} fusion(bf16[8,128,128]{2,1,0:T(8,128)(2,1)S(1)} %copy-done, s32[1024]{0:T(1024)S(1)} %pad_clamp_fusion.2), kind=kCustom, calls=%fused_computation.3 | custom fusion | bytes 1048640 | tf_op jit(solution)/shard_map/gather | solution.py:8
  22.2 0.7 %gather_fusion = s32[16]{0:T(128)S(1)} fusion(s32[8]{0:T(128)S(1)} %get-tuple-element.2, s32[1024]{0:T(1024)S(1)} %pad_clamp_fusion.2), kind=kCustom, calls=%fused_computation | custom fusion | bytes 192 | tf_op jit(solution)/shard_map/gather | solution.py:8
  22.9 0.1 fusion.21
  23.0 0.1 reshape_squeeze.6
  23.1 0.1 pad_add_fusion
  23.1 6.6 %all-to-all-done.1 = bf16[8,4,32,128]{3,2,1,0:T(8,128)(2,1)S(1)} async-done(((bf16[8,4,32,128]{3,2,1,0:T(8,128)(2,1)}), bf16[8,4,32,128]{3,2,1,0:T(8,128)(2,1)S(1)}, u32[]{:S(2)}, u32[]{:S(2)}) %all-to-all-start.1) | async-done | bytes 262176 | tf_op jit(solution)/shard_map/all_to_all | solution.py:91
  29.8 0.4 fusion.2
  30.3 0.6 %convolution_convert_fusion = bf16[8,32,128]{2,0,1:T(8,128)(2,1)S(1)} fusion(f32[32,32,128]{2,1,0:T(8,128)S(1)} %pad_maximum_fusion, s32[32]{0:T(128)S(1)} %pad_add_fusion), kind=kOutput, calls=%fused_computation.5 | convolution fusion | flops 12615936 | bytes 589952 | tf_op jit(solution)/shard_map/sfi,sb->fbi/dot_general | solution.py:105
  30.9 1.6 %collective-permute-start.1 = (bf16[32,1024]{1,0:T(8,128)(2,1)S(1)}, bf16[32,1024]{1,0:T(8,128)(2,1)S(1)}, u32[]{:S(2)}, u32[]{:S(2)}) collective-permute-start(bf16[32,1024]{1,0:T(8,128)(2,1)S(1)} %bitcast.80), channel_id=1, source_target_pairs={{0,2},{1,3},{2,0},{3,1},{4,6},{5,7},{6,4},{7,5},{8,10},{9,11},{10,... | collective-permute-start | bytes 196616 | tf_op jit(solution)/shard_map/ppermute | solution.py:24
  32.4 0.0 collective-permute-start
  32.4 2.8 %collective-permute-done.1 = bf16[32,1024]{1,0:T(8,128)(2,1)S(1)} collective-permute-done((bf16[32,1024]{1,0:T(8,128)(2,1)S(1)}, bf16[32,1024]{1,0:T(8,128)(2,1)S(1)}, u32[]{:S(2)}, u32[]{:S(2)}) %collective-permute-start.1) | collective-permute-done | bytes 65568 | tf_op jit(solution)/shard_map/ppermute | solution.py:24
  35.2 0.0 collective-permute-start.2
  35.2 0.0 copy-start.5
  35.2 0.0 collective-permute-done
  35.2 1.2 %collective-permute-done.2 = bf16[32,1024]{1,0:T(8,128)(2,1)S(1)} collective-permute-done((bf16[32,1024]{1,0:T(8,128)(2,1)S(1)}, bf16[32,1024]{1,0:T(8,128)(2,1)S(1)}, u32[]{:S(2)}, u32[]{:S(2)}) %collective-permute-start.2) | collective-permute-done | bytes 65568 | tf_op jit(solution)/shard_map/ppermute | solution.py:26
  36.5 0.0 copy-done.5
  36.5 0.0 copy-start.4
  36.5 1.3 %multiply_convert_fusion.1 = (bf16[1024,256]{1,0:T(8,128)(2,1)}, f32[1024,256]{1,0:T(8,128)S(1)}) fusion(bf16[128,256]{1,0:T(8,128)(2,1)S(1)} %copy-done.5, bf16[32,1024]{1,0:T(8,128)(2,1)S(1)} %get-tuple-element.5, bf16[32,1024]{1,0:T(8,128)(2,1)S(1)} %get-tuple-element.6, bf16[32,1024]{1,0:T(8,128)(2,1)S(1)} %get-tuple-element.7, ...), kind=kOutput, calls=%fused_computation.10 | convolution fusion | flops 69468160 | bytes 1900544 | tf_op jit(solution)/shard_map/dot_general | solution.py:108
  37.8 0.0 copy-done.4
  37.8 0.5 %fusion.5 = f32[32,256]{1,0:T(8,128)S(1)} fusion(f32[1024,256]{1,0:T(8,128)S(1)} %get-tuple-element.14, bf16[1024,256]{1,0:T(8,128)(2,1)S(1)} %copy-done.4, bf16[4,8,8,128]{3,2,1,0:T(8,128)(2,1)S(1)} %bitcast.77), kind=kOutput, calls=%fused_computation.17 | convolution fusion | flops 19398656 | bytes 1671168 | tf_op jit(solution)/shard_map/dot_general | solution.py:116
  38.4 12.1 %all_to_all.15 = f32[8,32,256]{2,1,0:T(8,128)S(1)} all-to-all(f32[8,32,256]{2,1,0:T(8,128)S(1)} %broadcast_in_dim.38), channel_id=1, replica_groups=mesh['row'=8,'col'=4] {'row'}, dimensions={0} | all-to-all | bytes 524288 | tf_op jit(solution)/shard_map/all_to_all | solution.py:43
  50.5 0.6 %fusion.15 = f32[32,256]{1,0:T(8,128)} fusion(f32[8,32,256]{2,1,0:T(8,128)S(1)} %all_to_all.15), kind=kLoop, calls=%fused_computation.35 | loop fusion | flops 57344 | bytes 294912 | tf_op jit(solution)/shard_map/add | solution.py:46
  (22 shorter events, 0.3 us)
Async XLA Ops:
  0.6 9.9 %copy-start = (bf16[8,128,128]{2,1,0:T(8,128)(2,1)S(1)}, bf16[8,128,128]{2,1,0:T(8,128)(2,1)}, u32[]{:S(2)}) copy-start(bf16[8,128,128]{2,1,0:T(8,128)(2,1)} %param.7) | copy-start | bytes 786436
  0.7 0.7 %copy-start.2 = (s32[8,2]{0,1:T(2,128)S(1)}, s32[8,2]{0,1:T(2,128)}, u32[]{:S(2)}) copy-start(s32[8,2]{0,1:T(2,128)} %param.9) | copy-start | bytes 196
  0.7 0.7 %copy-start.3 = (s32[8,1]{0,1:T(1,128)S(1)}, s32[8,1]{0,1:T(1,128)}, u32[]{:S(2)}) copy-start(s32[8,1]{0,1:T(1,128)} %param.8) | copy-start | bytes 100
  2.5 7.5 %copy-start.1 = (bf16[32,1024]{1,0:T(8,128)(2,1)S(1)}, bf16[32,1024]{1,0:T(8,128)(2,1)}, u32[]{:S(2)}) copy-start(bf16[32,1024]{1,0:T(8,128)(2,1)} %param.6) | copy-start | bytes 196612
  2.5 14.1 %all-to-all-start = ((s32[8,8,128]{2,1,0:T(8,128)}), s32[8,8,128]{2,1,0:T(8,128)S(1)}, u32[]{:S(2)}, u32[]{:S(2)}) async-start(s32[8,8,128]{2,1,0:T(8,128)} %fusion), calls=%async_computation | async-start | bytes 65536 | tf_op jit(solution)/shard_map/all_to_all | solution.py:87
  18.1 11.6 %all-to-all-start.1 = ((bf16[8,4,32,128]{3,2,1,0:T(8,128)(2,1)}), bf16[8,4,32,128]{3,2,1,0:T(8,128)(2,1)S(1)}, u32[]{:S(2)}, u32[]{:S(2)}) async-start(bf16[8,4,32,128]{3,2,1,0:T(8,128)(2,1)} %constant_dynamic-update-slice_fusion), calls=%async_computation.1 | async-start | bytes 524288 | tf_op jit(solution)/shard_map/all_to_all | solution.py:91
  30.9 4.3 %collective-permute-start.1 = (bf16[32,1024]{1,0:T(8,128)(2,1)S(1)}, bf16[32,1024]{1,0:T(8,128)(2,1)S(1)}, u32[]{:S(2)}, u32[]{:S(2)}) collective-permute-start(bf16[32,1024]{1,0:T(8,128)(2,1)S(1)} %bitcast.80), channel_id=1, source_target_pairs={{0,2},{1,3},{2,0},{3,1},{4,6},{5,7},{6,4},{7,5},{8,10},{9,11},{10,... | collective-permute-start | bytes 196616 | tf_op jit(solution)/shard_map/ppermute | solution.py:24
  32.4 2.8 %collective-permute-start = (bf16[32,1024]{1,0:T(8,128)(2,1)S(1)}, bf16[32,1024]{1,0:T(8,128)(2,1)S(1)}, u32[]{:S(2)}, u32[]{:S(2)}) collective-permute-start(bf16[32,1024]{1,0:T(8,128)(2,1)S(1)} %bitcast.81), channel_id=1, source_target_pairs={{0,1},{1,0},{2,3},{3,2},{4,5},{5,4},{6,7},{7,6},{8,9},{9,8},{10,11... | collective-permute-start | bytes 196616 | tf_op jit(solution)/shard_map/ppermute | solution.py:25
  35.2 1.3 %collective-permute-start.2 = (bf16[32,1024]{1,0:T(8,128)(2,1)S(1)}, bf16[32,1024]{1,0:T(8,128)(2,1)S(1)}, u32[]{:S(2)}, u32[]{:S(2)}) collective-permute-start(bf16[32,1024]{1,0:T(8,128)(2,1)S(1)} %collective-permute-done.1), channel_id=1, source_target_pairs={{0,1},{1,0},{2,3},{3,2},{4,5},{5,4},{6,7},{7,6},{8,9},{9,8},{10,11... | collective-permute-start | bytes 196616 | tf_op jit(solution)/shard_map/ppermute | solution.py:26
  35.2 1.3 %copy-start.5 = (bf16[128,256]{1,0:T(8,128)(2,1)S(1)}, bf16[128,256]{1,0:T(8,128)(2,1)}, u32[]{:S(2)}) copy-start(bf16[128,256]{1,0:T(8,128)(2,1)} %param.10) | copy-start | bytes 196612
  36.5 1.3 %copy-start.4 = (bf16[1024,256]{1,0:T(8,128)(2,1)S(1)}, bf16[1024,256]{1,0:T(8,128)(2,1)}, u32[]{:S(2)}) copy-start(bf16[1024,256]{1,0:T(8,128)(2,1)} %param.11) | copy-start | bytes 1572868

commit v15 on v13

--- a/solution.py
+++ b/solution.py
@@ -77,14 +77,11 @@
     ).astype(jnp.bfloat16)
     outgoing = jnp.zeros((n_row * capacity, feat_q, tile_dim), jnp.bfloat16)
     outgoing = outgoing.at[slot].set(mirror_terms, mode="promise_in_bounds", unique_indices=True)
-    base = jnp.concatenate(
-        [jnp.zeros_like(outgoing), outgoing], axis=0
-    ).reshape(2, n_row, capacity, feat_q, tile_dim).transpose(1, 0, 2, 3, 4)
-    base = base.reshape(n_row, 2 * capacity, feat_q, tile_dim)
+    mirror_half = outgoing.reshape(n_row, capacity, feat_q, tile_dim)
     got_ids = lax.all_to_all(requests, "row", split_axis=0, concat_axis=0, tiled=True)
     block_ids = got_ids[:, :, 0]
     asked = rows_of(xb, block_ids.reshape(-1)).reshape(n_row, capacity, feat_q, tile_dim)
-    payload = lax.dynamic_update_slice(base, asked, (0, 0, 0, 0))
+    payload = jnp.concatenate([asked, mirror_half], axis=1)
     both = lax.all_to_all(payload, "row", split_axis=0, concat_axis=0, tiled=True)
     fetched = both[:, :capacity].reshape(n_row * capacity, feat_q, tile_dim)
     incoming = both[:, capacity:].reshape(n_row * capacity, feat_q, tile_dim)

time: 51.1 us -> 51.2 us (level)
  local copies, waits for them, and re-layouts: 5.92 us -> 4.49 us
  other arithmetic: 2.74 us -> 3.47 us
  waiting for transfers between devices: 13.9 us -> 14.6 us
    all_to_all x1, waiting for transfers between devices: 3.27 us -> 4.03 us  [body(): lax.all_to_all(requests, 'row', split_axis=0, concat_axis=0, tiled=True)]
    concatenate x0 -> x1, other arithmetic: none -> 0.73 us  [body(): payload = jnp.concatenate([asked, mirror_half], axis=1)]
    transpose x1 -> x0, local copies, waits for them, and re-layouts: 0.72 us -> none  [body(): base = jnp.concatenate([jnp.zeros_like(outgoing), outgoing], axis=0).resh...]
    dynamic_update_slice x1 -> x0, local copies, waits for them, and re-layouts: 0.68 us -> none  [body(): payload = lax.dynamic_update_slice(base, asked, (0, 0, 0, 0))]
  transfers between devices with their start and end apart: 5 -> 5, of which waited for: 4 -> 4; matrix products, arithmetic and copies ran while one was open for 9% -> 8% of each run, Pallas kernels for 0% -> 0%
where the time goes in v15:
time: 51.2 us; the launch traced here: 50.8 us
  waiting for transfers between devices  14.6 us (29%)
  starting transfers between devices  12.3 us (24%)
  blocking collectives  12.1 us (24%)
  local copies, waits for them, and re-layouts  4.49 us (9%)
  other arithmetic  3.47 us (7%)
  matrix products  2.99 us (6%)
  between operations  0.82 us (2%)
    all_to_all x1, blocking collectives, sum_over_row(): lax.all_to_all(every, 'row', split_axis=0, concat_axis=0, tiled=True)  12.1 us
    all_to_all x1, starting transfers between devices, body(): lax.all_to_all(requests, 'row', split_axis=0, concat_axis=0, tiled=True)  7.28 us
    all_to_all x1, waiting for transfers between devices, body(): lax.all_to_all(payload, 'row', split_axis=0, concat_axis=0, tiled=True)  6.58 us
    all_to_all x1, waiting for transfers between devices, body(): lax.all_to_all(requests, 'row', split_axis=0, concat_axis=0, tiled=True)  4.03 us
    all_to_all x1, starting transfers between devices, body(): lax.all_to_all(payload, 'row', split_axis=0, concat_axis=0, tiled=True)  3.41 us
    ppermute x1, waiting for transfers between devices, gather_groups(): across = lax.ppermute(z_part, 'col', [(i, i ^ 2) for i in range(n_col)])  2.77 us
    gather x4, local copies, waits for them, and re-layouts, rows_of(): return a.at[idx].get(mode='promise_in_bounds')  2.45 us
    ppermute x1, starting transfers between devices, gather_groups(): across = lax.ppermute(z_part, 'col', [(i, i ^ 2) for i in range(n_col)])  1.56 us
  transfers between devices with their start and end apart: 5, of which 4 were waited for; matrix products, arithmetic and copies ran while one was open for 8% of the time, Pallas kernels for 0%

profile of v15, /device:TPU:0, one launch (start us, length us, event | category | flops | bytes accessed | tf_op | source)
XLA Modules:
  0.0 50.8 jit_solution(6865814443005872355)
XLA Ops:
  0.6 0.0 copy-start
  0.6 0.8 %and_select_fusion.3 = (s32[8]{0:T(128)S(1)}, s32[8,1]{0,1:T(1,128)S(1)}) fusion(s32[8,2]{0,1:T(2,128)} %param.9, s32[8,1]{0,1:T(1,128)} %param.8), kind=kLoop, calls=%fused_computation.65 | loop fusion | flops 120 | bytes 160 | tf_op jit(solution)/shard_map/jit(remainder)/select_n | solution.py:62
  1.5 0.2 convert_reduce_fusion
  1.7 0.7 %select_reduce_fusion = s32[8,2,128]{2,1,0:T(2,128)} fusion(s32[8]{0:T(128)S(1)} %get-tuple-element.10, s32[8,2]{1,0:T(8,128)S(1)} %multiply_add_fusion, s32[8]{0:T(128)S(1)} %multiply_add_fusion.1), kind=kLoop, calls=%fused_computation.33 | loop fusion | flops 47104 | bytes 8320 | tf_op jit(solution)/shard_map/reduce_sum | solution.py:70
  2.4 7.3 %all-to-all-start = ((s32[8,2,128]{2,1,0:T(2,128)}), s32[8,2,128]{2,1,0:T(2,128)S(1)}, u32[]{:S(2)}, u32[]{:S(2)}) async-start(s32[8,2,128]{2,1,0:T(2,128)} %select_reduce_fusion), calls=%async_computation | async-start | bytes 16384 | tf_op jit(solution)/shard_map/all_to_all | solution.py:81
  9.7 0.1 select_reduce_fusion.1
  9.8 0.9 %bitcast_bitcast_fusion = bf16[8,32,128]{2,1,0:T(8,128)(2,1)S(1)} fusion(bf16[32,1024]{1,0:T(8,128)(2,1)} %param.6), kind=kLoop, calls=%fused_computation.28 | loop fusion | bytes 131072 | tf_op jit(solution)/shard_map/transpose | solution.py:57
  10.6 0.6 %gather_fusion.2 = bf16[8,32,128]{2,1,0:T(8,128)(2,1)S(1)} fusion(bf16[8,32,128]{2,1,0:T(8,128)(2,1)S(1)} %bitcast_bitcast_fusion, s32[1024]{0:T(1024)S(1)} %pad_clamp_fusion), kind=kCustom, calls=%fused_computation.2 | custom fusion | bytes 131104 | tf_op jit(solution)/shard_map/gather | solution.py:8
  11.2 0.0 copy-done
  11.2 0.2 convolution_convert_fusion.1
  11.4 0.7 %scatter_fusion = bf16[16,32,128]{2,1,0:T(8,128)(2,1)S(1)} fusion(bf16[16,32,128]{2,1,0:T(8,128)(2,1)S(1)} %broadcast_in_dim.71, s32[8]{0:T(128)S(1)} %fusion.23, bf16[8,32,128]{2,1,0:T(8,128)(2,1)S(1)} %convolution_convert_fusion.1), kind=kCustom, calls=%fused_computation.4 | custom fusion | bytes 196640 | tf_op jit(solution)/shard_map/scatter | solution.py:79
  12.1 4.0 %all-to-all-done = s32[8,2,128]{2,1,0:T(2,128)S(1)} async-done(((s32[8,2,128]{2,1,0:T(2,128)}), s32[8,2,128]{2,1,0:T(2,128)S(1)}, u32[]{:S(2)}, u32[]{:S(2)}) %all-to-all-start) | async-done | bytes 8224 | tf_op jit(solution)/shard_map/all_to_all | solution.py:81
  16.2 0.2 slice_reduce_fusion
  16.4 0.1 reshape_squeeze.7
  16.5 0.6 %gather_fusion.1 = bf16[16,32,128]{2,1,0:T(8,128)(2,1)S(1)} fusion(bf16[8,32,128]{2,1,0:T(8,128)(2,1)S(1)} %bitcast_bitcast_fusion, s32[1024]{0:T(1024)S(1)} %pad_clamp_fusion.1), kind=kCustom, calls=%fused_computation.1 | custom fusion | bytes 262208 | tf_op jit(solution)/shard_map/gather | solution.py:8
  17.1 0.7 %pad_maximum_fusion.1 = bf16[8,4,32,128]{3,2,1,0:T(8,128)(2,1)} fusion(bf16[8,2,32,128]{3,2,1,0:T(8,128)(2,1)S(1)} %bitcast.78, bf16[8,2,32,128]{3,2,1,0:T(8,128)(2,1)S(1)} %bitcast.83), kind=kLoop, calls=%fused_computation.16 | loop fusion | flops 131072 | bytes 524288 | tf_op jit(solution)/shard_map/concatenate | solution.py:84
  17.8 3.4 %all-to-all-start.1 = ((bf16[8,4,32,128]{3,2,1,0:T(8,128)(2,1)}), bf16[8,4,32,128]{3,2,1,0:T(8,128)(2,1)S(1)}, u32[]{:S(2)}, u32[]{:S(2)}) async-start(bf16[8,4,32,128]{3,2,1,0:T(8,128)(2,1)} %pad_maximum_fusion.1), calls=%async_computation.1 | async-start | bytes 524288 | tf_op jit(solution)/shard_map/all_to_all | solution.py:85
  21.2 0.6 %gather_fusion.3 = bf16[16,128,128]{2,1,0:T(8,128)(2,1)S(1)} fusion(bf16[8,128,128]{2,1,0:T(8,128)(2,1)S(1)} %copy-done, s32[1024]{0:T(1024)S(1)} %pad_clamp_fusion.2), kind=kCustom, calls=%fused_computation.3 | custom fusion | bytes 1048640 | tf_op jit(solution)/shard_map/gather | solution.py:8
  21.9 0.7 %gather_fusion = s32[16]{0:T(128)S(1)} fusion(s32[8]{0:T(128)S(1)} %get-tuple-element.2, s32[1024]{0:T(1024)S(1)} %pad_clamp_fusion.2), kind=kCustom, calls=%fused_computation | custom fusion | bytes 192 | tf_op jit(solution)/shard_map/gather | solution.py:8
  22.5 0.1 fusion.15
  22.6 0.1 reshape_squeeze.6
  22.7 0.1 pad_add_fusion
  22.8 6.6 %all-to-all-done.1 = bf16[8,4,32,128]{3,2,1,0:T(8,128)(2,1)S(1)} async-done(((bf16[8,4,32,128]{3,2,1,0:T(8,128)(2,1)}), bf16[8,4,32,128]{3,2,1,0:T(8,128)(2,1)S(1)}, u32[]{:S(2)}, u32[]{:S(2)}) %all-to-all-start.1) | async-done | bytes 262176 | tf_op jit(solution)/shard_map/all_to_all | solution.py:85
  29.4 0.4 fusion.1
  29.9 0.6 %convolution_convert_fusion = bf16[8,32,128]{2,0,1:T(8,128)(2,1)S(1)} fusion(f32[32,32,128]{2,1,0:T(8,128)S(1)} %pad_maximum_fusion, s32[32]{0:T(128)S(1)} %pad_add_fusion), kind=kOutput, calls=%fused_computation.5 | convolution fusion | flops 12615936 | bytes 589952 | tf_op jit(solution)/shard_map/sfi,sb->fbi/dot_general | solution.py:99
  30.5 1.6 %collective-permute-start.1 = (bf16[32,1024]{1,0:T(8,128)(2,1)S(1)}, bf16[32,1024]{1,0:T(8,128)(2,1)S(1)}, u32[]{:S(2)}, u32[]{:S(2)}) collective-permute-start(bf16[32,1024]{1,0:T(8,128)(2,1)S(1)} %bitcast.84), channel_id=1, source_target_pairs={{0,2},{1,3},{2,0},{3,1},{4,6},{5,7},{6,4},{7,5},{8,10},{9,11},{10,... | collective-permute-start | bytes 196616 | tf_op jit(solution)/shard_map/ppermute | solution.py:24
  32.1 0.0 collective-permute-start
  32.1 2.8 %collective-permute-done.1 = bf16[32,1024]{1,0:T(8,128)(2,1)S(1)} collective-permute-done((bf16[32,1024]{1,0:T(8,128)(2,1)S(1)}, bf16[32,1024]{1,0:T(8,128)(2,1)S(1)}, u32[]{:S(2)}, u32[]{:S(2)}) %collective-permute-start.1) | collective-permute-done | bytes 65568 | tf_op jit(solution)/shard_map/ppermute | solution.py:24
  34.9 0.0 collective-permute-start.2
  34.9 0.0 copy-start.2
  34.9 0.0 collective-permute-done
  34.9 1.2 %collective-permute-done.2 = bf16[32,1024]{1,0:T(8,128)(2,1)S(1)} collective-permute-done((bf16[32,1024]{1,0:T(8,128)(2,1)S(1)}, bf16[32,1024]{1,0:T(8,128)(2,1)S(1)}, u32[]{:S(2)}, u32[]{:S(2)}) %collective-permute-start.2) | collective-permute-done | bytes 65568 | tf_op jit(solution)/shard_map/ppermute | solution.py:26
  36.2 0.0 copy-done.2
  36.2 0.0 copy-start.1
  36.2 1.3 %multiply_convert_fusion.1 = (bf16[1024,256]{1,0:T(8,128)(2,1)}, f32[1024,256]{1,0:T(8,128)S(1)}) fusion(bf16[128,256]{1,0:T(8,128)(2,1)S(1)} %copy-done.2, bf16[32,1024]{1,0:T(8,128)(2,1)S(1)} %get-tuple-element.5, bf16[32,1024]{1,0:T(8,128)(2,1)S(1)} %get-tuple-element.6, bf16[32,1024]{1,0:T(8,128)(2,1)S(1)} %get-tuple-element.7, ...), kind=kOutput, calls=%fused_computation.8 | convolution fusion | flops 69468160 | bytes 1900544 | tf_op jit(solution)/shard_map/dot_general | solution.py:102
  37.5 0.0 copy-done.1
  37.5 0.5 %fusion.4 = f32[32,256]{1,0:T(8,128)S(1)} fusion(f32[1024,256]{1,0:T(8,128)S(1)} %get-tuple-element.15, bf16[1024,256]{1,0:T(8,128)(2,1)S(1)} %copy-done.1, bf16[4,8,8,128]{3,2,1,0:T(8,128)(2,1)S(1)} %bitcast.81), kind=kOutput, calls=%fused_computation.15 | convolution fusion | flops 19398656 | bytes 1671168 | tf_op jit(solution)/shard_map/dot_general | solution.py:110
  38.0 12.1 %all_to_all.15 = f32[8,32,256]{2,1,0:T(8,128)S(1)} all-to-all(f32[8,32,256]{2,1,0:T(8,128)S(1)} %broadcast_in_dim.74), channel_id=1, replica_groups=mesh['row'=8,'col'=4] {'row'}, dimensions={0} | all-to-all | bytes 524288 | tf_op jit(solution)/shard_map/all_to_all | solution.py:43
  50.2 0.6 %fusion.14 = f32[32,256]{1,0:T(8,128)} fusion(f32[8,32,256]{2,1,0:T(8,128)S(1)} %all_to_all.15), kind=kLoop, calls=%fused_computation.35 | loop fusion | flops 57344 | bytes 294912 | tf_op jit(solution)/shard_map/add | solution.py:46
  (18 shorter events, 0.3 us)
Async XLA Ops:
  0.6 10.5 %copy-start = (bf16[8,128,128]{2,1,0:T(8,128)(2,1)S(1)}, bf16[8,128,128]{2,1,0:T(8,128)(2,1)}, u32[]{:S(2)}) copy-start(bf16[8,128,128]{2,1,0:T(8,128)(2,1)} %param.7) | copy-start | bytes 786436
  2.4 13.8 %all-to-all-start = ((s32[8,2,128]{2,1,0:T(2,128)}), s32[8,2,128]{2,1,0:T(2,128)S(1)}, u32[]{:S(2)}, u32[]{:S(2)}) async-start(s32[8,2,128]{2,1,0:T(2,128)} %select_reduce_fusion), calls=%async_computation | async-start | bytes 16384 | tf_op jit(solution)/shard_map/all_to_all | solution.py:81
  17.8 11.6 %all-to-all-start.1 = ((bf16[8,4,32,128]{3,2,1,0:T(8,128)(2,1)}), bf16[8,4,32,128]{3,2,1,0:T(8,128)(2,1)S(1)}, u32[]{:S(2)}, u32[]{:S(2)}) async-start(bf16[8,4,32,128]{3,2,1,0:T(8,128)(2,1)} %pad_maximum_fusion.1), calls=%async_computation.1 | async-start | bytes 524288 | tf_op jit(solution)/shard_map/all_to_all | solution.py:85
  30.5 4.3 %collective-permute-start.1 = (bf16[32,1024]{1,0:T(8,128)(2,1)S(1)}, bf16[32,1024]{1,0:T(8,128)(2,1)S(1)}, u32[]{:S(2)}, u32[]{:S(2)}) collective-permute-start(bf16[32,1024]{1,0:T(8,128)(2,1)S(1)} %bitcast.84), channel_id=1, source_target_pairs={{0,2},{1,3},{2,0},{3,1},{4,6},{5,7},{6,4},{7,5},{8,10},{9,11},{10,... | collective-permute-start | bytes 196616 | tf_op jit(solution)/shard_map/ppermute | solution.py:24
  32.1 2.8 %collective-permute-start = (bf16[32,1024]{1,0:T(8,128)(2,1)S(1)}, bf16[32,1024]{1,0:T(8,128)(2,1)S(1)}, u32[]{:S(2)}, u32[]{:S(2)}) collective-permute-start(bf16[32,1024]{1,0:T(8,128)(2,1)S(1)} %bitcast.85), channel_id=1, source_target_pairs={{0,1},{1,0},{2,3},{3,2},{4,5},{5,4},{6,7},{7,6},{8,9},{9,8},{10,11... | collective-permute-start | bytes 196616 | tf_op jit(solution)/shard_map/ppermute | solution.py:25
  34.9 1.3 %collective-permute-start.2 = (bf16[32,1024]{1,0:T(8,128)(2,1)S(1)}, bf16[32,1024]{1,0:T(8,128)(2,1)S(1)}, u32[]{:S(2)}, u32[]{:S(2)}) collective-permute-start(bf16[32,1024]{1,0:T(8,128)(2,1)S(1)} %collective-permute-done.1), channel_id=1, source_target_pairs={{0,1},{1,0},{2,3},{3,2},{4,5},{5,4},{6,7},{7,6},{8,9},{9,8},{10,11... | collective-permute-start | bytes 196616 | tf_op jit(solution)/shard_map/ppermute | solution.py:26
  34.9 1.3 %copy-start.2 = (bf16[128,256]{1,0:T(8,128)(2,1)S(1)}, bf16[128,256]{1,0:T(8,128)(2,1)}, u32[]{:S(2)}) copy-start(bf16[128,256]{1,0:T(8,128)(2,1)} %param.10) | copy-start | bytes 196612
  36.2 1.3 %copy-start.1 = (bf16[1024,256]{1,0:T(8,128)(2,1)S(1)}, bf16[1024,256]{1,0:T(8,128)(2,1)}, u32[]{:S(2)}) copy-start(bf16[1024,256]{1,0:T(8,128)(2,1)} %param.11) | copy-start | bytes 1572868

commit v16 on v13

--- a/solution.py
+++ b/solution.py
@@ -98,8 +98,8 @@
     block_range = jnp.arange(n_blocks, dtype=jnp.int32)
     terms = jnp.concatenate([forward_terms, incoming.astype(jnp.float32)], axis=0)
     targets = jnp.concatenate([row_of_slot, block_ids.reshape(-1)], axis=0)
-    target_hot = (targets[:, None] == block_range[None, :]).astype(jnp.float32)
-    z_sum = jnp.einsum("sfi,sb->fbi", terms, target_hot, precision=lax.Precision.HIGHEST)
+    target_hot = targets[:, None] == block_range[None, :]
+    z_sum = jnp.sum(jnp.where(target_hot[:, None, :, None], terms[:, :, None, :], 0.0), axis=0)
     z_part = z_sum.reshape(feat_q, rows).astype(jnp.bfloat16)
     z_full = gather_groups(z_part, n_col)
     y_full = lax.dot_general(

time: 51.1 us -> 52.5 us (1.027)
  starting transfers between devices: 12.3 us -> 13 us
  other arithmetic: 2.74 us -> 3.41 us
  matrix products: 2.99 us -> 2.41 us
    all_to_all x1, waiting for transfers between devices: 6.58 us -> 8.27 us  [body(): lax.all_to_all(payload, 'row', split_axis=0, concat_axis=0, tiled=True)]
    all_to_all x1, waiting for transfers between devices: 3.27 us -> 1.85 us  [body(): lax.all_to_all(requests, 'row', split_axis=0, concat_axis=0, tiled=True)]
    all_to_all x1, starting transfers between devices: 3.41 us -> 4.15 us  [body(): lax.all_to_all(payload, 'row', split_axis=0, concat_axis=0, tiled=True)]
    dot_general x1 -> x0, matrix products: 0.58 us -> none  [body(): jnp.einsum('sfi,sb->fbi', terms, target_hot, precision=lax.Precision.HIGH...]
    reduce_sum x0 -> x1, other arithmetic: none -> 0.58 us  [body(): jnp.sum(jnp.where(target_hot[:, None, :, None], terms[:, :, None, :], 0.0...]
where the time goes in v16:
time: 52.5 us; the launch traced here: 52.2 us
  waiting for transfers between devices  14.1 us (27%)
  starting transfers between devices  13 us (25%)
  blocking collectives  12.5 us (24%)
  local copies, waits for them, and re-layouts  5.92 us (11%)
  other arithmetic  3.41 us (6%)
  matrix products  2.41 us (5%)
  between operations  0.82 us (2%)
    all_to_all x1, blocking collectives, sum_over_row(): lax.all_to_all(every, 'row', split_axis=0, concat_axis=0, tiled=True)  12.5 us
    all_to_all x1, waiting for transfers between devices, body(): lax.all_to_all(payload, 'row', split_axis=0, concat_axis=0, tiled=True)  8.27 us
    all_to_all x1, starting transfers between devices, body(): lax.all_to_all(requests, 'row', split_axis=0, concat_axis=0, tiled=True)  7.28 us
    all_to_all x1, starting transfers between devices, body(): lax.all_to_all(payload, 'row', split_axis=0, concat_axis=0, tiled=True)  4.15 us
    ppermute x1, waiting for transfers between devices, gather_groups(): across = lax.ppermute(z_part, 'col', [(i, i ^ 2) for i in range(n_col)])  2.77 us
    gather x4, local copies, waits for them, and re-layouts, rows_of(): return a.at[idx].get(mode='promise_in_bounds')  2.45 us
    all_to_all x1, waiting for transfers between devices, body(): lax.all_to_all(requests, 'row', split_axis=0, concat_axis=0, tiled=True)  1.85 us
    ppermute x1, starting transfers between devices, gather_groups(): across = lax.ppermute(z_part, 'col', [(i, i ^ 2) for i in range(n_col)])  1.56 us
  transfers between devices with their start and end apart: 5, of which 4 were waited for; matrix products, arithmetic and copies ran while one was open for 9% of the time, Pallas kernels for 0%

profile of v16, /device:TPU:0, one launch (start us, length us, event | category | flops | bytes accessed | tf_op | source)
XLA Modules:
  0.0 52.2 jit_solution(1040730922313485125)
XLA Ops:
  0.6 0.0 copy-start
  0.6 0.8 %and_select_fusion.3 = (s32[8]{0:T(128)S(1)}, s32[8,1]{0,1:T(1,128)S(1)}) fusion(s32[8,2]{0,1:T(2,128)} %param.9, s32[8,1]{0,1:T(1,128)} %param.8), kind=kLoop, calls=%fused_computation.61 | loop fusion | flops 120 | bytes 160 | tf_op jit(solution)/shard_map/jit(remainder)/select_n | solution.py:62
  1.5 0.2 convert_reduce_fusion
  1.7 0.7 %select_reduce_fusion.1 = s32[8,2,128]{2,1,0:T(2,128)} fusion(s32[8]{0:T(128)S(1)} %get-tuple-element.10, s32[8,2]{1,0:T(8,128)S(1)} %multiply_add_fusion, s32[8]{0:T(128)S(1)} %multiply_add_fusion.1), kind=kLoop, calls=%fused_computation.31 | loop fusion | flops 47104 | bytes 8320 | tf_op jit(solution)/shard_map/reduce_sum | solution.py:70
  2.4 7.3 %all-to-all-start = ((s32[8,2,128]{2,1,0:T(2,128)}), s32[8,2,128]{2,1,0:T(2,128)S(1)}, u32[]{:S(2)}, u32[]{:S(2)}) async-start(s32[8,2,128]{2,1,0:T(2,128)} %select_reduce_fusion.1), calls=%async_computation | async-start | bytes 16384 | tf_op jit(solution)/shard_map/all_to_all | solution.py:84
  9.7 0.1 fusion.14
  9.7 0.1 select_reduce_fusion.2
  9.8 0.9 %bitcast_bitcast_fusion = bf16[8,32,128]{2,1,0:T(8,128)(2,1)S(1)} fusion(bf16[32,1024]{1,0:T(8,128)(2,1)} %param.6), kind=kLoop, calls=%fused_computation.26 | loop fusion | bytes 131072 | tf_op jit(solution)/shard_map/transpose | solution.py:57
  10.7 0.6 %gather_fusion.1 = bf16[8,32,128]{2,1,0:T(8,128)(2,1)S(1)} fusion(bf16[8,32,128]{2,1,0:T(8,128)(2,1)S(1)} %bitcast_bitcast_fusion, s32[1024]{0:T(1024)S(1)} %pad_clamp_fusion.1), kind=kCustom, calls=%fused_computation.1 | custom fusion | bytes 131104 | tf_op jit(solution)/shard_map/gather | solution.py:8
  11.3 0.0 copy-done
  11.3 0.2 convolution_convert_fusion
  11.5 0.6 %gather_fusion.3 = bf16[16,128,128]{2,1,0:T(8,128)(2,1)S(1)} fusion(bf16[8,128,128]{2,1,0:T(8,128)(2,1)S(1)} %copy-done, s32[1024]{0:T(1024)S(1)} %pad_clamp_fusion.2), kind=kCustom, calls=%fused_computation.3 | custom fusion | bytes 1048640 | tf_op jit(solution)/shard_map/gather | solution.py:8
  12.1 0.7 %gather_fusion = s32[16]{0:T(128)S(1)} fusion(s32[8]{0:T(128)S(1)} %get-tuple-element.2, s32[1024]{0:T(1024)S(1)} %pad_clamp_fusion.2), kind=kCustom, calls=%fused_computation | custom fusion | bytes 192 | tf_op jit(solution)/shard_map/gather | solution.py:8
  12.8 0.7 %scatter_fusion = bf16[16,32,128]{2,1,0:T(8,128)(2,1)S(1)} fusion(bf16[16,32,128]{2,1,0:T(8,128)(2,1)S(1)} %broadcast.301, s32[8]{0:T(128)S(1)} %fusion.18, bf16[8,32,128]{2,1,0:T(8,128)(2,1)S(1)} %convolution_convert_fusion), kind=kCustom, calls=%fused_computation.4 | custom fusion | bytes 196640 | tf_op jit(solution)/shard_map/scatter | solution.py:79
  13.6 0.7 %copy.14 = bf16[8,2,2,32,128]{4,3,2,1,0:T(8,128)(2,1)} copy(bf16[8,2,2,32,128]{4,3,2,0,1:T(8,128)(2,1)S(1)} %bitcast.77) | data formatting | bytes 524288 | tf_op jit(solution)/shard_map/transpose | solution.py:82
  14.3 1.8 %all-to-all-done = s32[8,2,128]{2,1,0:T(2,128)S(1)} async-done(((s32[8,2,128]{2,1,0:T(2,128)}), s32[8,2,128]{2,1,0:T(2,128)S(1)}, u32[]{:S(2)}, u32[]{:S(2)}) %all-to-all-start) | async-done | bytes 8224 | tf_op jit(solution)/shard_map/all_to_all | solution.py:84
  16.2 0.2 slice_reduce_fusion
  16.4 0.1 reshape_squeeze.7
  16.5 0.6 %gather_fusion.2 = bf16[16,32,128]{2,1,0:T(8,128)(2,1)S(1)} fusion(bf16[8,32,128]{2,1,0:T(8,128)(2,1)S(1)} %bitcast_bitcast_fusion, s32[1024]{0:T(1024)S(1)} %pad_clamp_fusion), kind=kCustom, calls=%fused_computation.2 | custom fusion | bytes 262208 | tf_op jit(solution)/shard_map/gather | solution.py:8
  17.1 0.7 %constant_dynamic-update-slice_fusion = bf16[8,4,32,128]{3,2,1,0:T(8,128)(2,1)} fusion(bf16[8,4,32,128]{3,2,1,0:T(8,128)(2,1)} %bitcast.10, bf16[8,2,32,128]{3,2,1,0:T(8,128)(2,1)S(1)} %bitcast.82), kind=kLoop, calls=%fused_computation.85 | loop fusion | bytes 262144 | tf_op jit(solution)/shard_map/dynamic_update_slice | solution.py:87
  17.7 4.2 %all-to-all-start.1 = ((bf16[8,4,32,128]{3,2,1,0:T(8,128)(2,1)}), bf16[8,4,32,128]{3,2,1,0:T(8,128)(2,1)S(1)}, u32[]{:S(2)}, u32[]{:S(2)}) async-start(bf16[8,4,32,128]{3,2,1,0:T(8,128)(2,1)} %constant_dynamic-update-slice_fusion), calls=%async_computation.1 | async-start | bytes 524288 | tf_op jit(solution)/shard_map/all_to_all | solution.py:88
  21.9 0.1 reshape_squeeze.6
  22.0 0.1 pad_add_fusion
  22.1 0.1 iota_compare_fusion
  22.1 8.3 %all-to-all-done.1 = bf16[8,4,32,128]{3,2,1,0:T(8,128)(2,1)S(1)} async-done(((bf16[8,4,32,128]{3,2,1,0:T(8,128)(2,1)}), bf16[8,4,32,128]{3,2,1,0:T(8,128)(2,1)S(1)}, u32[]{:S(2)}, u32[]{:S(2)}) %all-to-all-start.1) | async-done | bytes 262176 | tf_op jit(solution)/shard_map/all_to_all | solution.py:88
  30.5 0.4 fusion
  30.9 0.0 copy-start.2
  31.0 0.6 %select_reduce_fusion = bf16[32,8,128]{2,1,0:T(8,128)(2,1)S(1)} fusion(f32[32,32,128]{2,1,0:T(8,128)S(1)} %pad_maximum_fusion, pred[32,8]{1,0:T(8,128)(4,1)S(1)} %iota_compare_fusion), kind=kLoop, calls=%fused_computation.5 | loop fusion | flops 2064384 | bytes 590080 | tf_op jit(solution)/shard_map/reduce_sum | solution.py:102
  31.6 1.6 %collective-permute-start.1 = (bf16[32,1024]{1,0:T(8,128)(2,1)S(1)}, bf16[32,1024]{1,0:T(8,128)(2,1)S(1)}, u32[]{:S(2)}, u32[]{:S(2)}) collective-permute-start(bf16[32,1024]{1,0:T(8,128)(2,1)S(1)} %bitcast.83), channel_id=1, source_target_pairs={{0,2},{1,3},{2,0},{3,1},{4,6},{5,7},{6,4},{7,5},{8,10},{9,11},{10,... | collective-permute-start | bytes 196616 | tf_op jit(solution)/shard_map/ppermute | solution.py:24
  33.1 0.0 collective-permute-start
  33.1 2.8 %collective-permute-done.1 = bf16[32,1024]{1,0:T(8,128)(2,1)S(1)} collective-permute-done((bf16[32,1024]{1,0:T(8,128)(2,1)S(1)}, bf16[32,1024]{1,0:T(8,128)(2,1)S(1)}, u32[]{:S(2)}, u32[]{:S(2)}) %collective-permute-start.1) | collective-permute-done | bytes 65568 | tf_op jit(solution)/shard_map/ppermute | solution.py:24
  35.9 0.0 collective-permute-start.2
  35.9 0.0 collective-permute-done
  35.9 1.2 %collective-permute-done.2 = bf16[32,1024]{1,0:T(8,128)(2,1)S(1)} collective-permute-done((bf16[32,1024]{1,0:T(8,128)(2,1)S(1)}, bf16[32,1024]{1,0:T(8,128)(2,1)S(1)}, u32[]{:S(2)}, u32[]{:S(2)}) %collective-permute-start.2) | collective-permute-done | bytes 65568 | tf_op jit(solution)/shard_map/ppermute | solution.py:26
  37.2 0.0 copy-done.2
  37.2 0.0 copy-start.1
  37.2 1.3 %multiply_convert_fusion.1 = (bf16[1024,256]{1,0:T(8,128)(2,1)}, f32[1024,256]{1,0:T(8,128)S(1)}) fusion(bf16[128,256]{1,0:T(8,128)(2,1)S(1)} %copy-done.2, bf16[32,1024]{1,0:T(8,128)(2,1)S(1)} %get-tuple-element.5, bf16[32,1024]{1,0:T(8,128)(2,1)S(1)} %get-tuple-element.6, bf16[32,1024]{1,0:T(8,128)(2,1)S(1)} %get-tuple-element.7, ...), kind=kOutput, calls=%fused_computation.8 | convolution fusion | flops 69468160 | bytes 1900544 | tf_op jit(solution)/shard_map/dot_general | solution.py:105
  38.5 0.0 copy-done.1
  38.5 0.5 %fusion.3 = f32[32,256]{1,0:T(8,128)S(1)} fusion(f32[1024,256]{1,0:T(8,128)S(1)} %get-tuple-element.15, bf16[1024,256]{1,0:T(8,128)(2,1)S(1)} %copy-done.1, bf16[4,8,8,128]{3,2,1,0:T(8,128)(2,1)S(1)} %bitcast.80), kind=kOutput, calls=%fused_computation.14 | convolution fusion | flops 19398656 | bytes 1671168 | tf_op jit(solution)/shard_map/dot_general | solution.py:113
  39.1 12.5 %all_to_all.15 = f32[8,32,256]{2,1,0:T(8,128)S(1)} all-to-all(f32[8,32,256]{2,1,0:T(8,128)S(1)} %broadcast_in_dim.95), channel_id=1, replica_groups=mesh['row'=8,'col'=4] {'row'}, dimensions={0} | all-to-all | bytes 524288 | tf_op jit(solution)/shard_map/all_to_all | solution.py:43
  51.5 0.6 %fusion.13 = f32[32,256]{1,0:T(8,128)} fusion(f32[8,32,256]{2,1,0:T(8,128)S(1)} %all_to_all.15), kind=kLoop, calls=%fused_computation.33 | loop fusion | flops 57344 | bytes 294912 | tf_op jit(solution)/shard_map/add | solution.py:46
  (19 shorter events, 0.3 us)
Async XLA Ops:
  0.6 10.6 %copy-start = (bf16[8,128,128]{2,1,0:T(8,128)(2,1)S(1)}, bf16[8,128,128]{2,1,0:T(8,128)(2,1)}, u32[]{:S(2)}) copy-start(bf16[8,128,128]{2,1,0:T(8,128)(2,1)} %param.7) | copy-start | bytes 786436
  2.4 13.8 %all-to-all-start = ((s32[8,2,128]{2,1,0:T(2,128)}), s32[8,2,128]{2,1,0:T(2,128)S(1)}, u32[]{:S(2)}, u32[]{:S(2)}) async-start(s32[8,2,128]{2,1,0:T(2,128)} %select_reduce_fusion.1), calls=%async_computation | async-start | bytes 16384 | tf_op jit(solution)/shard_map/all_to_all | solution.py:84
  17.7 12.7 %all-to-all-start.1 = ((bf16[8,4,32,128]{3,2,1,0:T(8,128)(2,1)}), bf16[8,4,32,128]{3,2,1,0:T(8,128)(2,1)S(1)}, u32[]{:S(2)}, u32[]{:S(2)}) async-start(bf16[8,4,32,128]{3,2,1,0:T(8,128)(2,1)} %constant_dynamic-update-slice_fusion), calls=%async_computation.1 | async-start | bytes 524288 | tf_op jit(solution)/shard_map/all_to_all | solution.py:88
  30.9 6.3 %copy-start.2 = (bf16[128,256]{1,0:T(8,128)(2,1)S(1)}, bf16[128,256]{1,0:T(8,128)(2,1)}, u32[]{:S(2)}) copy-start(bf16[128,256]{1,0:T(8,128)(2,1)} %param.10) | copy-start | bytes 196612
  31.6 4.3 %collective-permute-start.1 = (bf16[32,1024]{1,0:T(8,128)(2,1)S(1)}, bf16[32,1024]{1,0:T(8,128)(2,1)S(1)}, u32[]{:S(2)}, u32[]{:S(2)}) collective-permute-start(bf16[32,1024]{1,0:T(8,128)(2,1)S(1)} %bitcast.83), channel_id=1, source_target_pairs={{0,2},{1,3},{2,0},{3,1},{4,6},{5,7},{6,4},{7,5},{8,10},{9,11},{10,... | collective-permute-start | bytes 196616 | tf_op jit(solution)/shard_map/ppermute | solution.py:24
  33.1 2.8 %collective-permute-start = (bf16[32,1024]{1,0:T(8,128)(2,1)S(1)}, bf16[32,1024]{1,0:T(8,128)(2,1)S(1)}, u32[]{:S(2)}, u32[]{:S(2)}) collective-permute-start(bf16[32,1024]{1,0:T(8,128)(2,1)S(1)} %bitcast.84), channel_id=1, source_target_pairs={{0,1},{1,0},{2,3},{3,2},{4,5},{5,4},{6,7},{7,6},{8,9},{9,8},{10,11... | collective-permute-start | bytes 196616 | tf_op jit(solution)/shard_map/ppermute | solution.py:25
  35.9 1.3 %collective-permute-start.2 = (bf16[32,1024]{1,0:T(8,128)(2,1)S(1)}, bf16[32,1024]{1,0:T(8,128)(2,1)S(1)}, u32[]{:S(2)}, u32[]{:S(2)}) collective-permute-start(bf16[32,1024]{1,0:T(8,128)(2,1)S(1)} %collective-permute-done.1), channel_id=1, source_target_pairs={{0,1},{1,0},{2,3},{3,2},{4,5},{5,4},{6,7},{7,6},{8,9},{9,8},{10,11... | collective-permute-start | bytes 196616 | tf_op jit(solution)/shard_map/ppermute | solution.py:26
  37.2 1.3 %copy-start.1 = (bf16[1024,256]{1,0:T(8,128)(2,1)S(1)}, bf16[1024,256]{1,0:T(8,128)(2,1)}, u32[]{:S(2)}) copy-start(bf16[1024,256]{1,0:T(8,128)(2,1)} %param.11) | copy-start | bytes 1572868

commit v17 on v16

--- a/solution.py
+++ b/solution.py
@@ -92,14 +92,14 @@
     slot_used = jnp.any(slot_hot, axis=1)
     tiles_by_slot = jnp.where(slot_used[:, None, None], rows_of(tiles, tile_of_slot), 0)
     row_of_slot = jnp.where(slot_used, rows_of(row_local, tile_of_slot), -1)
-    forward_terms = jnp.einsum(
-        "sfj,sij->sfi", fetched, tiles_by_slot, preferred_element_type=jnp.float32
-    )
     block_range = jnp.arange(n_blocks, dtype=jnp.int32)
-    terms = jnp.concatenate([forward_terms, incoming.astype(jnp.float32)], axis=0)
+    sources = jnp.concatenate([fetched, incoming], axis=0)
     targets = jnp.concatenate([row_of_slot, block_ids.reshape(-1)], axis=0)
-    target_hot = targets[:, None] == block_range[None, :]
-    z_sum = jnp.sum(jnp.where(target_hot[:, None, :, None], terms[:, :, None, :], 0.0), axis=0)
+    keep = targets[None, :] == block_range[:, None]
+    placed = jnp.where(keep[:, :, None, None], sources[None], jnp.zeros((), sources.dtype))
+    identity = jnp.broadcast_to(jnp.eye(tile_dim, dtype=sources.dtype), (n_row * capacity, tile_dim, tile_dim))
+    right = jnp.concatenate([tiles_by_slot.transpose(0, 2, 1), identity], axis=0)
+    z_sum = jnp.einsum("bsfk,ski->fbi", placed, right, preferred_element_type=jnp.float32)
     z_part = z_sum.reshape(feat_q, rows).astype(jnp.bfloat16)
     z_full = gather_groups(z_part, n_col)
     y_full = lax.dot_general(

time: 52.5 us -> 52.8 us (level)
  other arithmetic: 3.41 us -> 2.83 us
    select_n x3, other arithmetic: 0.02 us -> 0.78 us  [rows_of(): return a.at[idx].get(mode='promise_in_bounds')]
    select_n x1, other arithmetic: 0.77 us -> 0.02 us  [body(): row_local = key % n_blocks]
    reduce_sum x1 -> x0, other arithmetic: 0.58 us -> none  [body(): jnp.sum(jnp.where(target_hot[:, None, :, None], terms[:, :, None, :], 0.0...]
    gather x4 -> x5, local copies, waits for them, and re-layouts: 2.45 us -> 2.76 us  [rows_of(): return a.at[idx].get(mode='promise_in_bounds')]
  transfers between devices with their start and end apart: 5 -> 5, of which waited for: 4 -> 4; matrix products, arithmetic and copies ran while one was open for 9% -> 10% of each run, Pallas kernels for 0% -> 0%
where the time goes in v17:
time: 52.8 us; the launch traced here: 52.4 us
  waiting for transfers between devices  13.7 us (26%)
  starting transfers between devices  13.4 us (25%)
  blocking collectives  12.5 us (24%)
  local copies, waits for them, and re-layouts  6.34 us (12%)
  other arithmetic  2.83 us (5%)
  matrix products  2.73 us (5%)
  between operations  0.85 us (2%)
    all_to_all x1, blocking collectives, sum_over_row(): lax.all_to_all(every, 'row', split_axis=0, concat_axis=0, tiled=True)  12.5 us
    all_to_all x1, waiting for transfers between devices, body(): lax.all_to_all(payload, 'row', split_axis=0, concat_axis=0, tiled=True)  8.31 us
    all_to_all x1, starting transfers between devices, body(): lax.all_to_all(requests, 'row', split_axis=0, concat_axis=0, tiled=True)  7.28 us
    all_to_all x1, starting transfers between devices, body(): lax.all_to_all(payload, 'row', split_axis=0, concat_axis=0, tiled=True)  4.6 us
    ppermute x1, waiting for transfers between devices, gather_groups(): across = lax.ppermute(z_part, 'col', [(i, i ^ 2) for i in range(n_col)])  2.77 us
    gather x5, local copies, waits for them, and re-layouts, rows_of(): return a.at[idx].get(mode='promise_in_bounds')  2.76 us
    ppermute x1, starting transfers between devices, gather_groups(): across = lax.ppermute(z_part, 'col', [(i, i ^ 2) for i in range(n_col)])  1.56 us
    all_to_all x1, waiting for transfers between devices, body(): lax.all_to_all(requests, 'row', split_axis=0, concat_axis=0, tiled=True)  1.41 us
  transfers between devices with their start and end apart: 5, of which 4 were waited for; matrix products, arithmetic and copies ran while one was open for 10% of the time, Pallas kernels for 0%

profile of v17, /device:TPU:0, one launch (start us, length us, event | category | flops | bytes accessed | tf_op | source)
XLA Modules:
  0.0 52.4 jit_solution(11233401948942970607)
XLA Ops:
  0.6 0.0 copy-start
  0.6 0.8 %fusion.32 = (s32[8]{0:T(128)S(1)}, s32[8,1]{0,1:T(1,128)S(1)}) fusion(s32[8,2]{0,1:T(2,128)} %param.9, s32[8,1]{0,1:T(1,128)} %param.8), kind=kLoop, calls=%fused_computation.84 | loop fusion | flops 144 | bytes 160 | tf_op jit(solution)/shard_map/select_n | solution.py:8
  1.5 0.2 convert_reduce_fusion
  1.7 0.7 %select_reduce_fusion = s32[8,2,128]{2,1,0:T(2,128)} fusion(s32[8]{0:T(128)S(1)} %get-tuple-element.11, s32[8,2]{1,0:T(8,128)S(1)} %multiply_add_fusion, s32[8]{0:T(128)S(1)} %multiply_add_fusion.1), kind=kLoop, calls=%fused_computation.37 | loop fusion | flops 47104 | bytes 8320 | tf_op jit(solution)/shard_map/reduce_sum | solution.py:70
  2.4 7.3 %all-to-all-start = ((s32[8,2,128]{2,1,0:T(2,128)}), s32[8,2,128]{2,1,0:T(2,128)S(1)}, u32[]{:S(2)}, u32[]{:S(2)}) async-start(s32[8,2,128]{2,1,0:T(2,128)} %select_reduce_fusion), calls=%async_computation | async-start | bytes 16384 | tf_op jit(solution)/shard_map/all_to_all | solution.py:84
  9.7 0.1 fusion.27
  9.7 0.1 select_reduce_fusion.1
  9.8 0.9 %bitcast_bitcast_fusion = bf16[8,32,128]{2,1,0:T(8,128)(2,1)S(1)} fusion(bf16[32,1024]{1,0:T(8,128)(2,1)} %param.6), kind=kLoop, calls=%fused_computation.32 | loop fusion | bytes 131072 | tf_op jit(solution)/shard_map/transpose | solution.py:57
  10.7 0.6 %gather_fusion.2 = bf16[8,32,128]{2,1,0:T(8,128)(2,1)S(1)} fusion(bf16[8,32,128]{2,1,0:T(8,128)(2,1)S(1)} %bitcast_bitcast_fusion, s32[1024]{0:T(1024)S(1)} %pad_clamp_fusion.1), kind=kCustom, calls=%fused_computation.2 | custom fusion | bytes 131104 | tf_op jit(solution)/shard_map/gather | solution.py:8
  11.3 0.0 copy-done
  11.3 0.2 convolution_convert_fusion
  11.5 0.7 %gather_fusion = bf16[16,128,128]{2,1,0:T(8,128)(2,1)S(1)} fusion(bf16[8,128,128]{2,1,0:T(8,128)(2,1)S(1)} %copy-done, s32[1024]{0:T(1024)S(1)} %pad_clamp_fusion.2), kind=kCustom, calls=%fused_computation | custom fusion | bytes 1048640 | tf_op jit(solution)/shard_map/gather | solution.py:8
  12.1 0.3 copy.19
  12.4 0.1 select_bitcast_fusion
  12.6 0.7 %gather_fusion.1 = s32[16]{0:T(128)S(1)} fusion(s32[8]{0:T(128)S(1)} %get-tuple-element.10, s32[1024]{0:T(1024)S(1)} %pad_clamp_fusion.2), kind=kCustom, calls=%fused_computation.1 | custom fusion | bytes 192 | tf_op jit(solution)/shard_map/gather | solution.py:8
  13.3 0.7 %scatter_fusion = bf16[16,32,128]{2,1,0:T(8,128)(2,1)S(1)} fusion(bf16[16,32,128]{2,1,0:T(8,128)(2,1)S(1)} %broadcast.303, s32[8]{0:T(128)S(1)} %fusion.31, bf16[8,32,128]{2,1,0:T(8,128)(2,1)S(1)} %convolution_convert_fusion), kind=kCustom, calls=%fused_computation.4 | custom fusion | bytes 196640 | tf_op jit(solution)/shard_map/scatter | solution.py:79
  14.0 0.7 %copy.21 = bf16[8,2,2,32,128]{4,3,2,1,0:T(8,128)(2,1)} copy(bf16[8,2,2,32,128]{4,3,2,0,1:T(8,128)(2,1)S(1)} %bitcast.89) | data formatting | bytes 524288 | tf_op jit(solution)/shard_map/transpose | solution.py:82
  14.8 1.4 %all-to-all-done = s32[8,2,128]{2,1,0:T(2,128)S(1)} async-done(((s32[8,2,128]{2,1,0:T(2,128)}), s32[8,2,128]{2,1,0:T(2,128)S(1)}, u32[]{:S(2)}, u32[]{:S(2)}) %all-to-all-start) | async-done | bytes 8224 | tf_op jit(solution)/shard_map/all_to_all | solution.py:84
  16.2 0.2 slice_reduce_fusion
  16.4 0.1 reshape_squeeze.7
  16.5 0.6 %gather_fusion.3 = bf16[16,32,128]{2,1,0:T(8,128)(2,1)S(1)} fusion(bf16[8,32,128]{2,1,0:T(8,128)(2,1)S(1)} %bitcast_bitcast_fusion, s32[1024]{0:T(1024)S(1)} %pad_clamp_fusion), kind=kCustom, calls=%fused_computation.3 | custom fusion | bytes 262208 | tf_op jit(solution)/shard_map/gather | solution.py:8
  17.1 0.7 %constant_dynamic-update-slice_fusion = bf16[8,4,32,128]{3,2,1,0:T(8,128)(2,1)} fusion(bf16[8,4,32,128]{3,2,1,0:T(8,128)(2,1)} %bitcast.12, bf16[8,2,32,128]{3,2,1,0:T(8,128)(2,1)S(1)} %bitcast.90), kind=kLoop, calls=%fused_computation.93 | loop fusion | bytes 262144 | tf_op jit(solution)/shard_map/dynamic_update_slice | solution.py:87
  17.7 4.6 %all-to-all-start.1 = ((bf16[8,4,32,128]{3,2,1,0:T(8,128)(2,1)}), bf16[8,4,32,128]{3,2,1,0:T(8,128)(2,1)S(1)}, u32[]{:S(2)}, u32[]{:S(2)}) async-start(bf16[8,4,32,128]{3,2,1,0:T(8,128)(2,1)} %constant_dynamic-update-slice_fusion), calls=%async_computation.1 | async-start | bytes 524288 | tf_op jit(solution)/shard_map/all_to_all | solution.py:88
  22.4 0.1 reshape_squeeze.6
  22.4 0.1 pad_add_fusion
  22.5 8.3 %all-to-all-done.1 = bf16[8,4,32,128]{3,2,1,0:T(8,128)(2,1)S(1)} async-done(((bf16[8,4,32,128]{3,2,1,0:T(8,128)(2,1)}), bf16[8,4,32,128]{3,2,1,0:T(8,128)(2,1)S(1)}, u32[]{:S(2)}, u32[]{:S(2)}) %all-to-all-start.1) | async-done | bytes 262176 | tf_op jit(solution)/shard_map/all_to_all | solution.py:88
  30.9 0.1 broadcast_in_dim.92
  31.0 0.0 copy-start.2
  31.0 0.8 %fusion.9 = bf16[8,4,8,128]{3,2,1,0:T(8,128)(2,1)S(1)} fusion(pred[8,32]{1,0:T(8,128)(4,1)S(1)} %iota_compare_fusion.1, bf16[16,128,128]{2,1,0:T(8,128)(2,1)S(1)} %broadcast_in_dim.92, bf16[16,128,128]{2,1,0:T(8,128)(2,1)S(1)} %select_bitcast_fusion, bf16[32,32,128]{2,1,0:T(8,128)(2,1)S(1)} %pad_maximum_fusion), kind=kOutput, calls=%fused_computation.11 | convolution fusion | flops 271613952 | bytes 1376512 | tf_op jit(solution)/shard_map/bsfk,ski->fbi/dot_general | solution.py:102
  31.8 1.6 %collective-permute-start.1 = (bf16[32,1024]{1,0:T(8,128)(2,1)S(1)}, bf16[32,1024]{1,0:T(8,128)(2,1)S(1)}, u32[]{:S(2)}, u32[]{:S(2)}) collective-permute-start(bf16[32,1024]{1,0:T(8,128)(2,1)S(1)} %bitcast.93), channel_id=1, source_target_pairs={{0,2},{1,3},{2,0},{3,1},{4,6},{5,7},{6,4},{7,5},{8,10},{9,11},{10,... | collective-permute-start | bytes 196616 | tf_op jit(solution)/shard_map/ppermute | solution.py:24
  33.4 0.0 collective-permute-start
  33.4 2.8 %collective-permute-done.1 = bf16[32,1024]{1,0:T(8,128)(2,1)S(1)} collective-permute-done((bf16[32,1024]{1,0:T(8,128)(2,1)S(1)}, bf16[32,1024]{1,0:T(8,128)(2,1)S(1)}, u32[]{:S(2)}, u32[]{:S(2)}) %collective-permute-start.1) | collective-permute-done | bytes 65568 | tf_op jit(solution)/shard_map/ppermute | solution.py:24
  36.1 0.0 collective-permute-start.2
  36.1 0.0 collective-permute-done
  36.1 1.2 %collective-permute-done.2 = bf16[32,1024]{1,0:T(8,128)(2,1)S(1)} collective-permute-done((bf16[32,1024]{1,0:T(8,128)(2,1)S(1)}, bf16[32,1024]{1,0:T(8,128)(2,1)S(1)}, u32[]{:S(2)}, u32[]{:S(2)}) %collective-permute-start.2) | collective-permute-done | bytes 65568 | tf_op jit(solution)/shard_map/ppermute | solution.py:26
  37.4 0.0 copy-done.2
  37.5 0.0 copy-start.1
  37.5 1.3 %multiply_convert_fusion.1 = (bf16[1024,256]{1,0:T(8,128)(2,1)}, f32[1024,256]{1,0:T(8,128)S(1)}) fusion(bf16[128,256]{1,0:T(8,128)(2,1)S(1)} %copy-done.2, bf16[32,1024]{1,0:T(8,128)(2,1)S(1)} %get-tuple-element.5, bf16[32,1024]{1,0:T(8,128)(2,1)S(1)} %get-tuple-element.6, bf16[32,1024]{1,0:T(8,128)(2,1)S(1)} %get-tuple-element.7, ...), kind=kOutput, calls=%fused_computation.16 | convolution fusion | flops 69468160 | bytes 1900544 | tf_op jit(solution)/shard_map/dot_general | solution.py:105
  38.7 0.0 copy-done.1
  38.7 0.5 fusion.16
  39.3 12.5 %all_to_all.15 = f32[8,32,256]{2,1,0:T(8,128)S(1)} all-to-all(f32[8,32,256]{2,1,0:T(8,128)S(1)} %broadcast_in_dim.99), channel_id=1, replica_groups=mesh['row'=8,'col'=4] {'row'}, dimensions={0} | all-to-all | bytes 524288 | tf_op jit(solution)/shard_map/all_to_all | solution.py:43
  51.8 0.6 %fusion.26 = f32[32,256]{1,0:T(8,128)} fusion(f32[8,32,256]{2,1,0:T(8,128)S(1)} %all_to_all.15), kind=kLoop, calls=%fused_computation.41 | loop fusion | flops 57344 | bytes 294912 | tf_op jit(solution)/shard_map/add | solution.py:46
  (20 shorter events, 0.3 us)
Async XLA Ops:
  0.6 10.6 %copy-start = (bf16[8,128,128]{2,1,0:T(8,128)(2,1)S(1)}, bf16[8,128,128]{2,1,0:T(8,128)(2,1)}, u32[]{:S(2)}) copy-start(bf16[8,128,128]{2,1,0:T(8,128)(2,1)} %param.7) | copy-start | bytes 786436
  2.4 13.8 %all-to-all-start = ((s32[8,2,128]{2,1,0:T(2,128)}), s32[8,2,128]{2,1,0:T(2,128)S(1)}, u32[]{:S(2)}, u32[]{:S(2)}) async-start(s32[8,2,128]{2,1,0:T(2,128)} %select_reduce_fusion), calls=%async_computation | async-start | bytes 16384 | tf_op jit(solution)/shard_map/all_to_all | solution.py:84
  17.7 13.1 %all-to-all-start.1 = ((bf16[8,4,32,128]{3,2,1,0:T(8,128)(2,1)}), bf16[8,4,32,128]{3,2,1,0:T(8,128)(2,1)S(1)}, u32[]{:S(2)}, u32[]{:S(2)}) async-start(bf16[8,4,32,128]{3,2,1,0:T(8,128)(2,1)} %constant_dynamic-update-slice_fusion), calls=%async_computation.1 | async-start | bytes 524288 | tf_op jit(solution)/shard_map/all_to_all | solution.py:88
  31.0 6.4 %copy-start.2 = (bf16[128,256]{1,0:T(8,128)(2,1)S(1)}, bf16[128,256]{1,0:T(8,128)(2,1)}, u32[]{:S(2)}) copy-start(bf16[128,256]{1,0:T(8,128)(2,1)} %param.10) | copy-start | bytes 196612
  31.8 4.3 %collective-permute-start.1 = (bf16[32,1024]{1,0:T(8,128)(2,1)S(1)}, bf16[32,1024]{1,0:T(8,128)(2,1)S(1)}, u32[]{:S(2)}, u32[]{:S(2)}) collective-permute-start(bf16[32,1024]{1,0:T(8,128)(2,1)S(1)} %bitcast.93), channel_id=1, source_target_pairs={{0,2},{1,3},{2,0},{3,1},{4,6},{5,7},{6,4},{7,5},{8,10},{9,11},{10,... | collective-permute-start | bytes 196616 | tf_op jit(solution)/shard_map/ppermute | solution.py:24
  33.4 2.8 %collective-permute-start = (bf16[32,1024]{1,0:T(8,128)(2,1)S(1)}, bf16[32,1024]{1,0:T(8,128)(2,1)S(1)}, u32[]{:S(2)}, u32[]{:S(2)}) collective-permute-start(bf16[32,1024]{1,0:T(8,128)(2,1)S(1)} %bitcast.94), channel_id=1, source_target_pairs={{0,1},{1,0},{2,3},{3,2},{4,5},{5,4},{6,7},{7,6},{8,9},{9,8},{10,11... | collective-permute-start | bytes 196616 | tf_op jit(solution)/shard_map/ppermute | solution.py:25
  36.1 1.3 %collective-permute-start.2 = (bf16[32,1024]{1,0:T(8,128)(2,1)S(1)}, bf16[32,1024]{1,0:T(8,128)(2,1)S(1)}, u32[]{:S(2)}, u32[]{:S(2)}) collective-permute-start(bf16[32,1024]{1,0:T(8,128)(2,1)S(1)} %collective-permute-done.1), channel_id=1, source_target_pairs={{0,1},{1,0},{2,3},{3,2},{4,5},{5,4},{6,7},{7,6},{8,9},{9,8},{10,11... | collective-permute-start | bytes 196616 | tf_op jit(solution)/shard_map/ppermute | solution.py:26
  37.5 1.3 %copy-start.1 = (bf16[1024,256]{1,0:T(8,128)(2,1)S(1)}, bf16[1024,256]{1,0:T(8,128)(2,1)}, u32[]{:S(2)}) copy-start(bf16[1024,256]{1,0:T(8,128)(2,1)} %param.11) | copy-start | bytes 1572868

commit v18 on v13

--- a/solution.py
+++ b/solution.py
@@ -39,12 +39,18 @@
 
 
 def sum_over_row(x, n_row):
-    every = jnp.broadcast_to(x[None], (n_row,) + x.shape)
-    parts = lax.all_to_all(every, "row", split_axis=0, concat_axis=0, tiled=True)
-    total = parts[0]
-    for i in range(1, n_row):
-        total = total + parts[i]
-    return total
+    if n_row & (n_row - 1):
+        every = jnp.broadcast_to(x[None], (n_row,) + x.shape)
+        parts = lax.all_to_all(every, "row", split_axis=0, concat_axis=0, tiled=True)
+        total = parts[0]
+        for i in range(1, n_row):
+            total = total + parts[i]
+        return total
+    k = 1
+    while k < n_row:
+        x = x + lax.ppermute(x, "row", [(i, i ^ k) for i in range(n_row)])
+        k *= 2
+    return x
 
 
 def body(x_t, tiles, tile_owner, tile_local, weight, cotangent):

time: 51.1 us -> 51.6 us (level)
  blocking collectives: 12.1 us -> 0 us
  waiting for transfers between devices: 13.9 us -> 24.7 us
  starting transfers between devices: 12.3 us -> 14.1 us
    all_to_all x1 -> x0, blocking collectives: 12.1 us -> none  [sum_over_row(): lax.all_to_all(every, 'row', split_axis=0, concat_axis=0, tiled=True)]
    ppermute x0 -> x3, waiting for transfers between devices: none -> 10.8 us  [sum_over_row(): x = x + lax.ppermute(x, 'row', [(i, i ^ k) for i in range(n_row)])]
    ppermute x0 -> x3, starting transfers between devices: none -> 1.89 us  [sum_over_row(): x = x + lax.ppermute(x, 'row', [(i, i ^ k) for i in range(n_row)])]
  transfers between devices with their start and end apart: 5 -> 8, of which waited for: 4 -> 7; matrix products, arithmetic and copies ran while one was open for 9% -> 9% of each run, Pallas kernels for 0% -> 0%
where the time goes in v18:
time: 51.6 us; the launch traced here: 51.3 us
  waiting for transfers between devices  24.7 us (48%)
  starting transfers between devices  14.1 us (27%)
  local copies, waits for them, and re-layouts  5.91 us (11%)
  matrix products  2.99 us (6%)
  other arithmetic  2.74 us (5%)
  between operations  0.83 us (2%)
    ppermute x3, waiting for transfers between devices, sum_over_row(): x = x + lax.ppermute(x, 'row', [(i, i ^ k) for i in range(n_row)])  10.8 us
    all_to_all x1, starting transfers between devices, body(): lax.all_to_all(requests, 'row', split_axis=0, concat_axis=0, tiled=True)  7.28 us
    all_to_all x1, waiting for transfers between devices, body(): lax.all_to_all(payload, 'row', split_axis=0, concat_axis=0, tiled=True)  6.58 us
    all_to_all x1, starting transfers between devices, body(): lax.all_to_all(payload, 'row', split_axis=0, concat_axis=0, tiled=True)  3.41 us
    all_to_all x1, waiting for transfers between devices, body(): lax.all_to_all(requests, 'row', split_axis=0, concat_axis=0, tiled=True)  3.27 us
    ppermute x1, waiting for transfers between devices, gather_groups(): across = lax.ppermute(z_part, 'col', [(i, i ^ 2) for i in range(n_col)])  2.77 us
    gather x4, local copies, waits for them, and re-layouts, rows_of(): return a.at[idx].get(mode='promise_in_bounds')  2.45 us
    ppermute x3, starting transfers between devices, sum_over_row(): x = x + lax.ppermute(x, 'row', [(i, i ^ k) for i in range(n_row)])  1.89 us
  transfers between devices with their start and end apart: 8, of which 7 were waited for; matrix products, arithmetic and copies ran while one was open for 9% of the time, Pallas kernels for 0%

profile of v18, /device:TPU:0, one launch (start us, length us, event | category | flops | bytes accessed | tf_op | source)
XLA Modules:
  0.0 51.3 jit_solution(8376695678008385281)
XLA Ops:
  0.6 0.0 copy-start
  0.6 0.8 %and_select_fusion.3 = (s32[8]{0:T(128)S(1)}, s32[8,1]{0,1:T(1,128)S(1)}) fusion(s32[8,2]{0,1:T(2,128)} %param.9, s32[8,1]{0,1:T(1,128)} %param.8), kind=kLoop, calls=%fused_computation.56 | loop fusion | flops 120 | bytes 160 | tf_op jit(solution)/shard_map/jit(remainder)/select_n | solution.py:68
  1.5 0.2 convert_reduce_fusion
  1.7 0.7 %select_reduce_fusion = s32[8,2,128]{2,1,0:T(2,128)} fusion(s32[8]{0:T(128)S(1)} %get-tuple-element.10, s32[8,2]{1,0:T(8,128)S(1)} %multiply_add_fusion, s32[8]{0:T(128)S(1)} %multiply_add_fusion.1), kind=kLoop, calls=%fused_computation.32 | loop fusion | flops 47104 | bytes 8320 | tf_op jit(solution)/shard_map/reduce_sum | solution.py:76
  2.4 7.3 %all-to-all-start = ((s32[8,2,128]{2,1,0:T(2,128)}), s32[8,2,128]{2,1,0:T(2,128)S(1)}, u32[]{:S(2)}, u32[]{:S(2)}) async-start(s32[8,2,128]{2,1,0:T(2,128)} %select_reduce_fusion), calls=%async_computation | async-start | bytes 16384 | tf_op jit(solution)/shard_map/all_to_all | solution.py:90
  9.7 0.1 select_reduce_fusion.1
  9.8 0.9 %bitcast_bitcast_fusion = bf16[8,32,128]{2,1,0:T(8,128)(2,1)S(1)} fusion(bf16[32,1024]{1,0:T(8,128)(2,1)} %param.6), kind=kLoop, calls=%fused_computation.27 | loop fusion | bytes 131072 | tf_op jit(solution)/shard_map/transpose | solution.py:63
  10.6 0.6 %gather_fusion.1 = bf16[8,32,128]{2,1,0:T(8,128)(2,1)S(1)} fusion(bf16[8,32,128]{2,1,0:T(8,128)(2,1)S(1)} %bitcast_bitcast_fusion, s32[1024]{0:T(1024)S(1)} %pad_clamp_fusion.1), kind=kCustom, calls=%fused_computation.1 | custom fusion | bytes 131104 | tf_op jit(solution)/shard_map/gather | solution.py:8
  11.2 0.0 copy-done
  11.2 0.2 convolution_convert_fusion.1
  11.4 0.7 %scatter_fusion = bf16[16,32,128]{2,1,0:T(8,128)(2,1)S(1)} fusion(bf16[16,32,128]{2,1,0:T(8,128)(2,1)S(1)} %broadcast.287, s32[8]{0:T(128)S(1)} %fusion.21, bf16[8,32,128]{2,1,0:T(8,128)(2,1)S(1)} %convolution_convert_fusion.1), kind=kCustom, calls=%fused_computation.4 | custom fusion | bytes 196640 | tf_op jit(solution)/shard_map/scatter | solution.py:85
  12.2 0.7 %copy.16 = bf16[8,2,2,32,128]{4,3,2,1,0:T(8,128)(2,1)} copy(bf16[8,2,2,32,128]{4,3,2,0,1:T(8,128)(2,1)S(1)} %bitcast.79) | data formatting | bytes 524288 | tf_op jit(solution)/shard_map/transpose | solution.py:88
  12.9 3.3 %all-to-all-done = s32[8,2,128]{2,1,0:T(2,128)S(1)} async-done(((s32[8,2,128]{2,1,0:T(2,128)}), s32[8,2,128]{2,1,0:T(2,128)S(1)}, u32[]{:S(2)}, u32[]{:S(2)}) %all-to-all-start) | async-done | bytes 8224 | tf_op jit(solution)/shard_map/all_to_all | solution.py:90
  16.2 0.2 slice_reduce_fusion
  16.4 0.1 reshape_squeeze.7
  16.5 0.6 %gather_fusion.2 = bf16[16,32,128]{2,1,0:T(8,128)(2,1)S(1)} fusion(bf16[8,32,128]{2,1,0:T(8,128)(2,1)S(1)} %bitcast_bitcast_fusion, s32[1024]{0:T(1024)S(1)} %pad_clamp_fusion), kind=kCustom, calls=%fused_computation.2 | custom fusion | bytes 262208 | tf_op jit(solution)/shard_map/gather | solution.py:8
  17.1 0.7 %constant_dynamic-update-slice_fusion = bf16[8,4,32,128]{3,2,1,0:T(8,128)(2,1)} fusion(bf16[8,4,32,128]{3,2,1,0:T(8,128)(2,1)} %bitcast.11, bf16[8,2,32,128]{3,2,1,0:T(8,128)(2,1)S(1)} %bitcast.84), kind=kLoop, calls=%fused_computation.80 | loop fusion | bytes 262144 | tf_op jit(solution)/shard_map/dynamic_update_slice | solution.py:93
  17.7 3.4 %all-to-all-start.1 = ((bf16[8,4,32,128]{3,2,1,0:T(8,128)(2,1)}), bf16[8,4,32,128]{3,2,1,0:T(8,128)(2,1)S(1)}, u32[]{:S(2)}, u32[]{:S(2)}) async-start(bf16[8,4,32,128]{3,2,1,0:T(8,128)(2,1)} %constant_dynamic-update-slice_fusion), calls=%async_computation.1 | async-start | bytes 524288 | tf_op jit(solution)/shard_map/all_to_all | solution.py:94
  21.2 0.6 %gather_fusion.3 = bf16[16,128,128]{2,1,0:T(8,128)(2,1)S(1)} fusion(bf16[8,128,128]{2,1,0:T(8,128)(2,1)S(1)} %copy-done, s32[1024]{0:T(1024)S(1)} %pad_clamp_fusion.2), kind=kCustom, calls=%fused_computation.3 | custom fusion | bytes 1048640 | tf_op jit(solution)/shard_map/gather | solution.py:8
  21.8 0.7 %gather_fusion = s32[16]{0:T(128)S(1)} fusion(s32[8]{0:T(128)S(1)} %get-tuple-element.2, s32[1024]{0:T(1024)S(1)} %pad_clamp_fusion.2), kind=kCustom, calls=%fused_computation | custom fusion | bytes 192 | tf_op jit(solution)/shard_map/gather | solution.py:8
  22.5 0.1 fusion.14
  22.6 0.1 reshape_squeeze.6
  22.7 0.1 pad_add_fusion
  22.8 6.6 %all-to-all-done.1 = bf16[8,4,32,128]{3,2,1,0:T(8,128)(2,1)S(1)} async-done(((bf16[8,4,32,128]{3,2,1,0:T(8,128)(2,1)}), bf16[8,4,32,128]{3,2,1,0:T(8,128)(2,1)S(1)}, u32[]{:S(2)}, u32[]{:S(2)}) %all-to-all-start.1) | async-done | bytes 262176 | tf_op jit(solution)/shard_map/all_to_all | solution.py:94
  29.4 0.4 fusion.1
  29.9 0.6 %convolution_convert_fusion = bf16[8,32,128]{2,0,1:T(8,128)(2,1)S(1)} fusion(f32[32,32,128]{2,1,0:T(8,128)S(1)} %pad_maximum_fusion, s32[32]{0:T(128)S(1)} %pad_add_fusion), kind=kOutput, calls=%fused_computation.5 | convolution fusion | flops 12615936 | bytes 589952 | tf_op jit(solution)/shard_map/sfi,sb->fbi/dot_general | solution.py:108
  30.5 1.6 %collective-permute-start.1 = (bf16[32,1024]{1,0:T(8,128)(2,1)S(1)}, bf16[32,1024]{1,0:T(8,128)(2,1)S(1)}, u32[]{:S(2)}, u32[]{:S(2)}) collective-permute-start(bf16[32,1024]{1,0:T(8,128)(2,1)S(1)} %bitcast.85), channel_id=1, source_target_pairs={{0,2},{1,3},{2,0},{3,1},{4,6},{5,7},{6,4},{7,5},{8,10},{9,11},{10,... | collective-permute-start | bytes 196616 | tf_op jit(solution)/shard_map/ppermute | solution.py:24
  32.1 0.0 collective-permute-start
  32.1 2.8 %collective-permute-done.1 = bf16[32,1024]{1,0:T(8,128)(2,1)S(1)} collective-permute-done((bf16[32,1024]{1,0:T(8,128)(2,1)S(1)}, bf16[32,1024]{1,0:T(8,128)(2,1)S(1)}, u32[]{:S(2)}, u32[]{:S(2)}) %collective-permute-start.1) | collective-permute-done | bytes 65568 | tf_op jit(solution)/shard_map/ppermute | solution.py:24
  34.8 0.0 collective-permute-start.2
  34.8 0.0 copy-start.2
  34.8 0.0 collective-permute-done
  34.8 1.2 %collective-permute-done.2 = bf16[32,1024]{1,0:T(8,128)(2,1)S(1)} collective-permute-done((bf16[32,1024]{1,0:T(8,128)(2,1)S(1)}, bf16[32,1024]{1,0:T(8,128)(2,1)S(1)}, u32[]{:S(2)}, u32[]{:S(2)}) %collective-permute-start.2) | collective-permute-done | bytes 65568 | tf_op jit(solution)/shard_map/ppermute | solution.py:26
  36.1 0.0 copy-done.2
  36.1 0.0 copy-start.1
  36.1 1.3 %multiply_convert_fusion.1 = (bf16[1024,256]{1,0:T(8,128)(2,1)}, f32[1024,256]{1,0:T(8,128)S(1)}) fusion(bf16[128,256]{1,0:T(8,128)(2,1)S(1)} %copy-done.2, bf16[32,1024]{1,0:T(8,128)(2,1)S(1)} %get-tuple-element.5, bf16[32,1024]{1,0:T(8,128)(2,1)S(1)} %get-tuple-element.6, bf16[32,1024]{1,0:T(8,128)(2,1)S(1)} %get-tuple-element.7, ...), kind=kOutput, calls=%fused_computation.8 | convolution fusion | flops 69468160 | bytes 1900544 | tf_op jit(solution)/shard_map/dot_general | solution.py:111
  37.4 0.0 copy-done.1
  37.4 0.5 %fusion.4 = f32[32,256]{1,0:T(8,128)S(1)} fusion(f32[1024,256]{1,0:T(8,128)S(1)} %get-tuple-element.15, bf16[1024,256]{1,0:T(8,128)(2,1)S(1)} %copy-done.1, bf16[4,8,8,128]{3,2,1,0:T(8,128)(2,1)S(1)} %bitcast.82), kind=kOutput, calls=%fused_computation.15 | convolution fusion | flops 19398656 | bytes 1671168 | tf_op jit(solution)/shard_map/dot_general | solution.py:119
  38.0 1.2 %collective-permute-start.3 = (f32[32,256]{1,0:T(8,128)S(1)}, f32[32,256]{1,0:T(8,128)S(1)}, u32[]{:S(2)}, u32[]{:S(2)}) collective-permute-start(f32[32,256]{1,0:T(8,128)S(1)} %fusion.4), channel_id=1, source_target_pairs={{0,4},{4,0},{8,12},{12,8},{16,20},{20,16},{24,28},{28,24},{1,5},{5... | collective-permute-start | bytes 98312 | tf_op jit(solution)/shard_map/ppermute | solution.py:51
  39.2 2.8 %collective-permute-done.3 = f32[32,256]{1,0:T(8,128)S(1)} collective-permute-done((f32[32,256]{1,0:T(8,128)S(1)}, f32[32,256]{1,0:T(8,128)S(1)}, u32[]{:S(2)}, u32[]{:S(2)}) %collective-permute-start.3) | collective-permute-done | bytes 32800 | tf_op jit(solution)/shard_map/ppermute | solution.py:51
  41.9 0.1 collective-permute-start.4
  42.0 3.8 %collective-permute-done.4 = f32[32,256]{1,0:T(8,128)S(1)} collective-permute-done((f32[32,256]{1,0:T(8,128)S(1)}, f32[32,256]{1,0:T(8,128)S(1)}, u32[]{:S(2)}, u32[]{:S(2)}) %collective-permute-start.4) | collective-permute-done | bytes 32800 | tf_op jit(solution)/shard_map/ppermute | solution.py:51
  45.9 0.6 %collective-permute-start.5 = (f32[32,256]{1,0:T(8,128)S(1)}, f32[32,256]{1,0:T(8,128)S(1)}, u32[]{:S(2)}, u32[]{:S(2)}) collective-permute-start(f32[32,256]{1,0:T(8,128)S(1)} %add.161), channel_id=1, source_target_pairs={{0,16},{4,20},{8,24},{12,28},{16,0},{20,4},{24,8},{28,12},{1,17},{... | collective-permute-start | bytes 98312 | tf_op jit(solution)/shard_map/ppermute | solution.py:51
  46.4 4.2 %collective-permute-done.5 = f32[32,256]{1,0:T(8,128)S(1)} collective-permute-done((f32[32,256]{1,0:T(8,128)S(1)}, f32[32,256]{1,0:T(8,128)S(1)}, u32[]{:S(2)}, u32[]{:S(2)}) %collective-permute-start.5) | collective-permute-done | bytes 32800 | tf_op jit(solution)/shard_map/ppermute | solution.py:51
  50.7 0.6 %add.162 = f32[32,256]{1,0:T(8,128)} add(f32[32,256]{1,0:T(8,128)S(1)} %add.161, f32[32,256]{1,0:T(8,128)S(1)} %collective-permute-done.5) | non-fusion elementwise | flops 8192 | bytes 98304 | tf_op jit(solution)/shard_map/add | solution.py:51
  (20 shorter events, 0.3 us)
Async XLA Ops:
  0.6 10.5 %copy-start = (bf16[8,128,128]{2,1,0:T(8,128)(2,1)S(1)}, bf16[8,128,128]{2,1,0:T(8,128)(2,1)}, u32[]{:S(2)}) copy-start(bf16[8,128,128]{2,1,0:T(8,128)(2,1)} %param.7) | copy-start | bytes 786436
  2.4 13.8 %all-to-all-start = ((s32[8,2,128]{2,1,0:T(2,128)}), s32[8,2,128]{2,1,0:T(2,128)S(1)}, u32[]{:S(2)}, u32[]{:S(2)}) async-start(s32[8,2,128]{2,1,0:T(2,128)} %select_reduce_fusion), calls=%async_computation | async-start | bytes 16384 | tf_op jit(solution)/shard_map/all_to_all | solution.py:90
  17.7 11.6 %all-to-all-start.1 = ((bf16[8,4,32,128]{3,2,1,0:T(8,128)(2,1)}), bf16[8,4,32,128]{3,2,1,0:T(8,128)(2,1)S(1)}, u32[]{:S(2)}, u32[]{:S(2)}) async-start(bf16[8,4,32,128]{3,2,1,0:T(8,128)(2,1)} %constant_dynamic-update-slice_fusion), calls=%async_computation.1 | async-start | bytes 524288 | tf_op jit(solution)/shard_map/all_to_all | solution.py:94
  30.5 4.3 %collective-permute-start.1 = (bf16[32,1024]{1,0:T(8,128)(2,1)S(1)}, bf16[32,1024]{1,0:T(8,128)(2,1)S(1)}, u32[]{:S(2)}, u32[]{:S(2)}) collective-permute-start(bf16[32,1024]{1,0:T(8,128)(2,1)S(1)} %bitcast.85), channel_id=1, source_target_pairs={{0,2},{1,3},{2,0},{3,1},{4,6},{5,7},{6,4},{7,5},{8,10},{9,11},{10,... | collective-permute-start | bytes 196616 | tf_op jit(solution)/shard_map/ppermute | solution.py:24
  32.1 2.8 %collective-permute-start = (bf16[32,1024]{1,0:T(8,128)(2,1)S(1)}, bf16[32,1024]{1,0:T(8,128)(2,1)S(1)}, u32[]{:S(2)}, u32[]{:S(2)}) collective-permute-start(bf16[32,1024]{1,0:T(8,128)(2,1)S(1)} %bitcast.86), channel_id=1, source_target_pairs={{0,1},{1,0},{2,3},{3,2},{4,5},{5,4},{6,7},{7,6},{8,9},{9,8},{10,11... | collective-permute-start | bytes 196616 | tf_op jit(solution)/shard_map/ppermute | solution.py:25
  34.8 1.3 %collective-permute-start.2 = (bf16[32,1024]{1,0:T(8,128)(2,1)S(1)}, bf16[32,1024]{1,0:T(8,128)(2,1)S(1)}, u32[]{:S(2)}, u32[]{:S(2)}) collective-permute-start(bf16[32,1024]{1,0:T(8,128)(2,1)S(1)} %collective-permute-done.1), channel_id=1, source_target_pairs={{0,1},{1,0},{2,3},{3,2},{4,5},{5,4},{6,7},{7,6},{8,9},{9,8},{10,11... | collective-permute-start | bytes 196616 | tf_op jit(solution)/shard_map/ppermute | solution.py:26
  34.8 1.3 %copy-start.2 = (bf16[128,256]{1,0:T(8,128)(2,1)S(1)}, bf16[128,256]{1,0:T(8,128)(2,1)}, u32[]{:S(2)}) copy-start(bf16[128,256]{1,0:T(8,128)(2,1)} %param.10) | copy-start | bytes 196612
  36.1 1.3 %copy-start.1 = (bf16[1024,256]{1,0:T(8,128)(2,1)S(1)}, bf16[1024,256]{1,0:T(8,128)(2,1)}, u32[]{:S(2)}) copy-start(bf16[1024,256]{1,0:T(8,128)(2,1)} %param.11) | copy-start | bytes 1572868
  38.0 4.0 %collective-permute-start.3 = (f32[32,256]{1,0:T(8,128)S(1)}, f32[32,256]{1,0:T(8,128)S(1)}, u32[]{:S(2)}, u32[]{:S(2)}) collective-permute-start(f32[32,256]{1,0:T(8,128)S(1)} %fusion.4), channel_id=1, source_target_pairs={{0,4},{4,0},{8,12},{12,8},{16,20},{20,16},{24,28},{28,24},{1,5},{5... | collective-permute-start | bytes 98312 | tf_op jit(solution)/shard_map/ppermute | solution.py:51
  41.9 3.9 %collective-permute-start.4 = (f32[32,256]{1,0:T(8,128)S(1)}, f32[32,256]{1,0:T(8,128)S(1)}, u32[]{:S(2)}, u32[]{:S(2)}) collective-permute-start(f32[32,256]{1,0:T(8,128)S(1)} %add.160), channel_id=1, source_target_pairs={{0,8},{4,12},{8,0},{12,4},{16,24},{20,28},{24,16},{28,20},{1,9},{5... | collective-permute-start | bytes 98312 | tf_op jit(solution)/shard_map/ppermute | solution.py:51
  45.9 4.8 %collective-permute-start.5 = (f32[32,256]{1,0:T(8,128)S(1)}, f32[32,256]{1,0:T(8,128)S(1)}, u32[]{:S(2)}, u32[]{:S(2)}) collective-permute-start(f32[32,256]{1,0:T(8,128)S(1)} %add.161), channel_id=1, source_target_pairs={{0,16},{4,20},{8,24},{12,28},{16,0},{20,4},{24,8},{28,12},{1,17},{... | collective-permute-start | bytes 98312 | tf_op jit(solution)/shard_map/ppermute | solution.py:51
